TPU v7x, 128 devices: a whole 4x4x4 slice. The times are simulated.
128 devices in a mesh: ctx: 32 (over z, y, x_hi), mp: 4 (over x_lo, core).
Axes of the slice: x: 4 (x_hi: 2, x_lo: 2; x = x_hi * 2 + x_lo), y: 4, z: 4, core: 2. Of those that a mesh axis runs over, the one named last changes fastest.
Arguments:
- queries: bfloat16 [2, 6144, 5120], P(None, 'ctx', 'mp'), may hold values from -24 to 24
- cache_keys: bfloat16 [6144, 5120], P(('ctx', 'mp')), may hold values from -26 to 26
- cache_values: bfloat16 [6144, 5120], P(('ctx', 'mp')), may hold values from -6 to 6
- douts: bfloat16 [2, 6144, 5120], P(None, 'ctx', 'mp'), may hold values from -6 to 6
- reads: int32 [32, 96], P('ctx'), may hold values from -1 to 383, as said below
Outputs:
- attn_out: bfloat16 [2, 6144, 5120], P(None, 'ctx', 'mp')
- d_queries: bfloat16 [2, 6144, 5120], P(None, 'ctx', 'mp')
- d_cache_keys: float32 [6144, 5120], P(('ctx', 'mp'))
- d_cache_values: float32 [6144, 5120], P(('ctx', 'mp'))
Inputs may be any that keep to these rules, and one draw needn't show every extreme that they name: Row c names, in rising order, the blocks that stretch c reads, then -1 in the remaining slots. Every named block ends at or before stretch c's last position. Block 0 is named in every row. Owner o holds blocks 3 * o to 3 * o + 2; a row names at most one block of an owner, and exactly one of each of the 4 owners of stretch c's own positions. Row c names min(96, 4 * (c + 1)) blocks.
All inputs are finite; a program needn't handle non-finite values.
Results may differ from a plain program's by a relative error of at most 0.017.
Values may be sent and summed in bfloat16 or wider, within the bound.
No kernel may reach another device: no remote copies, remote signals or barrier semaphores. Data moves between devices by JAX's collectives and lax.ppermute only.
A program may use at most 256 MiB of HBM per device.

v0:
```python
import math

import jax
import jax.numpy as jnp
from jax import lax
from jax.sharding import PartitionSpec as P

HD = 128
BLK = 16


group_slots = 32
neg_big = -1e30


def fetch_blocks(operands):
    return (
        lax.all_to_all(operands[0], ("ctx", "mp"), split_axis=0, concat_axis=0, tiled=True),
        lax.all_to_all(operands[1], ("ctx", "mp"), split_axis=0, concat_axis=0, tiled=True),
    )


def return_grads(operands):
    return (
        lax.all_to_all(
            operands[0].astype(jnp.bfloat16), ("ctx", "mp"), split_axis=0, concat_axis=0, tiled=True
        ).astype(jnp.float32),
        lax.all_to_all(
            operands[1].astype(jnp.bfloat16), ("ctx", "mp"), split_axis=0, concat_axis=0, tiled=True
        ).astype(jnp.float32),
    )


def attend_layer(
    query_rows, dout_rows, key_rows, value_rows, key_pos, key_live, query_pos, group_count, factor
):
    tok_rows, head_count, head_size = query_rows.shape
    group_span = group_slots * BLK
    key_total = key_rows.shape[0]

    def pieces(group_id):
        offset = group_id * group_span
        key_part = lax.dynamic_slice_in_dim(key_rows, offset, group_span, 0)
        value_part = lax.dynamic_slice_in_dim(value_rows, offset, group_span, 0)
        pos_part = lax.dynamic_slice_in_dim(key_pos, offset, group_span, 0)
        live_part = lax.dynamic_slice_in_dim(key_live, offset, group_span, 0)
        visible = (live_part[None, :] & (pos_part[None, :] <= query_pos[:, None]))[None]
        return (key_part, value_part, visible)

    def first_pass(group_id, running):
        row_top, row_total, stored = running
        key_part, value_part, visible = pieces(group_id)
        scores = (
            jnp.einsum("qhd,khd->hqk", query_rows, key_part, preferred_element_type=jnp.float32)
            * factor
        )
        scores = jnp.where(visible, scores, neg_big)
        stored = lax.dynamic_update_slice_in_dim(stored, scores, group_id * group_span, 2)
        new_top = jnp.maximum(row_top, jnp.max(scores, axis=2))
        raised = jnp.where(visible, jnp.exp(scores - new_top[:, :, None]), 0.0)
        return (new_top, row_total * jnp.exp(row_top - new_top) + jnp.sum(raised, axis=2), stored)

    start_top = jnp.full((head_count, tok_rows), neg_big, jnp.float32)
    start_total = jnp.zeros((head_count, tok_rows), jnp.float32)
    start_store = jnp.full((head_count, tok_rows, key_total), neg_big, jnp.float32)
    row_top, row_total, stored = lax.fori_loop(
        0, group_count, first_pass, (start_top, start_total, start_store)
    )

    def probabilities(group_id, visible):
        scores = lax.dynamic_slice_in_dim(stored, group_id * group_span, group_span, 2)
        return jnp.where(
            visible, jnp.exp(scores - row_top[:, :, None]) / row_total[:, :, None], 0.0
        )

    def second_pass(group_id, out_sum):
        key_part, value_part, visible = pieces(group_id)
        probs_low = probabilities(group_id, visible).astype(jnp.bfloat16)
        return out_sum + jnp.einsum(
            "hqk,khd->qhd", probs_low, value_part, preferred_element_type=jnp.float32
        )

    out_sum = lax.fori_loop(
        0, group_count, second_pass, jnp.zeros((tok_rows, head_count, head_size), jnp.float32)
    )
    attended = out_sum.astype(jnp.bfloat16)
    row_delta = jnp.sum(dout_rows.astype(jnp.float32) * attended.astype(jnp.float32), axis=2).T

    def third_pass(group_id, running):
        query_sum, key_grads, value_grads = running
        key_part, value_part, visible = pieces(group_id)
        prob_full = probabilities(group_id, visible)
        probs_low = prob_full.astype(jnp.bfloat16)
        d_probs = jnp.einsum(
            "qhd,khd->hqk", dout_rows, value_part, preferred_element_type=jnp.float32
        )
        d_scores = (prob_full * (d_probs - row_delta[:, :, None])).astype(jnp.bfloat16)
        query_sum = query_sum + jnp.einsum(
            "hqk,khd->qhd", d_scores, key_part, preferred_element_type=jnp.float32
        )
        key_part_grad = (
            jnp.einsum("hqk,qhd->khd", d_scores, query_rows, preferred_element_type=jnp.float32)
            * factor
        )
        value_part_grad = jnp.einsum(
            "hqk,qhd->khd", probs_low, dout_rows, preferred_element_type=jnp.float32
        )
        offset = group_id * group_span
        key_grads = lax.dynamic_update_slice_in_dim(key_grads, key_part_grad, offset, 0)
        value_grads = lax.dynamic_update_slice_in_dim(value_grads, value_part_grad, offset, 0)
        return (query_sum, key_grads, value_grads)

    empty_grads = jnp.zeros(key_rows.shape, jnp.float32)
    start_query = jnp.zeros((tok_rows, head_count, head_size), jnp.float32)
    query_sum, key_grads, value_grads = lax.fori_loop(
        0, group_count, third_pass, (start_query, empty_grads, empty_grads)
    )
    d_query = (query_sum * factor).astype(jnp.bfloat16)
    width = head_count * head_size
    return (
        attended.reshape(tok_rows, width),
        d_query.reshape(tok_rows, width),
        key_grads,
        value_grads,
    )


def on_device(queries, cache_keys, cache_values, douts, reads):
    layer_count, tok_rows, head_width = queries.shape
    kv_rows, full_width = cache_keys.shape
    ctx_count = lax.axis_size("ctx")
    mp_count = lax.axis_size("mp")
    owner_count = ctx_count * mp_count
    head_count = head_width // HD
    per_owner = kv_rows // BLK
    my_owner = lax.axis_index(("ctx", "mp"))
    my_stretch = lax.axis_index("ctx")
    factor = 1.0 / math.sqrt(HD)
    all_lists = lax.all_gather(reads, "ctx", axis=0, tiled=True)
    owner_hit = (all_lists >= 0) & (all_lists // per_owner == my_owner)
    chosen = jnp.sum(jnp.where(owner_hit, all_lists - my_owner * per_owner, 0), axis=1)
    wanted = jnp.any(owner_hit, axis=1)
    picker = (chosen[:, None] == jnp.arange(per_owner, dtype=jnp.int32)[None, :]) & wanted[:, None]
    picker_low = picker.astype(jnp.bfloat16)
    picker_full = picker.astype(jnp.float32)

    def outgoing(cache_rows):
        block_grid = cache_rows.reshape(per_owner, BLK * full_width)
        picked = jnp.dot(picker_low, block_grid, preferred_element_type=jnp.float32).astype(
            jnp.bfloat16
        )
        picked = picked.reshape(ctx_count, BLK, mp_count, head_width).transpose(0, 2, 1, 3)
        return picked.reshape(owner_count, BLK, head_width)

    def absorb(returned):
        block_grid = returned.reshape(ctx_count, mp_count, BLK, head_width).transpose(0, 2, 1, 3)
        block_grid = block_grid.reshape(ctx_count, BLK * full_width)
        summed = jnp.dot(
            picker_full.T,
            block_grid,
            precision=lax.Precision.HIGHEST,
            preferred_element_type=jnp.float32,
        )
        return summed.reshape(kv_rows, full_width)

    own_list = reads[0]
    owner_ids = jnp.arange(owner_count, dtype=jnp.int32)
    slot_hit = (own_list[:, None] >= 0) & (own_list[:, None] // per_owner == owner_ids[None, :])
    slot_live = jnp.any(slot_hit, axis=0)
    slot_block = jnp.sum(
        jnp.where(slot_hit, own_list[:, None] - owner_ids[None, :] * per_owner, 0), axis=0
    )
    slot_start = owner_ids * kv_rows + slot_block * BLK
    group_count = owner_count // group_slots
    key_pos = (slot_start[:, None] + jnp.arange(BLK, dtype=jnp.int32)[None, :]).reshape(-1)
    key_live = jnp.repeat(slot_live, BLK)
    query_pos = my_stretch * tok_rows + jnp.arange(tok_rows, dtype=jnp.int32)
    slot_shape = (owner_count, BLK, head_width)
    key_shape = (owner_count * BLK, head_count, HD)
    got_keys, got_values = fetch_blocks((outgoing(cache_keys), outgoing(cache_values)))
    key_rows = got_keys.reshape(key_shape)
    value_rows = got_values.reshape(key_shape)
    outputs = []
    query_grads = []
    key_total = jnp.zeros(key_shape, jnp.float32)
    value_total = jnp.zeros(key_shape, jnp.float32)
    for layer_id in range(layer_count):
        query_rows = queries[layer_id].reshape(tok_rows, head_count, HD)
        dout_rows = douts[layer_id].reshape(tok_rows, head_count, HD)
        attended, d_query, key_grads, value_grads = attend_layer(
            query_rows,
            dout_rows,
            key_rows,
            value_rows,
            key_pos,
            key_live,
            query_pos,
            group_count,
            factor,
        )
        outputs.append(attended)
        query_grads.append(d_query)
        key_total = key_total + key_grads
        value_total = value_total + value_grads
    sending = (key_total.reshape(slot_shape), value_total.reshape(slot_shape))
    back_keys, back_values = return_grads(sending)
    return (jnp.stack(outputs), jnp.stack(query_grads), absorb(back_keys), absorb(back_values))


def solution(mesh):
    return jax.shard_map(
        on_device,
        mesh=mesh,
        in_specs=(
            P(None, "ctx", "mp"),
            P(("ctx", "mp"), None),
            P(("ctx", "mp"), None),
            P(None, "ctx", "mp"),
            P("ctx", None),
        ),
        out_specs=(
            P(None, "ctx", "mp"),
            P(None, "ctx", "mp"),
            P(("ctx", "mp"), None),
            P(("ctx", "mp"), None),
        ),
        check_vma=False,
    )
```

profile of v0, /device:TPU:1, one launch (start us, length us, event | category | flops | bytes accessed | tf_op | source)
XLA Modules:
  0.0 779.1 jit_solution(3589189394489233096)
XLA Ops:
  2.4 83.1 %all-gather = s32[32,1,96]{2,1,0:T(1,128)S(1)} all-gather(s32[1,1,96]{2,1,0:T(1,128)} %bitcast.184), channel_id=1, replica_groups=mesh['ctx'=32,'mp'=4] {'ctx'}, dimensions={0}, use_global_device_ids=true | all-gather | bytes 12672 | tf_op jit(solution)/shard_map/all_gather | solution.py:139
  90.9 7.7 reshape.386
  98.6 5.9 copy.93
  104.5 19.5 %all-to-all-start = ((bf16[128,16,1280]{2,1,0:T(8,128)(2,1)}), bf16[128,16,1280]{2,1,0:T(8,128)(2,1)}, u32[]{:S(2)}, u32[]{:S(2)}) async-start(bf16[128,16,1280]{2,1,0:T(8,128)(2,1)} %bitcast.165), calls=%async_computation | async-start | bytes 10485760 | tf_op jit(solution)/shard_map/all_to_all | solution.py:19
  128.6 7.7 reshape.391
  136.4 5.8 copy.94
  142.2 45.8 %all-to-all-done = bf16[128,16,1280]{2,1,0:T(8,128)(2,1)} async-done(((bf16[128,16,1280]{2,1,0:T(8,128)(2,1)}), bf16[128,16,1280]{2,1,0:T(8,128)(2,1)}, u32[]{:S(2)}, u32[]{:S(2)}) %all-to-all-start) | async-done | bytes 5242912 | tf_op jit(solution)/shard_map/all_to_all | solution.py:19
  188.0 6.0 all-to-all-start.1
  202.1 11.3 %reshape.388 = bf16[2048,10,128]{2,1,0:T(8,128)(2,1)} reshape(bf16[128,16,1280]{2,1,0:T(8,128)(2,1)} %all-to-all-done) | data formatting | bytes 10485760 | tf_op jit(solution)/shard_map/reshape | solution.py:182
  213.4 7.0 copy.98
  220.5 37.4 %all-to-all-done.1 = bf16[128,16,1280]{2,1,0:T(8,128)(2,1)} async-done(((bf16[128,16,1280]{2,1,0:T(8,128)(2,1)}), bf16[128,16,1280]{2,1,0:T(8,128)(2,1)}, u32[]{:S(2)}, u32[]{:S(2)}) %all-to-all-start.1) | async-done | bytes 5242912 | tf_op jit(solution)/shard_map/all_to_all | solution.py:18
  257.8 11.3 %reshape.393 = bf16[2048,10,128]{2,1,0:T(8,128)(2,1)} reshape(bf16[128,16,1280]{2,1,0:T(8,128)(2,1)} %all-to-all-done.1) | data formatting | bytes 10485760 | tf_op jit(solution)/shard_map/reshape | solution.py:181
  269.1 7.1 copy.96
  276.2 7.5 broadcast.342.clone
  283.7 44.0 %while.102 = (s32[]{:T(128)}, f32[10,192]{1,0:T(8,128)S(1)}, f32[10,192]{1,0:T(8,128)}, f32[10,192,2048]{2,1,0:T(8,128)}, pred[2048]{0:T(1024)(128)(4,1)}, /*ind...) while((s32[]{:T(128)}, f32[10,192]{1,0:T(8,128)S(1)}, ...), condition=%wide.region_13.14_spmd.clone, body=%wide.region_10.13_spmd.clone.sunk | while | flops 259728960 | bytes 14002898 | solution.py:66
  288.6 4.9 fusion.140
  299.0 5.0 fusion.140
  310.3 5.0 fusion.140
  321.5 4.9 fusion.140
  327.8 23.0 %while.103 = (s32[]{:T(128)}, f32[192,10,128]{2,0,1:T(8,128)}, bf16[2048,10,128]{2,0,1:T(8,128)(2,1)}, pred[2048]{0:T(1024)(128)(4,1)}, s32[2048]{0:T(1024)S(1)}...) while((s32[]{:T(128)}, f32[192,10,128]{2,0,1:T(8,128)}, ...), condition=%wide.region_15.16_spmd.clone, body=%wide.region_14.15_spmd.clone.sunk | while | flops 256278720 | bytes 7440584 | solution.py:83
  328.7 4.5 fusion.143
  334.1 4.8 fusion.143
  339.9 4.8 fusion.143
  345.6 4.8 fusion.143
  352.3 7.5 broadcast.342.clone.1
  359.8 39.7 %while.100 = (s32[]{:T(128)}, f32[10,192]{1,0:T(8,128)S(1)}, f32[10,192]{1,0:T(8,128)S(1)}, f32[10,192,2048]{2,1,0:T(8,128)}, pred[2048]{0:T(1024)(128)(4,1)}, /...) while((s32[]{:T(128)}, f32[10,192]{1,0:T(8,128)S(1)}, ...), condition=%wide.region_7.8_spmd.clone, body=%wide.region_4.7_spmd.clone.sunk | while | flops 259728960 | bytes 14002898 | solution.py:66
  364.7 4.9 fusion.134
  374.6 5.0 fusion.134
  384.5 5.0 fusion.134
  394.5 4.9 fusion.134
  400.2 22.6 %while.101 = (s32[]{:T(128)}, f32[192,10,128]{2,0,1:T(8,128)}, bf16[2048,10,128]{2,0,1:T(8,128)(2,1)}, pred[2048]{0:T(1024)(128)(4,1)}, s32[2048]{0:T(1024)S(1)}...) while((s32[]{:T(128)}, f32[192,10,128]{2,0,1:T(8,128)}, ...), condition=%wide.region_9.10_spmd.clone, body=%wide.region_8.9_spmd.clone.sunk | while | flops 256278720 | bytes 7431880 | solution.py:83
  401.2 4.5 fusion.137
  406.6 4.8 fusion.137
  412.3 4.8 fusion.137
  418.1 4.8 fusion.137
  426.0 4.9 broadcast.343.clone
  430.8 4.8 broadcast.343.clone.1
  435.6 60.2 %while.105 = (s32[]{:T(128)}, f32[192,10,128]{2,0,1:T(8,128)S(1)}, f32[2048,10,128]{2,0,1:T(8,128)}, f32[2048,10,128]{2,0,1:T(8,128)}, bf16[2048,10,128]{2,0,1:T...) while((s32[]{:T(128)}, f32[192,10,128]{2,0,1:T(8,128)S(1)}, ...), condition=%wide.region_21.22_spmd.clone, body=%wide.region_20.21_spmd.clone.sunk | while | flops 1017807040 | bytes 27549068 | solution.py:115
  445.3 5.2 bitcast_dynamic-update-slice_fusion.11
  451.5 4.1 fusion.162
  460.3 5.2 bitcast_dynamic-update-slice_fusion.11
  475.4 5.3 bitcast_dynamic-update-slice_fusion.11
  481.7 4.0 fusion.162
  490.5 5.2 bitcast_dynamic-update-slice_fusion.11
  498.4 4.9 broadcast.343.clone.2
  503.3 4.8 broadcast.343.clone.3
  508.1 59.6 %while.104 = (s32[]{:T(128)}, f32[192,10,128]{2,0,1:T(8,128)S(1)}, f32[2048,10,128]{2,0,1:T(8,128)}, f32[2048,10,128]{2,0,1:T(8,128)}, bf16[2048,10,128]{2,0,1:T...) while((s32[]{:T(128)}, f32[192,10,128]{2,0,1:T(8,128)S(1)}, ...), condition=%wide.region_18.19_spmd.clone, body=%wide.region_17.18_spmd.clone.sunk | while | flops 1017807040 | bytes 27492208 | solution.py:115
  517.8 5.2 bitcast_dynamic-update-slice_fusion.9
  532.6 5.1 bitcast_dynamic-update-slice_fusion.9
  547.6 5.2 bitcast_dynamic-update-slice_fusion.9
  562.6 5.2 bitcast_dynamic-update-slice_fusion.9
  567.7 16.3 %add_convert_fusion = (bf16[2048,10,128]{2,0,1:T(8,128)(2,1)}, bf16[2048,10,128]{2,0,1:T(8,128)(2,1)S(1)}) fusion(f32[2048,10,128]{2,0,1:T(8,128)} %get-tuple-element.1128, f32[2048,10,128]{2,0,1:T(8,128)} %get-tuple-element.1129, f32[2048,10,128]{2,0,1:T(8,128)} %get-tuple-element.1126, f32[2048,10,128]{2,0,1:T(8,128)} %get-tuple-element.1127), kind=kLoop, calls=%fused_computation.84 | loop fusion | flops 10485760 | bytes 52428800 | tf_op jit(solution)/shard_map/convert_element_type | solution.py:29
  584.0 24.3 %copy.117 = bf16[2048,10,128]{2,1,0:T(8,128)(2,1)} copy(bf16[2048,10,128]{2,0,1:T(8,128)(2,1)S(1)} %get-tuple-element.1721) | data formatting | bytes 10485760 | tf_op jit(solution)/shard_map/convert_element_type | solution.py:26
  608.2 11.4 %convert_element_type.99 = bf16[128,16,1280]{2,1,0:T(8,128)(2,1)} reshape(bf16[2048,10,128]{2,1,0:T(8,128)(2,1)} %copy.117) | data formatting | bytes 10485760 | tf_op jit(solution)/shard_map/convert_element_type | solution.py:26
  619.6 5.6 all-to-all-start.2
  625.2 8.7 %copy.119 = bf16[2048,10,128]{2,1,0:T(8,128)(2,1)} copy(bf16[2048,10,128]{2,0,1:T(8,128)(2,1)} %get-tuple-element.1720) | data formatting | bytes 10485760 | tf_op jit(solution)/shard_map/convert_element_type | solution.py:29
  634.0 11.4 %convert_element_type.101 = bf16[128,16,1280]{2,1,0:T(8,128)(2,1)} reshape(bf16[2048,10,128]{2,1,0:T(8,128)(2,1)} %copy.119) | data formatting | bytes 10485760 | tf_op jit(solution)/shard_map/convert_element_type | solution.py:29
  645.3 43.8 %all-to-all-done.2 = bf16[128,16,1280]{2,1,0:T(8,128)(2,1)} async-done(((bf16[128,16,1280]{2,1,0:T(8,128)(2,1)}), bf16[128,16,1280]{2,1,0:T(8,128)(2,1)}, u32[]{:S(2)}, u32[]{:S(2)}) %all-to-all-start.2) | async-done | bytes 5242912 | tf_op jit(solution)/shard_map/all_to_all | solution.py:25
  689.2 6.0 all-to-all-start.3
  701.2 7.5 copy.126
  708.7 7.2 reshape.395
  721.0 37.9 %all-to-all-done.3 = bf16[128,16,1280]{2,1,0:T(8,128)(2,1)} async-done(((bf16[128,16,1280]{2,1,0:T(8,128)(2,1)}), bf16[128,16,1280]{2,1,0:T(8,128)(2,1)}, u32[]{:S(2)}, u32[]{:S(2)}) %all-to-all-start.3) | async-done | bytes 5242912 | tf_op jit(solution)/shard_map/all_to_all | solution.py:28
  758.9 7.5 copy.125
  766.5 7.1 reshape.398
  (308 shorter events, 164.6 us)
Async XLA Ops:
  86.9 37.9 %copy-start.21 = (pred[32]{0:T(512)(128)(4,1)}, pred[32]{0:T(512)(128)(4,1)S(1)}, u32[]{:S(2)}) copy-start(pred[32]{0:T(512)(128)(4,1)S(1)} %get-tuple-element.1706) | copy-start | bytes 100
  87.0 37.7 %copy-start.23 = (s32[32]{0:T(128)}, s32[32]{0:T(128)S(1)}, u32[]{:S(2)}) copy-start(s32[32]{0:T(128)S(1)} %fusion.63) | copy-start | bytes 388
  104.5 19.5 %copy-start.16 = (bf16[48,5120]{1,0:T(8,128)(2,1)S(1)}, bf16[48,5120]{1,0:T(8,128)(2,1)}, u32[]{:S(2)}) copy-start(bf16[48,5120]{1,0:T(8,128)(2,1)} %param.18) | copy-start | bytes 1474564
  104.5 83.5 %all-to-all-start = ((bf16[128,16,1280]{2,1,0:T(8,128)(2,1)}), bf16[128,16,1280]{2,1,0:T(8,128)(2,1)}, u32[]{:S(2)}, u32[]{:S(2)}) async-start(bf16[128,16,1280]{2,1,0:T(8,128)(2,1)} %bitcast.165), calls=%async_computation | async-start | bytes 10485760 | tf_op jit(solution)/shard_map/all_to_all | solution.py:19
  188.0 6.1 copy-start.25
  188.0 7.4 copy-start.11
  188.0 69.8 %all-to-all-start.1 = ((bf16[128,16,1280]{2,1,0:T(8,128)(2,1)}), bf16[128,16,1280]{2,1,0:T(8,128)(2,1)}, u32[]{:S(2)}, u32[]{:S(2)}) async-start(bf16[128,16,1280]{2,1,0:T(8,128)(2,1)} %bitcast.164), calls=%async_computation.1 | async-start | bytes 10485760 | tf_op jit(solution)/shard_map/all_to_all | solution.py:18
  201.1 12.3 %copy-start.8 = (bf16[1,192,1280]{1,2,0:T(8,128)(2,1)}, bf16[1,192,1280]{1,2,0:T(8,128)(2,1)S(1)}, u32[]{:S(2)}) copy-start(bf16[1,192,1280]{1,2,0:T(8,128)(2,1)S(1)} %copy.105) | copy-start | bytes 1474564
  352.3 72.9 %copy-start.5 = (bf16[192,10,128]{0,2,1:T(8,128)(2,1)}, bf16[192,10,128]{0,2,1:T(8,128)(2,1)S(1)}, u32[]{:S(2)}) copy-start(bf16[192,10,128]{0,2,1:T(8,128)(2,1)S(1)} %copy.104) | copy-start | bytes 1474564
  399.5 0.8 copy-start
  422.8 8.0 %copy-start.19 = (f32[10,192]{1,0:T(8,128)}, f32[10,192]{1,0:T(8,128)S(1)}, u32[]{:S(2)}) copy-start(f32[10,192]{1,0:T(8,128)S(1)} %get-tuple-element.2435) | copy-start | bytes 23044
  435.6 0.8 copy-start.9
  435.6 0.8 copy-start.12
  440.6 4.7 copy-start.18
  445.3 5.2 copy-start.10
  445.3 5.2 copy-start.13
  450.6 0.8 copy-start.9
  450.6 0.8 copy-start.12
  455.6 4.7 copy-start.18
  460.3 5.3 copy-start.10
  460.3 5.3 copy-start.13
  465.6 0.9 copy-start.9
  465.6 0.9 copy-start.12
  470.6 4.8 copy-start.18
  475.4 5.3 copy-start.10
  475.4 5.3 copy-start.13
  480.7 0.9 copy-start.9
  480.7 0.9 copy-start.12
  485.7 4.8 copy-start.18
  490.5 5.2 copy-start.10
  490.5 5.2 copy-start.13
  495.9 2.5 copy-start.3
  503.3 4.8 copy-start.1
  503.3 4.8 copy-start.2
  508.1 0.8 copy-start.14
  513.1 4.7 copy-start.17
  513.1 4.7 copy-start.20
  517.8 5.2 copy-start.15
  522.9 0.8 copy-start.14
  527.9 4.8 copy-start.17
  527.9 4.7 copy-start.20
  532.6 5.2 copy-start.15
  537.8 0.8 copy-start.14
  542.8 4.8 copy-start.17
  542.8 4.8 copy-start.20
  547.6 5.2 copy-start.15
  552.8 0.8 copy-start.14
  557.8 4.8 copy-start.17
  557.8 4.8 copy-start.20
  562.6 5.2 copy-start.15
  619.6 69.5 %all-to-all-start.2 = ((bf16[128,16,1280]{2,1,0:T(8,128)(2,1)}), bf16[128,16,1280]{2,1,0:T(8,128)(2,1)}, u32[]{:S(2)}, u32[]{:S(2)}) async-start(bf16[128,16,1280]{2,1,0:T(8,128)(2,1)} %convert_element_type.99), calls=%async_computation.2 | async-start | bytes 10485760 | tf_op jit(solution)/shard_map/all_to_all | solution.py:25
  645.3 49.8 %copy-start.6 = (bf16[192,10,128]{0,2,1:T(8,128)(2,1)S(1)}, bf16[192,10,128]{0,2,1:T(8,128)(2,1)}, u32[]{:S(2)}) copy-start(bf16[192,10,128]{0,2,1:T(8,128)(2,1)} %copy-done.5) | copy-start | bytes 1474564
  645.3 49.8 %copy-start.7 = (bf16[192,10,128]{0,2,1:T(8,128)(2,1)S(1)}, bf16[192,10,128]{0,2,1:T(8,128)(2,1)}, u32[]{:S(2)}) copy-start(bf16[192,10,128]{0,2,1:T(8,128)(2,1)} %copy.99) | copy-start | bytes 1474564
  689.2 69.8 %all-to-all-start.3 = ((bf16[128,16,1280]{2,1,0:T(8,128)(2,1)}), bf16[128,16,1280]{2,1,0:T(8,128)(2,1)}, u32[]{:S(2)}, u32[]{:S(2)}) async-start(bf16[128,16,1280]{2,1,0:T(8,128)(2,1)} %convert_element_type.101), calls=%async_computation.3 | async-start | bytes 10485760 | tf_op jit(solution)/shard_map/all_to_all | solution.py:28
  695.2 3.7 copy-start.4
  708.7 7.2 copy-start.22
  708.7 7.2 copy-start.24
where the time goes:
time: 791 us; the launch traced here: 779 us
  local copies, waits for them, and re-layouts  225 us (28%)
  matrix products  196 us (25%)
  waiting for transfers between devices  165 us (21%)
  blocking collectives  83.1 us (11%)
  other arithmetic  70.7 us (9%)
  starting transfers between devices  37.1 us (5%)
    all_gather x1, blocking collectives, on_device(): all_lists = lax.all_gather(reads, 'ctx', axis=0, tiled=True)  83.1 us
    all_to_all x1, waiting for transfers between devices, fetch_blocks(): lax.all_to_all(operands[1], ('ctx', 'mp'), split_axis=0, concat_axis=0, t...  45.8 us
    all_to_all x1, waiting for transfers between devices, return_grads(): lax.all_to_all(operands[0].astype(jnp.bfloat16), ('ctx', 'mp'), split_axi...  43.8 us
    dot_general x8, matrix products, third_pass(): jnp.einsum('hqk,qhd->khd', probs_low, dout_rows, preferred_element_type=j...  41.6 us
    dynamic_update_slice x8, other arithmetic, first_pass(): lax.dynamic_update_slice_in_dim(stored, scores, group_id * group_span, 2)  39.6 us
    all_to_all x1, waiting for transfers between devices, return_grads(): lax.all_to_all(operands[1].astype(jnp.bfloat16), ('ctx', 'mp'), split_axi...  37.9 us
    dot_general x8, matrix products, second_pass(): jnp.einsum('hqk,khd->qhd', probs_low, value_part, preferred_element_type=...  37.7 us
    all_to_all x1, waiting for transfers between devices, fetch_blocks(): lax.all_to_all(operands[0], ('ctx', 'mp'), split_axis=0, concat_axis=0, t...  37.4 us
  transfers between devices with their start and end apart: 4, of which 4 were waited for; matrix products, arithmetic and copies ran while one was open for 12% of the time, Pallas kernels for 0%

commit v1 on v0

v1 whole, which is shorter than its diff:
```python
import functools
import math

import jax
import jax.numpy as jnp
from jax import lax
from jax.experimental import pallas as pl
from jax.experimental.pallas import tpu as pltpu
from jax.sharding import PartitionSpec as P

HD = 128
BLK = 16

neg_big = -1e30
far_pos = 1 << 30


def fetch_blocks(operands):
    return (
        lax.all_to_all(operands[0], ("ctx", "mp"), split_axis=0, concat_axis=0, tiled=True),
        lax.all_to_all(operands[1], ("ctx", "mp"), split_axis=0, concat_axis=0, tiled=True),
    )


def return_grads(operands):
    return (
        lax.all_to_all(operands[0], ("ctx", "mp"), split_axis=0, concat_axis=0, tiled=True),
        lax.all_to_all(operands[1], ("ctx", "mp"), split_axis=0, concat_axis=0, tiled=True),
    )


def attend_kernel(
    kpos_ref, q_ref, do_ref, k_ref, v_ref, o_ref, dq_ref, dk_ref, dv_ref, dk_acc, dv_acc,
    *, factor, layer_count
):
    layer_id = pl.program_id(1)
    q = q_ref[0]
    do = do_ref[0]
    k = k_ref[...]
    v = v_ref[...]
    tok_rows = q.shape[0]
    rows = lax.broadcasted_iota(jnp.int32, (tok_rows, 1), 0)
    visible = kpos_ref[...] <= rows
    scores = lax.dot_general(
        q, k, (((1,), (1,)), ((), ())), preferred_element_type=jnp.float32
    ) * factor
    scores = jnp.where(visible, scores, neg_big)
    row_top = jnp.max(scores, axis=1, keepdims=True)
    raised = jnp.exp(scores - row_top)
    row_total = jnp.sum(raised, axis=1, keepdims=True)
    probs = raised * (1.0 / row_total)
    probs_low = probs.astype(jnp.bfloat16)
    attended = jnp.dot(probs_low, v, preferred_element_type=jnp.float32).astype(jnp.bfloat16)
    o_ref[0] = attended
    row_delta = jnp.sum(
        do.astype(jnp.float32) * attended.astype(jnp.float32), axis=1, keepdims=True
    )
    d_probs = lax.dot_general(
        do, v, (((1,), (1,)), ((), ())), preferred_element_type=jnp.float32
    )
    d_scores = (probs * (d_probs - row_delta)).astype(jnp.bfloat16)
    dq = jnp.dot(d_scores, k, preferred_element_type=jnp.float32) * factor
    dq_ref[0] = dq.astype(jnp.bfloat16)
    dk = lax.dot_general(
        d_scores, q, (((0,), (0,)), ((), ())), preferred_element_type=jnp.float32
    ) * factor
    dv = lax.dot_general(
        probs_low, do, (((0,), (0,)), ((), ())), preferred_element_type=jnp.float32
    )

    @pl.when(layer_id == 0)
    def _():
        dk_acc[...] = dk
        dv_acc[...] = dv

    @pl.when(layer_id > 0)
    def _():
        dk_acc[...] += dk
        dv_acc[...] += dv

    @pl.when(layer_id == layer_count - 1)
    def _():
        dk_ref[...] = dk_acc[...].astype(jnp.bfloat16)
        dv_ref[...] = dv_acc[...].astype(jnp.bfloat16)


def attend(kpos_rel, queries, douts, key_rows, value_rows, factor):
    layer_count, tok_rows, head_width = queries.shape
    key_total = key_rows.shape[0]
    head_count = head_width // HD
    kernel = functools.partial(attend_kernel, factor=factor, layer_count=layer_count)
    tok_spec = pl.BlockSpec((1, tok_rows, HD), lambda h, l: (l, 0, h))
    key_spec = pl.BlockSpec((key_total, HD), lambda h, l: (0, h))
    return pl.pallas_call(
        kernel,
        grid=(head_count, layer_count),
        in_specs=[
            pl.BlockSpec((1, key_total), lambda h, l: (0, 0)),
            tok_spec,
            tok_spec,
            key_spec,
            key_spec,
        ],
        out_specs=[tok_spec, tok_spec, key_spec, key_spec],
        out_shape=[
            jax.ShapeDtypeStruct(queries.shape, jnp.bfloat16),
            jax.ShapeDtypeStruct(queries.shape, jnp.bfloat16),
            jax.ShapeDtypeStruct(key_rows.shape, jnp.bfloat16),
            jax.ShapeDtypeStruct(key_rows.shape, jnp.bfloat16),
        ],
        scratch_shapes=[
            pltpu.VMEM((key_total, HD), jnp.float32),
            pltpu.VMEM((key_total, HD), jnp.float32),
        ],
        compiler_params=pltpu.CompilerParams(
            dimension_semantics=("arbitrary", "arbitrary"),
            vmem_limit_bytes=48 * 1024 * 1024,
        ),
    )(kpos_rel, queries, douts, key_rows, value_rows)


def on_device(queries, cache_keys, cache_values, douts, reads):
    layer_count, tok_rows, head_width = queries.shape
    kv_rows, full_width = cache_keys.shape
    ctx_count = lax.axis_size("ctx")
    mp_count = lax.axis_size("mp")
    owner_count = ctx_count * mp_count
    per_owner = kv_rows // BLK
    my_owner = lax.axis_index(("ctx", "mp"))
    my_stretch = lax.axis_index("ctx")
    my_mp = lax.axis_index("mp")
    factor = 1.0 / math.sqrt(HD)
    placed = jnp.where(
        (jnp.arange(ctx_count, dtype=jnp.int32) == my_stretch)[:, None] & (my_mp == 0),
        reads,
        0,
    )
    all_lists = lax.psum(placed, ("ctx", "mp"))
    owner_hit = (all_lists >= 0) & (all_lists // per_owner == my_owner)
    chosen = jnp.sum(jnp.where(owner_hit, all_lists - my_owner * per_owner, 0), axis=1)
    wanted = jnp.any(owner_hit, axis=1)
    picker = (chosen[:, None] == jnp.arange(per_owner, dtype=jnp.int32)[None, :]) & wanted[:, None]
    picker_low = picker.astype(jnp.bfloat16)
    picker_full = picker.astype(jnp.float32)

    def outgoing(cache_rows):
        block_grid = cache_rows.reshape(per_owner, BLK * full_width)
        picked = jnp.dot(picker_low, block_grid, preferred_element_type=jnp.float32).astype(
            jnp.bfloat16
        )
        picked = picked.reshape(ctx_count, BLK, mp_count, head_width).transpose(0, 2, 1, 3)
        return picked.reshape(owner_count, BLK, head_width)

    def absorb(returned):
        block_grid = returned.reshape(ctx_count, mp_count, BLK, head_width).transpose(0, 2, 1, 3)
        block_grid = block_grid.reshape(ctx_count, BLK * full_width)
        summed = jnp.dot(
            picker_full.T,
            block_grid.astype(jnp.float32),
            precision=lax.Precision.HIGHEST,
            preferred_element_type=jnp.float32,
        )
        return summed.reshape(kv_rows, full_width)

    own_list = reads[0]
    owner_ids = jnp.arange(owner_count, dtype=jnp.int32)
    slot_hit = (own_list[:, None] >= 0) & (own_list[:, None] // per_owner == owner_ids[None, :])
    slot_live = jnp.any(slot_hit, axis=0)
    slot_block = jnp.sum(
        jnp.where(slot_hit, own_list[:, None] - owner_ids[None, :] * per_owner, 0), axis=0
    )
    slot_start = owner_ids * kv_rows + slot_block * BLK
    key_pos = (slot_start[:, None] + jnp.arange(BLK, dtype=jnp.int32)[None, :]).reshape(-1)
    key_live = jnp.repeat(slot_live, BLK)
    kpos_rel = jnp.where(key_live, key_pos - my_stretch * tok_rows, far_pos)
    kpos_rel = kpos_rel.reshape(1, -1).astype(jnp.int32)
    slot_shape = (owner_count, BLK, head_width)
    got_keys, got_values = fetch_blocks((outgoing(cache_keys), outgoing(cache_values)))
    key_rows = got_keys.reshape(owner_count * BLK, head_width)
    value_rows = got_values.reshape(owner_count * BLK, head_width)
    attended, d_query, key_grads, value_grads = attend(
        kpos_rel, queries, douts, key_rows, value_rows, factor
    )
    sending = (key_grads.reshape(slot_shape), value_grads.reshape(slot_shape))
    back_keys, back_values = return_grads(sending)
    return (attended, d_query, absorb(back_keys), absorb(back_values))


def solution(mesh):
    return jax.shard_map(
        on_device,
        mesh=mesh,
        in_specs=(
            P(None, "ctx", "mp"),
            P(("ctx", "mp"), None),
            P(("ctx", "mp"), None),
            P(None, "ctx", "mp"),
            P("ctx", None),
        ),
        out_specs=(
            P(None, "ctx", "mp"),
            P(None, "ctx", "mp"),
            P(("ctx", "mp"), None),
            P(("ctx", "mp"), None),
        ),
        check_vma=False,
    )
```

time: 791 us -> 440 us (0.56); the launches traced: 779 us -> 439 us
  matrix products: 196 us -> 14.5 us
  local copies, waits for them, and re-layouts: 225 us -> 62.3 us
  other arithmetic: 70.7 us -> 1.34 us
  blocking collectives: 83.1 us -> 138 us
  Pallas kernels: 0 us -> 50.7 us
  starting transfers between devices: 37.1 us -> 16.7 us
  waiting for transfers between devices: 165 us -> 154 us
    dot_general x50 -> x2, matrix products: 188 us -> 6.82 us  [absorb(): jnp.dot(picker_full.T, block_grid.astype(jnp.float32), precision=lax.Prec...]
    all_gather x1 -> x0, blocking collectives: 83.1 us -> none  [on_device(): all_lists = lax.all_gather(reads, 'ctx', axis=0, tiled=True)]
    all_to_all x0 -> x1, blocking collectives: none -> 69.7 us  [return_grads(): lax.all_to_all(operands[0], ('ctx', 'mp'), split_axis=0, concat_axis=0, t...]
    psum x0 -> x1, blocking collectives: none -> 68.7 us  [on_device(): all_lists = lax.psum(placed, ('ctx', 'mp'))]
    convert_element_type x6 -> x0, local copies, waits for them, and re-layouts: 56.3 us -> none  [the longest x2 35.7 us: return_grads(): operands[0].astype(jnp.bfloat16)]
    pallas_call x0 -> x1, Pallas kernels: none -> 50.7 us  [attend(): pl.pallas_call(kernel, grid=(head_count, layer_count), in_specs=[pl.Block...]
    dynamic_update_slice x8 -> x0, other arithmetic: 39.6 us -> none  [first_pass(): lax.dynamic_update_slice_in_dim(stored, scores, group_id * group_span, 2)]
    reshape x5 -> x0, local copies, waits for them, and re-layouts: 38.3 us -> none  [the longest x2 15 us: absorb(): returned.reshape(ctx_count, mp_count, BLK, head_width).transpose(0, 2, 1, 3)]
  transfers between devices with their start and end apart: 4 -> 3, of which waited for: 4 -> 3; matrix products, arithmetic and copies ran while one was open for 12% -> 9% of each run, Pallas kernels for 0% -> 0%
where the time goes in v1:
time: 440 us; the launch traced here: 439 us
  waiting for transfers between devices  154 us (35%)
  blocking collectives  138 us (31%)
  local copies, waits for them, and re-layouts  62.3 us (14%)
  Pallas kernels  50.7 us (12%)
  starting transfers between devices  16.7 us (4%)
  matrix products  14.5 us (3%)
    all_to_all x1, blocking collectives, return_grads(): lax.all_to_all(operands[0], ('ctx', 'mp'), split_axis=0, concat_axis=0, t...  69.7 us
    psum x1, blocking collectives, on_device(): all_lists = lax.psum(placed, ('ctx', 'mp'))  68.7 us
    all_to_all x1, waiting for transfers between devices, fetch_blocks(): lax.all_to_all(operands[0], ('ctx', 'mp'), split_axis=0, concat_axis=0, t...  63.5 us
    pallas_call x1, Pallas kernels, attend(): pl.pallas_call(kernel, grid=(head_count, layer_count), in_specs=[pl.Block...  50.7 us
    all_to_all x1, waiting for transfers between devices, fetch_blocks(): lax.all_to_all(operands[1], ('ctx', 'mp'), split_axis=0, concat_axis=0, t...  45.9 us
    all_to_all x1, waiting for transfers between devices, return_grads(): lax.all_to_all(operands[1], ('ctx', 'mp'), split_axis=0, concat_axis=0, t...  44.3 us
    reshape x2, local copies, waits for them, and re-layouts, outgoing(): picked.reshape(ctx_count, BLK, mp_count, head_width).transpose(0, 2, 1, 3)  15.5 us
    transpose x2, local copies, waits for them, and re-layouts, absorb(): returned.reshape(ctx_count, mp_count, BLK, head_width).transpose(0, 2, 1, 3)  15 us
  transfers between devices with their start and end apart: 3, of which 3 were waited for; matrix products, arithmetic and copies ran while one was open for 9% of the time, Pallas kernels for 0%

profile of v1, /device:TPU:1, one launch (start us, length us, event | category | flops | bytes accessed | tf_op | source)
XLA Modules:
  0.0 438.5 jit_solution(2667938528909413304)
XLA Ops:
  0.7 0.7 broadcast_select_fusion
  1.4 68.7 %psum.7 = s32[32,96]{1,0:T(8,128)S(1)} all-reduce(s32[32,96]{1,0:T(8,128)S(1)} %broadcast_select_fusion), channel_id=1, replica_groups=mesh['ctx'=32,'mp'=4] {'ctx','mp'}, use_global_device_ids=true, to_apply=%region_2.3 | all-reduce | flops 3072 | bytes 24576 | tf_op jit(solution)/shard_map/psum | solution.py:138
  70.1 0.1 fusion.19
  70.2 1.7 reshape.160
  72.0 0.1 select_reduce_fusion.1
  72.1 3.9 convolution_convert_fusion
  76.0 7.7 %reshape.161 = bf16[32,16,4,1280]{3,2,1,0:T(4,128)(2,1)} reshape(bf16[32,81920]{1,0:T(8,128)(2,1)} %convolution_convert_fusion) | data formatting | bytes 10485760 | tf_op jit(solution)/shard_map/reshape | solution.py:151
  83.7 5.9 %copy.18 = bf16[32,4,16,1280]{3,2,1,0:T(8,128)(2,1)} copy(bf16[32,4,16,1280]{3,1,2,0:T(4,128)(2,1)} %bitcast.24) | data formatting | bytes 10485760 | tf_op jit(solution)/shard_map/transpose | solution.py:151
  89.7 0.0 copy-start.2
  89.7 5.6 %all-to-all-start.1 = ((bf16[128,16,1280]{2,1,0:T(8,128)(2,1)}), bf16[128,16,1280]{2,1,0:T(8,128)(2,1)}, u32[]{:S(2)}, u32[]{:S(2)}) async-start(bf16[128,16,1280]{2,1,0:T(8,128)(2,1)} %bitcast.22), calls=%async_computation.1 | async-start | bytes 10485760 | tf_op jit(solution)/shard_map/all_to_all | solution.py:21
  95.2 0.0 copy-done.2
  95.2 0.7 reshape.156
  96.0 3.8 convolution_convert_fusion.1
  99.8 7.7 %reshape.157 = bf16[32,16,4,1280]{3,2,1,0:T(4,128)(2,1)} reshape(bf16[32,81920]{1,0:T(8,128)(2,1)} %convolution_convert_fusion.1) | data formatting | bytes 10485760 | tf_op jit(solution)/shard_map/reshape | solution.py:151
  107.5 5.8 %copy.17 = bf16[32,4,16,1280]{3,2,1,0:T(8,128)(2,1)} copy(bf16[32,4,16,1280]{3,1,2,0:T(4,128)(2,1)} %bitcast.25) | data formatting | bytes 10485760 | tf_op jit(solution)/shard_map/transpose | solution.py:151
  113.3 45.9 %all-to-all-done.1 = bf16[128,16,1280]{2,1,0:T(8,128)(2,1)} async-done(((bf16[128,16,1280]{2,1,0:T(8,128)(2,1)}), bf16[128,16,1280]{2,1,0:T(8,128)(2,1)}, u32[]{:S(2)}, u32[]{:S(2)}) %all-to-all-start.1) | async-done | bytes 5242912 | tf_op jit(solution)/shard_map/all_to_all | solution.py:21
  159.2 0.0 copy-start.3
  159.2 0.0 copy-start
  159.2 0.0 copy-start.1
  159.2 5.7 %all-to-all-start = ((bf16[128,16,1280]{2,1,0:T(8,128)(2,1)}), bf16[128,16,1280]{2,1,0:T(8,128)(2,1)}, u32[]{:S(2)}, u32[]{:S(2)}) async-start(bf16[128,16,1280]{2,1,0:T(8,128)(2,1)} %bitcast.21), calls=%async_computation | async-start | bytes 10485760 | tf_op jit(solution)/shard_map/all_to_all | solution.py:20
  164.9 0.0 copy-done.3
  164.9 0.1 fusion.1
  165.0 0.1 select_reduce_fusion
  165.2 0.1 subtract_select_fusion
  165.3 0.1 select_n.44.kpos_ref
  165.4 63.5 %all-to-all-done = bf16[128,16,1280]{2,1,0:T(8,128)(2,1)} async-done(((bf16[128,16,1280]{2,1,0:T(8,128)(2,1)}), bf16[128,16,1280]{2,1,0:T(8,128)(2,1)}, u32[]{:S(2)}, u32[]{:S(2)}) %all-to-all-start) | async-done | bytes 5242912 | tf_op jit(solution)/shard_map/all_to_all | solution.py:20
  228.8 0.0 copy-done
  228.8 0.0 copy-done.1
  228.8 50.7 %shard_map.84 = (bf16[2,192,1280]{2,1,0:T(8,128)(2,1)}, bf16[2,192,1280]{2,1,0:T(8,128)(2,1)}, bf16[2048,1280]{1,0:T(8,128)(2,1)}, bf16[2048,1280]{1,0:T(8,128)(2,1)}) custom-call(s32[1,2048]{1,0:T(1,128)S(1)} %select_n.44.kpos_ref, bf16[2,192,1280]{2,1,0:T(8,128)(2,1)S(1)} %copy-done, bf16[2,192,1280]{2,1,0:T(8,128)(2,1)S(1)} %copy-done.1, ...), custom_call_target="tpu_custom_call" | custom-call | tf_op jit(solution)/shard_map/pallas_call | solution.py:94
  279.6 69.7 %all_to_all.20 = bf16[128,16,1280]{2,1,0:T(8,128)(2,1)} all-to-all(bf16[128,16,1280]{2,1,0:T(8,128)(2,1)} %bitcast.27), channel_id=1, replica_groups=mesh['ctx'=32,'mp'=4] {'ctx','mp'}, dimensions={0} | all-to-all | bytes 10485760 | tf_op jit(solution)/shard_map/all_to_all | solution.py:27
  349.3 5.5 %all-to-all-start.3 = ((bf16[128,16,1280]{2,1,0:T(8,128)(2,1)}), bf16[128,16,1280]{2,1,0:T(8,128)(2,1)}, u32[]{:S(2)}, u32[]{:S(2)}) async-start(bf16[128,16,1280]{2,1,0:T(8,128)(2,1)} %bitcast.26), calls=%async_computation.3 | async-start | bytes 10485760 | tf_op jit(solution)/shard_map/all_to_all | solution.py:28
  354.8 7.4 %copy.19 = bf16[32,16,4,1280]{3,2,1,0:T(4,128)(2,1)} copy(bf16[32,16,4,1280]{3,1,2,0:T(8,128)(2,1)} %bitcast.23) | data formatting | bytes 10485760 | tf_op jit(solution)/shard_map/transpose | solution.py:155
  362.2 7.1 %reshape.166 = bf16[32,81920]{1,0:T(8,128)(2,1)} reshape(bf16[32,16,4,1280]{3,2,1,0:T(4,128)(2,1)} %copy.19) | data formatting | bytes 10485760 | tf_op jit(solution)/shard_map/reshape | solution.py:156
  369.3 3.4 fusion.7
  372.7 1.7 reshape.167
  374.4 44.3 %all-to-all-done.3 = bf16[128,16,1280]{2,1,0:T(8,128)(2,1)} async-done(((bf16[128,16,1280]{2,1,0:T(8,128)(2,1)}), bf16[128,16,1280]{2,1,0:T(8,128)(2,1)}, u32[]{:S(2)}, u32[]{:S(2)}) %all-to-all-start.3) | async-done | bytes 5242912 | tf_op jit(solution)/shard_map/all_to_all | solution.py:28
  418.8 7.5 %copy.20 = bf16[32,16,4,1280]{3,2,1,0:T(4,128)(2,1)} copy(bf16[32,16,4,1280]{3,1,2,0:T(8,128)(2,1)} %bitcast.12) | data formatting | bytes 10485760 | tf_op jit(solution)/shard_map/transpose | solution.py:155
  426.3 7.1 %reshape.170 = bf16[32,81920]{1,0:T(8,128)(2,1)} reshape(bf16[32,16,4,1280]{3,2,1,0:T(4,128)(2,1)} %copy.20) | data formatting | bytes 10485760 | tf_op jit(solution)/shard_map/reshape | solution.py:156
  433.4 3.4 fusion.5
  436.8 1.7 reshape.171
  (5 shorter events, 0.0 us)
Async XLA Ops:
  89.7 5.6 %copy-start.2 = (bf16[48,5120]{1,0:T(8,128)(2,1)S(1)}, bf16[48,5120]{1,0:T(8,128)(2,1)}, u32[]{:S(2)}) copy-start(bf16[48,5120]{1,0:T(8,128)(2,1)} %param.6) | copy-start | bytes 1474564
  89.7 69.5 %all-to-all-start.1 = ((bf16[128,16,1280]{2,1,0:T(8,128)(2,1)}), bf16[128,16,1280]{2,1,0:T(8,128)(2,1)}, u32[]{:S(2)}, u32[]{:S(2)}) async-start(bf16[128,16,1280]{2,1,0:T(8,128)(2,1)} %bitcast.22), calls=%async_computation.1 | async-start | bytes 10485760 | tf_op jit(solution)/shard_map/all_to_all | solution.py:21
  159.2 5.7 %copy-start.3 = (s32[1,96]{1,0:T(1,128)S(1)}, s32[1,96]{1,0:T(1,128)}, u32[]{:S(2)}) copy-start(s32[1,96]{1,0:T(1,128)} %param.9) | copy-start | bytes 1156
  159.2 69.6 %copy-start = (bf16[2,192,1280]{2,1,0:T(8,128)(2,1)S(1)}, bf16[2,192,1280]{2,1,0:T(8,128)(2,1)}, u32[]{:S(2)}) copy-start(bf16[2,192,1280]{2,1,0:T(8,128)(2,1)} %q_ref.1) | copy-start | bytes 2949124
  159.2 69.6 %copy-start.1 = (bf16[2,192,1280]{2,1,0:T(8,128)(2,1)S(1)}, bf16[2,192,1280]{2,1,0:T(8,128)(2,1)}, u32[]{:S(2)}) copy-start(bf16[2,192,1280]{2,1,0:T(8,128)(2,1)} %do_ref.1) | copy-start | bytes 2949124
  159.2 69.6 %all-to-all-start = ((bf16[128,16,1280]{2,1,0:T(8,128)(2,1)}), bf16[128,16,1280]{2,1,0:T(8,128)(2,1)}, u32[]{:S(2)}, u32[]{:S(2)}) async-start(bf16[128,16,1280]{2,1,0:T(8,128)(2,1)} %bitcast.21), calls=%async_computation | async-start | bytes 10485760 | tf_op jit(solution)/shard_map/all_to_all | solution.py:20
  349.3 69.5 %all-to-all-start.3 = ((bf16[128,16,1280]{2,1,0:T(8,128)(2,1)}), bf16[128,16,1280]{2,1,0:T(8,128)(2,1)}, u32[]{:S(2)}, u32[]{:S(2)}) async-start(bf16[128,16,1280]{2,1,0:T(8,128)(2,1)} %bitcast.26), calls=%async_computation.3 | async-start | bytes 10485760 | tf_op jit(solution)/shard_map/all_to_all | solution.py:28

commit v2 on v1

v2 whole, which is shorter than its diff:
```python
import functools
import math

import jax
import jax.numpy as jnp
from jax import lax
from jax.experimental import pallas as pl
from jax.experimental.pallas import tpu as pltpu
from jax.sharding import PartitionSpec as P

HD = 128
BLK = 16

neg_big = -1e30
far_pos = 1 << 30


def exchange(operand):
    return lax.all_to_all(operand, ("ctx", "mp"), split_axis=0, concat_axis=0, tiled=True)


def attend_kernel(
    kpos_ref, q_ref, do_ref, kv_ref, o_ref, dq_ref, dkv_ref, dk_acc, dv_acc,
    *, factor, layer_count
):
    layer_id = pl.program_id(1)
    q = q_ref[0]
    do = do_ref[0]
    key_total = dk_acc.shape[0]
    k = kv_ref[:, 0].reshape(key_total, HD)
    v = kv_ref[:, 1].reshape(key_total, HD)
    tok_rows = q.shape[0]
    rows = lax.broadcasted_iota(jnp.int32, (tok_rows, 1), 0)
    visible = kpos_ref[...] <= rows
    scores = lax.dot_general(
        q, k, (((1,), (1,)), ((), ())), preferred_element_type=jnp.float32
    ) * factor
    scores = jnp.where(visible, scores, neg_big)
    row_top = jnp.max(scores, axis=1, keepdims=True)
    raised = jnp.exp(scores - row_top)
    row_total = jnp.sum(raised, axis=1, keepdims=True)
    probs = raised * (1.0 / row_total)
    probs_low = probs.astype(jnp.bfloat16)
    attended = jnp.dot(probs_low, v, preferred_element_type=jnp.float32).astype(jnp.bfloat16)
    o_ref[0] = attended
    row_delta = jnp.sum(
        do.astype(jnp.float32) * attended.astype(jnp.float32), axis=1, keepdims=True
    )
    d_probs = lax.dot_general(
        do, v, (((1,), (1,)), ((), ())), preferred_element_type=jnp.float32
    )
    d_scores = (probs * (d_probs - row_delta)).astype(jnp.bfloat16)
    dq = jnp.dot(d_scores, k, preferred_element_type=jnp.float32) * factor
    dq_ref[0] = dq.astype(jnp.bfloat16)
    dk = lax.dot_general(
        d_scores, q, (((0,), (0,)), ((), ())), preferred_element_type=jnp.float32
    ) * factor
    dv = lax.dot_general(
        probs_low, do, (((0,), (0,)), ((), ())), preferred_element_type=jnp.float32
    )

    @pl.when(layer_id == 0)
    def _():
        dk_acc[...] = dk
        dv_acc[...] = dv

    @pl.when(layer_id > 0)
    def _():
        dk_acc[...] += dk
        dv_acc[...] += dv

    @pl.when(layer_id == layer_count - 1)
    def _():
        dkv_ref[:, 0] = dk_acc[...].astype(jnp.bfloat16).reshape(dkv_ref.shape[0], BLK, HD)
        dkv_ref[:, 1] = dv_acc[...].astype(jnp.bfloat16).reshape(dkv_ref.shape[0], BLK, HD)


def attend(kpos_rel, queries, douts, kv_rows, factor):
    layer_count, tok_rows, head_width = queries.shape
    slot_count = kv_rows.shape[0]
    key_total = slot_count * BLK
    head_count = head_width // HD
    kernel = functools.partial(attend_kernel, factor=factor, layer_count=layer_count)
    tok_spec = pl.BlockSpec((1, tok_rows, HD), lambda h, l: (l, 0, h))
    kv_spec = pl.BlockSpec((slot_count, 2, BLK, HD), lambda h, l: (0, 0, 0, h))
    return pl.pallas_call(
        kernel,
        grid=(head_count, layer_count),
        in_specs=[
            pl.BlockSpec((1, key_total), lambda h, l: (0, 0)),
            tok_spec,
            tok_spec,
            kv_spec,
        ],
        out_specs=[tok_spec, tok_spec, kv_spec],
        out_shape=[
            jax.ShapeDtypeStruct(queries.shape, jnp.bfloat16),
            jax.ShapeDtypeStruct(queries.shape, jnp.bfloat16),
            jax.ShapeDtypeStruct(kv_rows.shape, jnp.bfloat16),
        ],
        scratch_shapes=[
            pltpu.VMEM((key_total, HD), jnp.float32),
            pltpu.VMEM((key_total, HD), jnp.float32),
        ],
        compiler_params=pltpu.CompilerParams(
            dimension_semantics=("arbitrary", "arbitrary"),
            vmem_limit_bytes=48 * 1024 * 1024,
        ),
    )(kpos_rel, queries, douts, kv_rows)


def on_device(queries, cache_keys, cache_values, douts, reads):
    layer_count, tok_rows, head_width = queries.shape
    kv_rows, full_width = cache_keys.shape
    ctx_count = lax.axis_size("ctx")
    mp_count = lax.axis_size("mp")
    owner_count = ctx_count * mp_count
    per_owner = kv_rows // BLK
    my_owner = lax.axis_index(("ctx", "mp"))
    my_stretch = lax.axis_index("ctx")
    my_mp = lax.axis_index("mp")
    factor = 1.0 / math.sqrt(HD)
    spread = jnp.broadcast_to(reads, (owner_count, reads.shape[1]))
    all_lists = exchange(spread).reshape(ctx_count, mp_count, -1)[:, 0, :]
    owner_hit = (all_lists >= 0) & (all_lists // per_owner == my_owner)
    chosen = jnp.sum(jnp.where(owner_hit, all_lists - my_owner * per_owner, 0), axis=1)
    wanted = jnp.any(owner_hit, axis=1)
    picker = (chosen[:, None] == jnp.arange(per_owner, dtype=jnp.int32)[None, :]) & wanted[:, None]
    picker_low = picker.astype(jnp.bfloat16)

    def by_block(cache_rows):
        return cache_rows.reshape(per_owner, BLK, mp_count, head_width).transpose(0, 2, 1, 3)

    def outgoing():
        block_grid = jnp.stack([by_block(cache_keys), by_block(cache_values)], axis=2)
        block_grid = block_grid.reshape(per_owner, mp_count * 2 * BLK * head_width)
        picked = jnp.dot(picker_low, block_grid, preferred_element_type=jnp.float32)
        return picked.astype(jnp.bfloat16).reshape(owner_count, 2, BLK, head_width)

    def absorb(returned):
        block_grid = returned.reshape(ctx_count, mp_count * 2 * BLK * head_width)
        summed = jnp.dot(picker_low.T, block_grid, preferred_element_type=jnp.float32)
        summed = summed.reshape(per_owner, mp_count, 2, BLK, head_width).transpose(2, 0, 3, 1, 4)
        summed = summed.reshape(2, kv_rows, full_width)
        return summed[0], summed[1]

    own_list = reads[0]
    owner_ids = jnp.arange(owner_count, dtype=jnp.int32)
    slot_hit = (own_list[:, None] >= 0) & (own_list[:, None] // per_owner == owner_ids[None, :])
    slot_live = jnp.any(slot_hit, axis=0)
    slot_block = jnp.sum(
        jnp.where(slot_hit, own_list[:, None] - owner_ids[None, :] * per_owner, 0), axis=0
    )
    slot_start = owner_ids * kv_rows + slot_block * BLK
    key_pos = (slot_start[:, None] + jnp.arange(BLK, dtype=jnp.int32)[None, :]).reshape(-1)
    key_live = jnp.repeat(slot_live, BLK)
    kpos_rel = jnp.where(key_live, key_pos - my_stretch * tok_rows, far_pos)
    kpos_rel = kpos_rel.reshape(1, -1).astype(jnp.int32)
    kv_rows_got = exchange(outgoing())
    attended, d_query, kv_grads = attend(kpos_rel, queries, douts, kv_rows_got, factor)
    grad_keys, grad_values = absorb(exchange(kv_grads))
    return (attended, d_query, grad_keys, grad_values)


def solution(mesh):
    return jax.shard_map(
        on_device,
        mesh=mesh,
        in_specs=(
            P(None, "ctx", "mp"),
            P(("ctx", "mp"), None),
            P(("ctx", "mp"), None),
            P(None, "ctx", "mp"),
            P("ctx", None),
        ),
        out_specs=(
            P(None, "ctx", "mp"),
            P(None, "ctx", "mp"),
            P(("ctx", "mp"), None),
            P(("ctx", "mp"), None),
        ),
        check_vma=False,
    )
```

time: 440 us -> 396 us (0.900)
  waiting for transfers between devices: 154 us -> 128 us
  local copies, waits for them, and re-layouts: 62.3 us -> 40.3 us
  matrix products: 14.5 us -> 21 us
    psum x1 -> x0, blocking collectives: 68.7 us -> none  [on_device(): all_lists = lax.psum(placed, ('ctx', 'mp'))]
    all_to_all x1, blocking collectives: 69.7 us -> 137 us  [exchange(): lax.all_to_all(operand, ('ctx', 'mp'), split_axis=0, concat_axis=0, tiled...]
    transpose x4 -> x0, local copies, waits for them, and re-layouts: 26.7 us -> none  [the longest x2 15 us: absorb(): returned.reshape(ctx_count, mp_count, BLK, head_width).transpose(0, 2, 1, 3)]
    all_to_all x3 -> x2, waiting for transfers between devices: 154 us -> 128 us  [exchange(): lax.all_to_all(operand, ('ctx', 'mp'), split_axis=0, concat_axis=0, tiled...]
    unnamed x8 -> x10, local copies, waits for them, and re-layouts: 0.01 us -> 13.5 us
    reshape x8 -> x4, local copies, waits for them, and re-layouts: 35.5 us -> 23.6 us  [the longest x1 10.4 us: absorb(): block_grid = returned.reshape(ctx_count, mp_count * 2 * BLK * head_width)]
    dot_general x4 -> x2, matrix products: 14.5 us -> 21 us  [the longest x1 15.5 us: absorb(): jnp.dot(picker_low.T, block_grid, preferred_element_type=jnp.float32)]
    all_to_all x3 -> x2, starting transfers between devices: 16.7 us -> 17 us  [exchange(): lax.all_to_all(operand, ('ctx', 'mp'), split_axis=0, concat_axis=0, tiled...]
  transfers between devices with their start and end apart: 3 -> 2, of which waited for: 3 -> 2; matrix products, arithmetic and copies ran while one was open for 9% -> 1% of each run, Pallas kernels for 0% -> 0%
where the time goes in v2:
time: 396 us
  blocking collectives  137 us (35%)
  waiting for transfers between devices  128 us (32%)
  Pallas kernels  50.6 us (13%)
  local copies, waits for them, and re-layouts  40.3 us (10%)
  matrix products  21 us (5%)
  starting transfers between devices  17 us (4%)
    all_to_all x1, blocking collectives, exchange(): lax.all_to_all(operand, ('ctx', 'mp'), split_axis=0, concat_axis=0, tiled...  137 us
    all_to_all x2, waiting for transfers between devices, exchange(): lax.all_to_all(operand, ('ctx', 'mp'), split_axis=0, concat_axis=0, tiled...  128 us
    pallas_call x1, Pallas kernels, attend(): pl.pallas_call(kernel, grid=(head_count, layer_count), in_specs=[pl.Block...  50.6 us
    all_to_all x2, starting transfers between devices, exchange(): lax.all_to_all(operand, ('ctx', 'mp'), split_axis=0, concat_axis=0, tiled...  17 us
    dot_general x1, matrix products, absorb(): jnp.dot(picker_low.T, block_grid, preferred_element_type=jnp.float32)  15.5 us
    unnamed x10, local copies, waits for them, and re-layouts  13.5 us
    reshape x1, local copies, waits for them, and re-layouts, absorb(): block_grid = returned.reshape(ctx_count, mp_count * 2 * BLK * head_width)  10.4 us
    reshape x1, local copies, waits for them, and re-layouts, outgoing(): return picked.astype(jnp.bfloat16).reshape(owner_count, 2, BLK, head_width)  10.4 us
  transfers between devices with their start and end apart: 2, of which 2 were waited for; matrix products, arithmetic and copies ran while one was open for 1% of the time, Pallas kernels for 0%

profile of v2, /device:TPU:1, one launch (start us, length us, event | category | flops | bytes accessed | tf_op | source)
XLA Modules:
  0.0 395.6 jit_solution(9190968283798677668)
XLA Ops:
  0.6 1.3 broadcast_in_dim.28
  1.9 11.5 %all-to-all-start = ((s32[128,1,96]{2,1,0:T(1,128)}), s32[128,1,96]{2,1,0:T(1,128)S(1)}, u32[]{:S(2)}, u32[]{:S(2)}) async-start(s32[128,1,96]{2,1,0:T(1,128)} %broadcast_in_dim.28), calls=%async_computation | async-start | bytes 131072 | tf_op jit(solution)/shard_map/all_to_all | solution.py:19
  13.4 1.4 reshape.149
  14.8 1.4 reshape.150
  16.2 0.1 copy_bitcast_fusion
  16.4 0.1 pad_maximum_fusion
  16.5 0.8 copy.46
  17.3 5.7 %all-to-all-done = s32[128,1,96]{2,1,0:T(1,128)S(1)} async-done(((s32[128,1,96]{2,1,0:T(1,128)}), s32[128,1,96]{2,1,0:T(1,128)S(1)}, u32[]{:S(2)}, u32[]{:S(2)}) %all-to-all-start) | async-done | bytes 49184 | tf_op jit(solution)/shard_map/all_to_all | solution.py:19
  23.0 0.1 fusion.18
  23.2 0.1 select_reduce_fusion.1
  23.3 5.6 %convolution_convert_fusion = bf16[32,163840]{1,0:T(8,128)(2,1)} fusion(bf16[3,163840]{1,0:T(4,128)(2,1)S(1)} %bitcast.59, s32[32]{0:T(128)S(1)} %select_reduce_fusion.1, pred[32]{0:T(512)(128)(4,1)S(1)} %get-tuple-element.10), kind=kOutput, calls=%fused_computation | convolution fusion | flops 36700352 | bytes 11468960 | tf_op jit(solution)/shard_map/dot_general | solution.py:137
  28.8 10.4 %reshape.152 = bf16[128,2,16,1280]{3,2,1,0:T(8,128)(2,1)} reshape(bf16[32,163840]{1,0:T(8,128)(2,1)} %convolution_convert_fusion) | data formatting | bytes 20971520 | tf_op jit(solution)/shard_map/reshape | solution.py:138
  39.2 0.0 copy-start.2
  39.2 0.0 copy-start
  39.2 0.0 copy-start.1
  39.2 5.5 %all-to-all-start.1 = ((bf16[128,2,16,1280]{3,2,1,0:T(8,128)(2,1)}), bf16[128,2,16,1280]{3,2,1,0:T(8,128)(2,1)}, u32[]{:S(2)}, u32[]{:S(2)}) async-start(bf16[128,2,16,1280]{3,2,1,0:T(8,128)(2,1)} %reshape.152), calls=%async_computation.1 | async-start | bytes 20971520 | tf_op jit(solution)/shard_map/all_to_all | solution.py:19
  44.8 0.0 copy-done.2
  44.8 0.1 fusion.6
  44.9 0.1 select_reduce_fusion
  45.1 0.1 subtract_select_fusion
  45.2 0.1 select_n.40.kpos_ref
  45.3 122.6 %all-to-all-done.1.kv_ref = bf16[128,2,16,1280]{3,2,1,0:T(8,128)(2,1)} async-done(((bf16[128,2,16,1280]{3,2,1,0:T(8,128)(2,1)}), bf16[128,2,16,1280]{3,2,1,0:T(8,128)(2,1)}, u32[]{:S(2)}, u32[]{:S(2)}) %all-to-all-start.1) | async-done | bytes 10485792 | tf_op jit(solution)/shard_map/all_to_all | solution.py:19
  167.9 0.0 copy-done
  167.9 0.0 copy-done.1
  167.9 50.6 %shard_map.84 = (bf16[2,192,1280]{2,1,0:T(8,128)(2,1)}, bf16[2,192,1280]{2,1,0:T(8,128)(2,1)}, bf16[128,2,16,1280]{3,2,1,0:T(8,128)(2,1)}) custom-call(s32[1,2048]{1,0:T(1,128)S(1)} %select_n.40.kpos_ref, bf16[2,192,1280]{2,1,0:T(8,128)(2,1)S(1)} %copy-done, bf16[2,192,1280]{2,1,0:T(8,128)(2,1)S(1)} %copy-done.1, ...), custom_call_target="tpu_custom_call" | custom-call | tf_op jit(solution)/shard_map/pallas_call | solution.py:86
  218.5 136.9 %all_to_all.16 = bf16[128,2,16,1280]{3,2,1,0:T(8,128)(2,1)} all-to-all(bf16[128,2,16,1280]{3,2,1,0:T(8,128)(2,1)} %get-tuple-element.9), channel_id=1, replica_groups=mesh['ctx'=32,'mp'=4] {'ctx','mp'}, dimensions={0} | all-to-all | bytes 20971520 | tf_op jit(solution)/shard_map/all_to_all | solution.py:19
  355.4 10.4 %reshape.153 = bf16[32,163840]{1,0:T(8,128)(2,1)} reshape(bf16[128,2,16,1280]{3,2,1,0:T(8,128)(2,1)} %all_to_all.16) | data formatting | bytes 20971520 | tf_op jit(solution)/shard_map/reshape | solution.py:141
  365.8 10.4 %copy.47 = bf16[4,8,128,1280]{3,2,1,0:T(8,128)(2,1)} copy(bf16[4,8,128,1280]{3,1,2,0:T(8,128)(2,1)} %bitcast.58) | data formatting | bytes 20971520
  376.2 15.5 %fusion.2 = f32[2,3,16,4,1280]{4,1,2,0,3:T(4,128)S(1)} fusion(bf16[4,2,16,1280,32]{3,2,1,0,4:T(8,128)(2,1)} %bitcast.57, s32[32]{0:T(128)S(1)} %select_reduce_fusion.1, pred[32]{0:T(512)(128)(4,1)S(1)} %get-tuple-element.10), kind=kOutput, calls=%fused_computation.3 | convolution fusion | flops 31457472 | bytes 12452000 | tf_op jit(solution)/shard_map/dot_general | solution.py:142
  391.7 0.5 fusion.19
  392.1 0.6 copy.44
  392.8 1.1 copy.49
  393.9 0.6 copy.43
  394.5 1.1 copy.48
  (5 shorter events, 0.0 us)
Async XLA Ops:
  1.9 21.1 %all-to-all-start = ((s32[128,1,96]{2,1,0:T(1,128)}), s32[128,1,96]{2,1,0:T(1,128)S(1)}, u32[]{:S(2)}, u32[]{:S(2)}) async-start(s32[128,1,96]{2,1,0:T(1,128)} %broadcast_in_dim.28), calls=%async_computation | async-start | bytes 131072 | tf_op jit(solution)/shard_map/all_to_all | solution.py:19
  39.2 5.6 %copy-start.2 = (s32[1,96]{1,0:T(1,128)S(1)}, s32[1,96]{1,0:T(1,128)}, u32[]{:S(2)}) copy-start(s32[1,96]{1,0:T(1,128)} %param.9) | copy-start | bytes 1156
  39.2 128.7 %copy-start = (bf16[2,192,1280]{2,1,0:T(8,128)(2,1)S(1)}, bf16[2,192,1280]{2,1,0:T(8,128)(2,1)}, u32[]{:S(2)}) copy-start(bf16[2,192,1280]{2,1,0:T(8,128)(2,1)} %q_ref.1) | copy-start | bytes 2949124
  39.2 128.7 %copy-start.1 = (bf16[2,192,1280]{2,1,0:T(8,128)(2,1)S(1)}, bf16[2,192,1280]{2,1,0:T(8,128)(2,1)}, u32[]{:S(2)}) copy-start(bf16[2,192,1280]{2,1,0:T(8,128)(2,1)} %do_ref.1) | copy-start | bytes 2949124
  39.2 128.6 %all-to-all-start.1 = ((bf16[128,2,16,1280]{3,2,1,0:T(8,128)(2,1)}), bf16[128,2,16,1280]{3,2,1,0:T(8,128)(2,1)}, u32[]{:S(2)}, u32[]{:S(2)}) async-start(bf16[128,2,16,1280]{3,2,1,0:T(8,128)(2,1)} %reshape.152), calls=%async_computation.1 | async-start | bytes 20971520 | tf_op jit(solution)/shard_map/all_to_all | solution.py:19

commit v3 on v2

--- a/solution.py
+++ b/solution.py
@@ -133,15 +133,18 @@
 
     def outgoing():
         block_grid = jnp.stack([by_block(cache_keys), by_block(cache_values)], axis=2)
-        block_grid = block_grid.reshape(per_owner, mp_count * 2 * BLK * head_width)
-        picked = jnp.dot(picker_low, block_grid, preferred_element_type=jnp.float32)
-        return picked.astype(jnp.bfloat16).reshape(owner_count, 2, BLK, head_width)
+        picked = jnp.zeros((ctx_count,) + block_grid.shape[1:], jnp.bfloat16)
+        for block_id in range(per_owner):
+            hit = picker[:, block_id].reshape(ctx_count, 1, 1, 1, 1)
+            picked = jnp.where(hit, block_grid[block_id][None], picked)
+        return picked.reshape(owner_count, 2, BLK, head_width)
 
     def absorb(returned):
-        block_grid = returned.reshape(ctx_count, mp_count * 2 * BLK * head_width)
-        summed = jnp.dot(picker_low.T, block_grid, preferred_element_type=jnp.float32)
-        summed = summed.reshape(per_owner, mp_count, 2, BLK, head_width).transpose(2, 0, 3, 1, 4)
-        summed = summed.reshape(2, kv_rows, full_width)
+        block_grid = returned.reshape(ctx_count, mp_count, 2, BLK, head_width)
+        summed = lax.dot_general(
+            picker_low, block_grid, (((0,), (0,)), ((), ())), preferred_element_type=jnp.float32
+        )
+        summed = summed.transpose(2, 0, 3, 1, 4).reshape(2, kv_rows, full_width)
         return summed[0], summed[1]
 
     own_list = reads[0]

time: 396 us -> 358 us (0.904)
  local copies, waits for them, and re-layouts: 40.3 us -> 8.86 us
  matrix products: 21 us -> 6.92 us
  other arithmetic: 0.71 us -> 8.14 us
    reshape x2 -> x0, local copies, waits for them, and re-layouts: 20.8 us -> none  [the longest x1 10.4 us: absorb(): block_grid = returned.reshape(ctx_count, mp_count * 2 * BLK * head_width)]
    dot_general x2 -> x1, matrix products: 21 us -> 6.92 us  [absorb(): lax.dot_general(picker_low, block_grid, (((0,), (0,)), ((), ())), preferr...]
    unnamed x10 -> x8, local copies, waits for them, and re-layouts: 13.5 us -> 2.24 us
    select_n x0 -> x1, other arithmetic: none -> 6.78 us  [outgoing(): picked = jnp.where(hit, block_grid[block_id][None], picked)]
where the time goes in v3:
time: 358 us
  blocking collectives  137 us (38%)
  waiting for transfers between devices  128 us (36%)
  Pallas kernels  50.5 us (14%)
  starting transfers between devices  17 us (5%)
  local copies, waits for them, and re-layouts  8.86 us (2%)
  other arithmetic  8.14 us (2%)
  matrix products  6.92 us (2%)
    all_to_all x1, blocking collectives, exchange(): lax.all_to_all(operand, ('ctx', 'mp'), split_axis=0, concat_axis=0, tiled...  137 us
    all_to_all x2, waiting for transfers between devices, exchange(): lax.all_to_all(operand, ('ctx', 'mp'), split_axis=0, concat_axis=0, tiled...  128 us
    pallas_call x1, Pallas kernels, attend(): pl.pallas_call(kernel, grid=(head_count, layer_count), in_specs=[pl.Block...  50.5 us
    all_to_all x2, starting transfers between devices, exchange(): lax.all_to_all(operand, ('ctx', 'mp'), split_axis=0, concat_axis=0, tiled...  17 us
  transfers between devices with their start and end apart: 2, of which 2 were waited for; matrix products, arithmetic and copies ran while one was open for 1% of the time, Pallas kernels for 0%

profile of v3, /device:TPU:1, one launch (start us, length us, event | category | flops | bytes accessed | tf_op | source)
XLA Modules:
  0.0 357.6 jit_solution(10444288667367135427)
XLA Ops:
  0.6 1.3 broadcast_in_dim.97
  1.9 11.5 %all-to-all-start = ((s32[128,1,96]{2,1,0:T(1,128)}), s32[128,1,96]{2,1,0:T(1,128)S(1)}, u32[]{:S(2)}, u32[]{:S(2)}) async-start(s32[128,1,96]{2,1,0:T(1,128)} %broadcast_in_dim.97), calls=%async_computation | async-start | bytes 131072 | tf_op jit(solution)/shard_map/all_to_all | solution.py:19
  13.4 1.4 reshape.151
  14.8 1.4 reshape.152
  16.2 0.7 fusion.10
  17.1 5.9 %all-to-all-done = s32[128,1,96]{2,1,0:T(1,128)S(1)} async-done(((s32[128,1,96]{2,1,0:T(1,128)}), s32[128,1,96]{2,1,0:T(1,128)S(1)}, u32[]{:S(2)}, u32[]{:S(2)}) %all-to-all-start) | async-done | bytes 49184 | tf_op jit(solution)/shard_map/all_to_all | solution.py:19
  23.0 0.1 fusion.19
  23.2 0.1 select_reduce_fusion.1
  23.3 0.1 broadcast_in_dim.99
  23.4 0.1 broadcast_in_dim.100
  23.5 0.1 broadcast_in_dim.113
  23.6 0.1 broadcast_in_dim.114
  23.7 0.1 broadcast_in_dim.106
  23.8 0.1 broadcast_in_dim.107
  23.9 6.8 %fusion.1 = bf16[128,2,16,1280]{3,2,1,0:T(8,128)(2,1)} fusion(pred[128]{0:T(512)(128)(4,1)S(1)} %broadcast_in_dim.114, pred[128]{0:T(512)(128)(4,1)S(1)} %broadcast_in_dim.107, pred[128]{0:T(512)(128)(4,1)S(1)} %broadcast_in_dim.100, bf16[4,2,16,1280]{3,2,1,0:T(8,128)(2,1)S(1)} %copy.49, bf16[4,2,16,1280]{3,2,1,0:T(8,128)(2,1)S(1)} %copy.48, ...), kind=kLoop, calls=%fused_computation.2 | loop fusion | flops 15728640 | bytes 11469184 | tf_op jit(solution)/shard_map/jit(_where)/select_n | solution.py:139
  30.7 0.0 copy-start.2
  30.7 0.0 copy-start
  30.7 0.0 copy-start.1
  30.7 5.5 %all-to-all-start.1 = ((bf16[128,2,16,1280]{3,2,1,0:T(8,128)(2,1)}), bf16[128,2,16,1280]{3,2,1,0:T(8,128)(2,1)}, u32[]{:S(2)}, u32[]{:S(2)}) async-start(bf16[128,2,16,1280]{3,2,1,0:T(8,128)(2,1)} %fusion.1), calls=%async_computation.1 | async-start | bytes 20971520 | tf_op jit(solution)/shard_map/all_to_all | solution.py:19
  36.2 0.0 copy-done.2
  36.3 0.1 fusion.13
  36.4 0.1 select_reduce_fusion
  36.5 0.1 subtract_select_fusion
  36.6 0.1 select_n.53.kpos_ref
  36.7 122.6 %all-to-all-done.1.kv_ref = bf16[128,2,16,1280]{3,2,1,0:T(8,128)(2,1)} async-done(((bf16[128,2,16,1280]{3,2,1,0:T(8,128)(2,1)}), bf16[128,2,16,1280]{3,2,1,0:T(8,128)(2,1)}, u32[]{:S(2)}, u32[]{:S(2)}) %all-to-all-start.1) | async-done | bytes 10485792 | tf_op jit(solution)/shard_map/all_to_all | solution.py:19
  159.3 0.0 copy-done
  159.3 0.0 copy-done.1
  159.3 50.5 %shard_map.84 = (bf16[2,192,1280]{2,1,0:T(8,128)(2,1)}, bf16[2,192,1280]{2,1,0:T(8,128)(2,1)}, bf16[128,2,16,1280]{3,2,1,0:T(8,128)(2,1)}) custom-call(s32[1,2048]{1,0:T(1,128)S(1)} %select_n.53.kpos_ref, bf16[2,192,1280]{2,1,0:T(8,128)(2,1)S(1)} %copy-done, bf16[2,192,1280]{2,1,0:T(8,128)(2,1)S(1)} %copy-done.1, ...), custom_call_target="tpu_custom_call" | custom-call | tf_op jit(solution)/shard_map/pallas_call | solution.py:86
  209.8 136.9 %all_to_all.16 = bf16[128,2,16,1280]{3,2,1,0:T(8,128)(2,1)S(1)} all-to-all(bf16[128,2,16,1280]{3,2,1,0:T(8,128)(2,1)} %get-tuple-element.9), channel_id=1, replica_groups=mesh['ctx'=32,'mp'=4] {'ctx','mp'}, dimensions={0} | all-to-all | bytes 20971520 | tf_op jit(solution)/shard_map/all_to_all | solution.py:19
  346.7 6.9 %fusion.4 = f32[2,3,16,4,1280]{4,1,2,0,3:T(4,128)S(1)} fusion(bf16[32,4,2,16,1280]{4,3,2,1,0:T(8,128)(2,1)S(1)} %bitcast.66, pred[32,3]{0,1:T(4,128)(4,1)S(1)} %fusion.17), kind=kOutput, calls=%fused_computation.5 | convolution fusion | flops 31457280 | bytes 12451936 | tf_op jit(solution)/shard_map/dot_general | solution.py:144
  353.6 0.5 fusion.20
  354.1 0.6 copy.52
  354.7 1.1 copy.55
  355.9 0.6 copy.51
  356.5 1.1 copy.54
  (10 shorter events, 0.2 us)
Async XLA Ops:
  1.9 21.1 %all-to-all-start = ((s32[128,1,96]{2,1,0:T(1,128)}), s32[128,1,96]{2,1,0:T(1,128)S(1)}, u32[]{:S(2)}, u32[]{:S(2)}) async-start(s32[128,1,96]{2,1,0:T(1,128)} %broadcast_in_dim.97), calls=%async_computation | async-start | bytes 131072 | tf_op jit(solution)/shard_map/all_to_all | solution.py:19
  30.7 5.6 %copy-start.2 = (s32[1,96]{1,0:T(1,128)S(1)}, s32[1,96]{1,0:T(1,128)}, u32[]{:S(2)}) copy-start(s32[1,96]{1,0:T(1,128)} %param.9) | copy-start | bytes 1156
  30.7 128.6 %copy-start = (bf16[2,192,1280]{2,1,0:T(8,128)(2,1)S(1)}, bf16[2,192,1280]{2,1,0:T(8,128)(2,1)}, u32[]{:S(2)}) copy-start(bf16[2,192,1280]{2,1,0:T(8,128)(2,1)} %q_ref.1) | copy-start | bytes 2949124
  30.7 128.6 %copy-start.1 = (bf16[2,192,1280]{2,1,0:T(8,128)(2,1)S(1)}, bf16[2,192,1280]{2,1,0:T(8,128)(2,1)}, u32[]{:S(2)}) copy-start(bf16[2,192,1280]{2,1,0:T(8,128)(2,1)} %do_ref.1) | copy-start | bytes 2949124
  30.7 128.6 %all-to-all-start.1 = ((bf16[128,2,16,1280]{3,2,1,0:T(8,128)(2,1)}), bf16[128,2,16,1280]{3,2,1,0:T(8,128)(2,1)}, u32[]{:S(2)}, u32[]{:S(2)}) async-start(bf16[128,2,16,1280]{3,2,1,0:T(8,128)(2,1)} %fusion.1), calls=%async_computation.1 | async-start | bytes 20971520 | tf_op jit(solution)/shard_map/all_to_all | solution.py:19

commit v4 on v3

--- a/solution.py
+++ b/solution.py
@@ -75,27 +75,29 @@
         dkv_ref[:, 1] = dv_acc[...].astype(jnp.bfloat16).reshape(dkv_ref.shape[0], BLK, HD)
 
 
-def attend(kpos_rel, queries, douts, kv_rows, factor):
-    layer_count, tok_rows, head_width = queries.shape
-    slot_count = kv_rows.shape[0]
+def attend(kpos_rel, queries, douts, kv_rows, factor, head_offset):
+    layer_count, tok_rows, _ = queries.shape
+    slot_count, _, _, chunk_width = kv_rows.shape
     key_total = slot_count * BLK
-    head_count = head_width // HD
+    head_count = chunk_width // HD
     kernel = functools.partial(attend_kernel, factor=factor, layer_count=layer_count)
-    tok_spec = pl.BlockSpec((1, tok_rows, HD), lambda h, l: (l, 0, h))
+    tok_in = pl.BlockSpec((1, tok_rows, HD), lambda h, l: (l, 0, h + head_offset))
+    tok_out = pl.BlockSpec((1, tok_rows, HD), lambda h, l: (l, 0, h))
     kv_spec = pl.BlockSpec((slot_count, 2, BLK, HD), lambda h, l: (0, 0, 0, h))
+    tok_shape = (layer_count, tok_rows, chunk_width)
     return pl.pallas_call(
         kernel,
         grid=(head_count, layer_count),
         in_specs=[
             pl.BlockSpec((1, key_total), lambda h, l: (0, 0)),
-            tok_spec,
-            tok_spec,
+            tok_in,
+            tok_in,
             kv_spec,
         ],
-        out_specs=[tok_spec, tok_spec, kv_spec],
+        out_specs=[tok_out, tok_out, kv_spec],
         out_shape=[
-            jax.ShapeDtypeStruct(queries.shape, jnp.bfloat16),
-            jax.ShapeDtypeStruct(queries.shape, jnp.bfloat16),
+            jax.ShapeDtypeStruct(tok_shape, jnp.bfloat16),
+            jax.ShapeDtypeStruct(tok_shape, jnp.bfloat16),
             jax.ShapeDtypeStruct(kv_rows.shape, jnp.bfloat16),
         ],
         scratch_shapes=[
@@ -131,21 +133,22 @@
     def by_block(cache_rows):
         return cache_rows.reshape(per_owner, BLK, mp_count, head_width).transpose(0, 2, 1, 3)
 
-    def outgoing():
-        block_grid = jnp.stack([by_block(cache_keys), by_block(cache_values)], axis=2)
-        picked = jnp.zeros((ctx_count,) + block_grid.shape[1:], jnp.bfloat16)
+    block_grid = jnp.stack([by_block(cache_keys), by_block(cache_values)], axis=2)
+    chunk_width = (head_width // HD // 2) * HD
+    chunk_grids = (block_grid[..., :chunk_width], block_grid[..., chunk_width:])
+
+    def outgoing(chunk_grid):
+        picked = jnp.zeros((ctx_count,) + chunk_grid.shape[1:], jnp.bfloat16)
         for block_id in range(per_owner):
             hit = picker[:, block_id].reshape(ctx_count, 1, 1, 1, 1)
-            picked = jnp.where(hit, block_grid[block_id][None], picked)
-        return picked.reshape(owner_count, 2, BLK, head_width)
+            picked = jnp.where(hit, chunk_grid[block_id][None], picked)
+        return picked.reshape((owner_count,) + chunk_grid.shape[2:])
 
     def absorb(returned):
-        block_grid = returned.reshape(ctx_count, mp_count, 2, BLK, head_width)
-        summed = lax.dot_general(
+        block_grid = returned.reshape((ctx_count, mp_count) + returned.shape[1:])
+        return lax.dot_general(
             picker_low, block_grid, (((0,), (0,)), ((), ())), preferred_element_type=jnp.float32
         )
-        summed = summed.transpose(2, 0, 3, 1, 4).reshape(2, kv_rows, full_width)
-        return summed[0], summed[1]
 
     own_list = reads[0]
     owner_ids = jnp.arange(owner_count, dtype=jnp.int32)
@@ -159,10 +162,24 @@
     key_live = jnp.repeat(slot_live, BLK)
     kpos_rel = jnp.where(key_live, key_pos - my_stretch * tok_rows, far_pos)
     kpos_rel = kpos_rel.reshape(1, -1).astype(jnp.int32)
-    kv_rows_got = exchange(outgoing())
-    attended, d_query, kv_grads = attend(kpos_rel, queries, douts, kv_rows_got, factor)
-    grad_keys, grad_values = absorb(exchange(kv_grads))
-    return (attended, d_query, grad_keys, grad_values)
+    src_ctx = jnp.arange(owner_count, dtype=jnp.int32) // mp_count
+    kv_first = exchange(outgoing(chunk_grids[0]))
+    out_first, dq_first, grads_first = attend(kpos_rel, queries, douts, kv_first, factor, 0)
+    later = (src_ctx >= my_stretch).reshape(owner_count, 1, 1, 1)
+    mixed = exchange(jnp.where(later, outgoing(chunk_grids[1]), grads_first))
+    own_grads = lax.dynamic_slice_in_dim(grads_first, my_stretch * mp_count, mp_count, 0)
+    own_back = lax.all_to_all(own_grads, "mp", split_axis=0, concat_axis=0, tiled=True)
+    back_first = lax.dynamic_update_slice_in_dim(mixed, own_back, my_stretch * mp_count, 0)
+    head_offset = chunk_width // HD
+    out_second, dq_second, grads_second = attend(
+        kpos_rel, queries, douts, mixed, factor, head_offset
+    )
+    back_second = exchange(grads_second)
+    summed = jnp.concatenate([absorb(back_first), absorb(back_second)], axis=-1)
+    summed = summed.transpose(2, 0, 3, 1, 4).reshape(2, kv_rows, full_width)
+    attended = jnp.concatenate([out_first, out_second], axis=-1)
+    d_query = jnp.concatenate([dq_first, dq_second], axis=-1)
+    return (attended, d_query, summed[0], summed[1])
 
 
 def solution(mesh):

time: 358 us -> 312 us (0.87)
  blocking collectives: 137 us -> 0 us
  waiting for transfers between devices: 128 us -> 186 us
  starting transfers between devices: 17 us -> 32.4 us
  other arithmetic: 8.14 us -> 13.3 us
  matrix products: 6.92 us -> 12 us
  local copies, waits for them, and re-layouts: 8.86 us -> 12.9 us
    all_to_all x1 -> x0, blocking collectives: 137 us -> none  [exchange(): lax.all_to_all(operand, ('ctx', 'mp'), split_axis=0, concat_axis=0, tiled...]
    all_to_all x2 -> x4, waiting for transfers between devices: 128 us -> 186 us  [exchange(): lax.all_to_all(operand, ('ctx', 'mp'), split_axis=0, concat_axis=0, tiled...]
    all_to_all x2 -> x4, starting transfers between devices: 17 us -> 27.5 us  [exchange(): lax.all_to_all(operand, ('ctx', 'mp'), split_axis=0, concat_axis=0, tiled...]
    dot_general x1 -> x2, matrix products: 6.92 us -> 12 us  [absorb(): lax.dot_general(picker_low, block_grid, (((0,), (0,)), ((), ())), preferr...]
    all_to_all x0 -> x1, starting transfers between devices: none -> 4.94 us  [on_device(): lax.all_to_all(own_grads, 'mp', split_axis=0, concat_axis=0, tiled=True)]
    select_n x1 -> x2, other arithmetic: 6.78 us -> 9.98 us  [the longest x1 6.45 us: on_device(): mixed = exchange(jnp.where(later, outgoing(chunk_grids[1]), grads_first))]
    pallas_call x1 -> x2, Pallas kernels: 50.5 us -> 53 us  [attend(): pl.pallas_call(kernel, grid=(head_count, layer_count), in_specs=[pl.Block...]
  transfers between devices with their start and end apart: 2 -> 5, of which waited for: 2 -> 4; matrix products, arithmetic and copies ran while one was open for 1% -> 5% of each run, Pallas kernels for 0% -> 9%
where the time goes in v4:
time: 312 us; the launch traced here: 311 us
  waiting for transfers between devices  186 us (60%)
  Pallas kernels  53 us (17%)
  starting transfers between devices  32.4 us (10%)
  other arithmetic  13.3 us (4%)
  local copies, waits for them, and re-layouts  12.9 us (4%)
  matrix products  12 us (4%)
    all_to_all x4, waiting for transfers between devices, exchange(): lax.all_to_all(operand, ('ctx', 'mp'), split_axis=0, concat_axis=0, tiled...  186 us
    pallas_call x2, Pallas kernels, attend(): pl.pallas_call(kernel, grid=(head_count, layer_count), in_specs=[pl.Block...  53 us
    all_to_all x4, starting transfers between devices, exchange(): lax.all_to_all(operand, ('ctx', 'mp'), split_axis=0, concat_axis=0, tiled...  27.5 us
    dot_general x2, matrix products, absorb(): lax.dot_general(picker_low, block_grid, (((0,), (0,)), ((), ())), preferr...  12 us
    select_n x1, other arithmetic, on_device(): mixed = exchange(jnp.where(later, outgoing(chunk_grids[1]), grads_first))  6.45 us
  transfers between devices with their start and end apart: 5, of which 4 were waited for; matrix products, arithmetic and copies ran while one was open for 5% of the time, Pallas kernels for 9%

profile of v4, /device:TPU:1, one launch (start us, length us, event | category | flops | bytes accessed | tf_op | source)
XLA Modules:
  0.0 310.8 jit_solution(9967478063347075306)
XLA Ops:
  0.6 1.3 broadcast_in_dim.138
  1.9 11.5 %all-to-all-start = ((s32[128,1,96]{2,1,0:T(1,128)}), s32[128,1,96]{2,1,0:T(1,128)S(1)}, u32[]{:S(2)}, u32[]{:S(2)}) async-start(s32[128,1,96]{2,1,0:T(1,128)} %broadcast_in_dim.138), calls=%async_computation | async-start | bytes 131072 | tf_op jit(solution)/shard_map/all_to_all | solution.py:19
  13.4 1.4 reshape.176
  14.8 1.4 reshape.177
  16.2 0.6 fusion.15
  16.9 6.1 %all-to-all-done = s32[128,1,96]{2,1,0:T(1,128)S(1)} async-done(((s32[128,1,96]{2,1,0:T(1,128)}), s32[128,1,96]{2,1,0:T(1,128)S(1)}, u32[]{:S(2)}, u32[]{:S(2)}) %all-to-all-start) | async-done | bytes 49184 | tf_op jit(solution)/shard_map/all_to_all | solution.py:19
  23.0 0.1 fusion.29
  23.2 0.1 select_reduce_fusion.1
  23.3 0.1 broadcast_in_dim.140
  23.4 0.1 broadcast_in_dim.141
  23.5 0.1 broadcast_in_dim.154
  23.6 0.1 broadcast_in_dim.155
  23.7 0.1 broadcast_in_dim.147
  23.8 0.1 broadcast_in_dim.148
  23.9 3.5 %fusion.4 = bf16[128,2,16,640]{3,2,1,0:T(8,128)(2,1)} fusion(pred[128]{0:T(512)(128)(4,1)S(1)} %broadcast_in_dim.155, pred[128]{0:T(512)(128)(4,1)S(1)} %broadcast_in_dim.148, pred[128]{0:T(512)(128)(4,1)S(1)} %broadcast_in_dim.141, bf16[4,2,16,640]{3,2,1,0:T(8,128)(2,1)S(1)} %copy.65, bf16[4,2,16,640]{3,2,1,0:T(8,128)(2,1)S(1)} %copy.64, ...), kind=kLoop, calls=%fused_computation.6 | loop fusion | flops 7864320 | bytes 5734784 | tf_op jit(solution)/shard_map/jit(_where)/select_n | solution.py:144
  27.4 0.0 copy-start.4
  27.4 0.0 copy-start
  27.4 0.0 copy-start.1
  27.4 5.4 %all-to-all-start.1 = ((bf16[128,2,16,640]{3,2,1,0:T(8,128)(2,1)}), bf16[128,2,16,640]{3,2,1,0:T(8,128)(2,1)}, u32[]{:S(2)}, u32[]{:S(2)}) async-start(bf16[128,2,16,640]{3,2,1,0:T(8,128)(2,1)} %fusion.4), calls=%async_computation.1 | async-start | bytes 10485760 | tf_op jit(solution)/shard_map/all_to_all | solution.py:19
  32.8 0.0 copy-done.4
  32.9 0.1 fusion.21
  33.0 0.1 select_reduce_fusion
  33.1 0.1 subtract_select_fusion
  33.2 0.1 select_n.82.kpos_ref
  33.4 63.4 %all-to-all-done.1.kv_ref = bf16[128,2,16,640]{3,2,1,0:T(8,128)(2,1)} async-done(((bf16[128,2,16,640]{3,2,1,0:T(8,128)(2,1)}), bf16[128,2,16,640]{3,2,1,0:T(8,128)(2,1)}, u32[]{:S(2)}, u32[]{:S(2)}) %all-to-all-start.1) | async-done | bytes 5242912 | tf_op jit(solution)/shard_map/all_to_all | solution.py:19
  96.8 0.0 copy-done
  96.8 0.0 copy-done.1
  96.8 26.4 %shard_map.84 = (bf16[2,192,640]{2,1,0:T(8,128)(2,1)S(1)}, bf16[2,192,640]{2,1,0:T(8,128)(2,1)S(1)}, bf16[128,2,16,640]{3,2,1,0:T(8,128)(2,1)}) custom-call(s32[1,2048]{1,0:T(1,128)S(1)} %select_n.82.kpos_ref, bf16[2,192,1280]{2,1,0:T(8,128)(2,1)S(1)} %copy-done, bf16[2,192,1280]{2,1,0:T(8,128)(2,1)S(1)} %copy-done.1, ...), custom_call_target="tpu_custom_call" | custom-call | tf_op jit(solution)/shard_map/pallas_call | solution.py:88
  123.2 6.4 %fusion.2 = bf16[128,2,16,640]{3,2,1,0:T(8,128)(2,1)} fusion(bf16[128,2,16,640]{3,2,1,0:T(8,128)(2,1)} %get-tuple-element.11, pred[128]{0:T(512)(128)(4,1)S(1)} %fusion.28, pred[128]{0:T(512)(128)(4,1)S(1)} %broadcast_in_dim.155, pred[128]{0:T(512)(128)(4,1)S(1)} %broadcast_in_dim.148, pred[128]{0:T(512)(128)(4,1)S(1)} %broadcast_in_dim.141, ...), kind=kLoop, calls=%fused_computation.3 | loop fusion | flops 10485760 | bytes 10977792 | tf_op jit(solution)/shard_map/jit(_where)/select_n | solution.py:169
  129.7 5.5 %all-to-all-start.2 = ((bf16[128,2,16,640]{3,2,1,0:T(8,128)(2,1)}), bf16[128,2,16,640]{3,2,1,0:T(8,128)(2,1)}, u32[]{:S(2)}, u32[]{:S(2)}) async-start(bf16[128,2,16,640]{3,2,1,0:T(8,128)(2,1)} %fusion.2), calls=%async_computation.2 | async-start | bytes 10485760 | tf_op jit(solution)/shard_map/all_to_all | solution.py:19
  135.2 1.6 constant_dynamic-slice_fusion
  136.8 62.4 %all-to-all-done.2.kv_ref = bf16[128,2,16,640]{3,2,1,0:T(8,128)(2,1)} async-done(((bf16[128,2,16,640]{3,2,1,0:T(8,128)(2,1)}), bf16[128,2,16,640]{3,2,1,0:T(8,128)(2,1)}, u32[]{:S(2)}, u32[]{:S(2)}) %all-to-all-start.2) | async-done | bytes 5242912 | tf_op jit(solution)/shard_map/all_to_all | solution.py:19
  199.2 4.9 %all-to-all-start.3 = ((bf16[4,2,16,640]{3,2,1,0:T(8,128)(2,1)}), bf16[4,2,16,640]{3,2,1,0:T(8,128)(2,1)}, u32[]{:S(2)}, u32[]{:S(2)}) async-start(bf16[4,2,16,640]{3,2,1,0:T(8,128)(2,1)} %constant_dynamic-slice_fusion), calls=%async_computation.3 | async-start | bytes 327680 | tf_op jit(solution)/shard_map/all_to_all | solution.py:171
  204.1 26.5 %shard_map.85 = (bf16[2,192,640]{2,1,0:T(8,128)(2,1)S(1)}, bf16[2,192,640]{2,1,0:T(8,128)(2,1)S(1)}, bf16[128,2,16,640]{3,2,1,0:T(8,128)(2,1)}) custom-call(s32[1,2048]{1,0:T(1,128)S(1)} %select_n.82.kpos_ref, bf16[2,192,1280]{2,1,0:T(8,128)(2,1)S(1)} %copy-done, bf16[2,192,1280]{2,1,0:T(8,128)(2,1)S(1)} %copy-done.1, ...), custom_call_target="tpu_custom_call" | custom-call | tf_op jit(solution)/shard_map/pallas_call | solution.py:88
  230.7 0.0 copy-start.2
  230.7 0.8 copy-done.2
  231.4 0.0 all-to-all-done.3
  231.4 0.0 copy-start.3
  231.4 5.0 %all-to-all-start.4 = ((bf16[128,2,16,640]{3,2,1,0:T(8,128)(2,1)}), bf16[128,2,16,640]{3,2,1,0:T(8,128)(2,1)}, u32[]{:S(2)}, u32[]{:S(2)}) async-start(bf16[128,2,16,640]{3,2,1,0:T(8,128)(2,1)} %get-tuple-element.15), calls=%async_computation.4 | async-start | bytes 10485760 | tf_op jit(solution)/shard_map/all_to_all | solution.py:19
  236.5 1.6 constant_dynamic-update-slice_fusion
  238.1 0.0 copy-done.3
  238.1 1.4 pad_maximum_fusion
  239.5 6.0 %fusion.7 = f32[3,4,2,16,640]{4,0,3,2,1:T(4,128)S(1)} fusion(bf16[32,4,2,16,640]{4,3,2,1,0:T(8,128)(2,1)} %bitcast.31, pred[32,3]{0,1:T(4,128)(4,1)S(1)} %fusion.25), kind=kOutput, calls=%fused_computation.9 | convolution fusion | flops 15728640 | bytes 6226016 | tf_op jit(solution)/shard_map/dot_general | solution.py:149
  245.5 54.6 %all-to-all-done.4 = bf16[128,2,16,640]{3,2,1,0:T(8,128)(2,1)} async-done(((bf16[128,2,16,640]{3,2,1,0:T(8,128)(2,1)}), bf16[128,2,16,640]{3,2,1,0:T(8,128)(2,1)}, u32[]{:S(2)}, u32[]{:S(2)}) %all-to-all-start.4) | async-done | bytes 5242912 | tf_op jit(solution)/shard_map/all_to_all | solution.py:19
  300.1 6.0 %fusion.5 = f32[3,4,2,16,640]{4,0,3,2,1:T(4,128)S(1)} fusion(bf16[32,4,2,16,640]{4,3,2,1,0:T(8,128)(2,1)} %bitcast.33, pred[32,3]{0,1:T(4,128)(4,1)S(1)} %fusion.25), kind=kOutput, calls=%fused_computation.7 | convolution fusion | flops 15728640 | bytes 6226016 | tf_op jit(solution)/shard_map/dot_general | solution.py:149
  306.1 0.7 maximum_bitcast_fusion
  306.8 0.5 fusion.30
  307.3 0.6 copy.72
  307.9 1.1 copy.75
  309.0 0.6 copy.71
  309.7 1.1 copy.74
  (14 shorter events, 0.2 us)
Async XLA Ops:
  1.9 21.1 %all-to-all-start = ((s32[128,1,96]{2,1,0:T(1,128)}), s32[128,1,96]{2,1,0:T(1,128)S(1)}, u32[]{:S(2)}, u32[]{:S(2)}) async-start(s32[128,1,96]{2,1,0:T(1,128)} %broadcast_in_dim.138), calls=%async_computation | async-start | bytes 131072 | tf_op jit(solution)/shard_map/all_to_all | solution.py:19
  27.4 5.4 %copy-start.4 = (s32[1,96]{1,0:T(1,128)S(1)}, s32[1,96]{1,0:T(1,128)}, u32[]{:S(2)}) copy-start(s32[1,96]{1,0:T(1,128)} %param.9) | copy-start | bytes 1156
  27.4 69.4 %copy-start = (bf16[2,192,1280]{2,1,0:T(8,128)(2,1)S(1)}, bf16[2,192,1280]{2,1,0:T(8,128)(2,1)}, u32[]{:S(2)}) copy-start(bf16[2,192,1280]{2,1,0:T(8,128)(2,1)} %q_ref.3) | copy-start | bytes 2949124
  27.4 69.4 %copy-start.1 = (bf16[2,192,1280]{2,1,0:T(8,128)(2,1)S(1)}, bf16[2,192,1280]{2,1,0:T(8,128)(2,1)}, u32[]{:S(2)}) copy-start(bf16[2,192,1280]{2,1,0:T(8,128)(2,1)} %do_ref.3) | copy-start | bytes 2949124
  27.4 69.4 %all-to-all-start.1 = ((bf16[128,2,16,640]{3,2,1,0:T(8,128)(2,1)}), bf16[128,2,16,640]{3,2,1,0:T(8,128)(2,1)}, u32[]{:S(2)}, u32[]{:S(2)}) async-start(bf16[128,2,16,640]{3,2,1,0:T(8,128)(2,1)} %fusion.4), calls=%async_computation.1 | async-start | bytes 10485760 | tf_op jit(solution)/shard_map/all_to_all | solution.py:19
  129.7 69.5 %all-to-all-start.2 = ((bf16[128,2,16,640]{3,2,1,0:T(8,128)(2,1)}), bf16[128,2,16,640]{3,2,1,0:T(8,128)(2,1)}, u32[]{:S(2)}, u32[]{:S(2)}) async-start(bf16[128,2,16,640]{3,2,1,0:T(8,128)(2,1)} %fusion.2), calls=%async_computation.2 | async-start | bytes 10485760 | tf_op jit(solution)/shard_map/all_to_all | solution.py:19
  199.2 32.3 %all-to-all-start.3 = ((bf16[4,2,16,640]{3,2,1,0:T(8,128)(2,1)}), bf16[4,2,16,640]{3,2,1,0:T(8,128)(2,1)}, u32[]{:S(2)}, u32[]{:S(2)}) async-start(bf16[4,2,16,640]{3,2,1,0:T(8,128)(2,1)} %constant_dynamic-slice_fusion), calls=%async_computation.3 | async-start | bytes 327680 | tf_op jit(solution)/shard_map/all_to_all | solution.py:171
  230.7 0.8 copy-start.2
  231.4 6.7 %copy-start.3 = (bf16[2,192,640]{2,1,0:T(8,128)(2,1)S(1)}, bf16[2,192,640]{2,1,0:T(8,128)(2,1)}, u32[]{:S(2)}) copy-start(bf16[2,192,640]{2,1,0:T(8,128)(2,1)} %copy-done.2) | copy-start | bytes 1474564
  231.4 68.7 %all-to-all-start.4 = ((bf16[128,2,16,640]{3,2,1,0:T(8,128)(2,1)}), bf16[128,2,16,640]{3,2,1,0:T(8,128)(2,1)}, u32[]{:S(2)}, u32[]{:S(2)}) async-start(bf16[128,2,16,640]{3,2,1,0:T(8,128)(2,1)} %get-tuple-element.15), calls=%async_computation.4 | async-start | bytes 10485760 | tf_op jit(solution)/shard_map/all_to_all | solution.py:19

commit v5 on v4

--- a/solution.py
+++ b/solution.py
@@ -13,6 +13,7 @@
 
 neg_big = -1e30
 far_pos = 1 << 30
+chunk_count = 5
 
 
 def exchange(operand):
@@ -134,8 +135,10 @@
         return cache_rows.reshape(per_owner, BLK, mp_count, head_width).transpose(0, 2, 1, 3)
 
     block_grid = jnp.stack([by_block(cache_keys), by_block(cache_values)], axis=2)
-    chunk_width = (head_width // HD // 2) * HD
-    chunk_grids = (block_grid[..., :chunk_width], block_grid[..., chunk_width:])
+    chunk_width = head_width // chunk_count
+    chunk_grids = [
+        block_grid[..., part * chunk_width:(part + 1) * chunk_width] for part in range(chunk_count)
+    ]
 
     def outgoing(chunk_grid):
         picked = jnp.zeros((ctx_count,) + chunk_grid.shape[1:], jnp.bfloat16)
@@ -162,23 +165,29 @@
     key_live = jnp.repeat(slot_live, BLK)
     kpos_rel = jnp.where(key_live, key_pos - my_stretch * tok_rows, far_pos)
     kpos_rel = kpos_rel.reshape(1, -1).astype(jnp.int32)
-    src_ctx = jnp.arange(owner_count, dtype=jnp.int32) // mp_count
-    kv_first = exchange(outgoing(chunk_grids[0]))
-    out_first, dq_first, grads_first = attend(kpos_rel, queries, douts, kv_first, factor, 0)
-    later = (src_ctx >= my_stretch).reshape(owner_count, 1, 1, 1)
-    mixed = exchange(jnp.where(later, outgoing(chunk_grids[1]), grads_first))
-    own_grads = lax.dynamic_slice_in_dim(grads_first, my_stretch * mp_count, mp_count, 0)
-    own_back = lax.all_to_all(own_grads, "mp", split_axis=0, concat_axis=0, tiled=True)
-    back_first = lax.dynamic_update_slice_in_dim(mixed, own_back, my_stretch * mp_count, 0)
-    head_offset = chunk_width // HD
-    out_second, dq_second, grads_second = attend(
-        kpos_rel, queries, douts, mixed, factor, head_offset
-    )
-    back_second = exchange(grads_second)
-    summed = jnp.concatenate([absorb(back_first), absorb(back_second)], axis=-1)
+    dest_ctx = jnp.arange(owner_count, dtype=jnp.int32) // mp_count
+    later = (dest_ctx >= my_stretch).reshape(owner_count, 1, 1, 1)
+    heads_per_chunk = chunk_width // HD
+    received = exchange(outgoing(chunk_grids[0]))
+    outs, dqs, absorbed = [], [], []
+    for part in range(chunk_count):
+        out_part, dq_part, grads_part = attend(
+            kpos_rel, queries, douts, received, factor, part * heads_per_chunk
+        )
+        outs.append(out_part)
+        dqs.append(dq_part)
+        if part + 1 < chunk_count:
+            received = exchange(jnp.where(later, outgoing(chunk_grids[part + 1]), grads_part))
+            own_grads = lax.dynamic_slice_in_dim(grads_part, my_stretch * mp_count, mp_count, 0)
+            own_back = lax.all_to_all(own_grads, "mp", split_axis=0, concat_axis=0, tiled=True)
+            back = lax.dynamic_update_slice_in_dim(received, own_back, my_stretch * mp_count, 0)
+        else:
+            back = exchange(grads_part)
+        absorbed.append(absorb(back))
+    summed = jnp.concatenate(absorbed, axis=-1)
     summed = summed.transpose(2, 0, 3, 1, 4).reshape(2, kv_rows, full_width)
-    attended = jnp.concatenate([out_first, out_second], axis=-1)
-    d_query = jnp.concatenate([dq_first, dq_second], axis=-1)
+    attended = jnp.concatenate(outs, axis=-1)
+    d_query = jnp.concatenate(dqs, axis=-1)
     return (attended, d_query, summed[0], summed[1])
 
 

time: 312 us -> 345 us (1.11)
  starting transfers between devices: 32.4 us -> 59.8 us
  waiting for transfers between devices: 186 us -> 160 us
  local copies, waits for them, and re-layouts: 12.9 us -> 33.2 us
  matrix products: 12 us -> 18.8 us
    all_to_all x4 -> x7, waiting for transfers between devices: 186 us -> 160 us  [exchange(): lax.all_to_all(operand, ('ctx', 'mp'), split_axis=0, concat_axis=0, tiled...]
    all_to_all x4 -> x7, starting transfers between devices: 27.5 us -> 41.7 us  [exchange(): lax.all_to_all(operand, ('ctx', 'mp'), split_axis=0, concat_axis=0, tiled...]
    all_to_all x1 -> x4, starting transfers between devices: 4.94 us -> 18.1 us  [on_device(): lax.all_to_all(own_grads, 'mp', split_axis=0, concat_axis=0, tiled=True)]
    unnamed x12 -> x75, local copies, waits for them, and re-layouts: 3.02 us -> 13.2 us
    dot_general x2 -> x5, matrix products: 12 us -> 18.8 us  [absorb(): lax.dot_general(picker_low, block_grid, (((0,), (0,)), ((), ())), preferr...]
    dynamic_slice x1 -> x4, local copies, waits for them, and re-layouts: 1.6 us -> 5.9 us  [on_device(): lax.dynamic_slice_in_dim(grads_part, my_stretch * mp_count, mp_count, 0)]
    pallas_call x2 -> x5, Pallas kernels: 53 us -> 56.4 us  [attend(): pl.pallas_call(kernel, grid=(head_count, layer_count), in_specs=[pl.Block...]
    select_n x1 -> x4, other arithmetic: 6.45 us -> 9.26 us  [on_device(): jnp.where(later, outgoing(chunk_grids[part + 1]), grads_part)]
  transfers between devices with their start and end apart: 5 -> 11, of which waited for: 4 -> 7; matrix products, arithmetic and copies ran while one was open for 5% -> 12% of each run, Pallas kernels for 9% -> 13%
where the time goes in v5:
time: 345 us; the launch traced here: 343 us
  waiting for transfers between devices  160 us (46%)
  starting transfers between devices  59.8 us (17%)
  Pallas kernels  56.4 us (16%)
  local copies, waits for them, and re-layouts  33.2 us (10%)
  matrix products  18.8 us (5%)
  other arithmetic  14.1 us (4%)
    all_to_all x7, waiting for transfers between devices, exchange(): lax.all_to_all(operand, ('ctx', 'mp'), split_axis=0, concat_axis=0, tiled...  160 us
    pallas_call x5, Pallas kernels, attend(): pl.pallas_call(kernel, grid=(head_count, layer_count), in_specs=[pl.Block...  56.4 us
    all_to_all x7, starting transfers between devices, exchange(): lax.all_to_all(operand, ('ctx', 'mp'), split_axis=0, concat_axis=0, tiled...  41.7 us
    dot_general x5, matrix products, absorb(): lax.dot_general(picker_low, block_grid, (((0,), (0,)), ((), ())), preferr...  18.8 us
    all_to_all x4, starting transfers between devices, on_device(): lax.all_to_all(own_grads, 'mp', split_axis=0, concat_axis=0, tiled=True)  18.1 us
    unnamed x75, local copies, waits for them, and re-layouts  13.2 us
    select_n x4, other arithmetic, on_device(): jnp.where(later, outgoing(chunk_grids[part + 1]), grads_part)  9.26 us
  transfers between devices with their start and end apart: 11, of which 7 were waited for; matrix products, arithmetic and copies ran while one was open for 12% of the time, Pallas kernels for 13%

profile of v5, /device:TPU:1, one launch (start us, length us, event | category | flops | bytes accessed | tf_op | source)
XLA Modules:
  0.0 343.0 jit_solution(1445972129595226526)
XLA Ops:
  0.6 1.3 broadcast_in_dim.255
  1.9 11.5 %all-to-all-start = ((s32[128,1,96]{2,1,0:T(1,128)}), s32[128,1,96]{2,1,0:T(1,128)S(1)}, u32[]{:S(2)}, u32[]{:S(2)}) async-start(s32[128,1,96]{2,1,0:T(1,128)} %broadcast_in_dim.255), calls=%async_computation | async-start | bytes 131072 | tf_op jit(solution)/shard_map/all_to_all | solution.py:20
  13.4 1.4 reshape.206
  14.8 1.4 reshape.207
  16.2 1.1 fusion.54
  17.4 5.6 %all-to-all-done = s32[128,1,96]{2,1,0:T(1,128)S(1)} async-done(((s32[128,1,96]{2,1,0:T(1,128)}), s32[128,1,96]{2,1,0:T(1,128)S(1)}, u32[]{:S(2)}, u32[]{:S(2)}) %all-to-all-start) | async-done | bytes 49184 | tf_op jit(solution)/shard_map/all_to_all | solution.py:20
  23.9 1.8 fusion.13
  25.7 5.4 %all-to-all-start.1 = ((bf16[128,2,16,256]{3,2,1,0:T(8,128)(2,1)}), bf16[128,2,16,256]{3,2,1,0:T(8,128)(2,1)}, u32[]{:S(2)}, u32[]{:S(2)}) async-start(bf16[128,2,16,256]{3,2,1,0:T(8,128)(2,1)} %fusion.13), calls=%async_computation.1 | async-start | bytes 4194304 | tf_op jit(solution)/shard_map/all_to_all | solution.py:20
  31.7 0.5 fusion.79
  32.2 29.1 %all-to-all-done.1.kv_ref = bf16[128,2,16,256]{3,2,1,0:T(8,128)(2,1)} async-done(((bf16[128,2,16,256]{3,2,1,0:T(8,128)(2,1)}), bf16[128,2,16,256]{3,2,1,0:T(8,128)(2,1)}, u32[]{:S(2)}, u32[]{:S(2)}) %all-to-all-start.1) | async-done | bytes 2097184 | tf_op jit(solution)/shard_map/all_to_all | solution.py:20
  61.4 11.2 %shard_map.84 = (bf16[2,192,256]{2,1,0:T(8,128)(2,1)S(1)}, bf16[2,192,256]{2,1,0:T(8,128)(2,1)S(1)}, bf16[128,2,16,256]{3,2,1,0:T(8,128)(2,1)S(1)}) custom-call(s32[1,2048]{1,0:T(1,128)S(1)} %select_n.133.kpos_ref, bf16[2,192,1280]{2,1,0:T(8,128)(2,1)S(1)} %copy-done, bf16[2,192,1280]{2,1,0:T(8,128)(2,1)S(1)} %copy-done.1, ...), custom_call_target="tpu_custom_call" | custom-call | tf_op jit(solution)/shard_map/pallas_call | solution.py:89
  72.6 1.3 copy-done.3
  74.0 3.1 fusion.11
  77.1 5.6 %all-to-all-start.2 = ((bf16[128,2,16,256]{3,2,1,0:T(8,128)(2,1)}), bf16[128,2,16,256]{3,2,1,0:T(8,128)(2,1)}, u32[]{:S(2)}, u32[]{:S(2)}) async-start(bf16[128,2,16,256]{3,2,1,0:T(8,128)(2,1)} %fusion.11), calls=%async_computation.2 | async-start | bytes 4194304 | tf_op jit(solution)/shard_map/all_to_all | solution.py:20
  82.7 1.5 constant_dynamic-slice_fusion.2
  84.1 28.8 %all-to-all-done.2.kv_ref = bf16[128,2,16,256]{3,2,1,0:T(8,128)(2,1)} async-done(((bf16[128,2,16,256]{3,2,1,0:T(8,128)(2,1)}), bf16[128,2,16,256]{3,2,1,0:T(8,128)(2,1)}, u32[]{:S(2)}, u32[]{:S(2)}) %all-to-all-start.2) | async-done | bytes 2097184 | tf_op jit(solution)/shard_map/all_to_all | solution.py:20
  112.9 4.2 %all-to-all-start.6 = ((bf16[4,2,16,256]{3,2,1,0:T(8,128)(2,1)}), bf16[4,2,16,256]{3,2,1,0:T(8,128)(2,1)S(1)}, u32[]{:S(2)}, u32[]{:S(2)}) async-start(bf16[4,2,16,256]{3,2,1,0:T(8,128)(2,1)} %constant_dynamic-slice_fusion.2), calls=%async_computation.6 | async-start | bytes 131072 | tf_op jit(solution)/shard_map/all_to_all | solution.py:182
  117.1 0.8 fusion.67
  118.1 11.3 %shard_map.85 = (bf16[2,192,256]{2,1,0:T(8,128)(2,1)S(1)}, bf16[2,192,256]{2,1,0:T(8,128)(2,1)S(1)}, bf16[128,2,16,256]{3,2,1,0:T(8,128)(2,1)S(1)}) custom-call(s32[1,2048]{1,0:T(1,128)S(1)} %select_n.133.kpos_ref, bf16[2,192,1280]{2,1,0:T(8,128)(2,1)S(1)} %copy-done, bf16[2,192,1280]{2,1,0:T(8,128)(2,1)S(1)} %copy-done.1, ...), custom_call_target="tpu_custom_call" | custom-call | tf_op jit(solution)/shard_map/pallas_call | solution.py:89
  129.4 1.4 copy-done.4
  130.8 2.0 fusion.8
  132.8 0.6 copy-done.10
  133.5 4.9 %all-to-all-start.3 = ((bf16[128,2,16,256]{3,2,1,0:T(8,128)(2,1)}), bf16[128,2,16,256]{3,2,1,0:T(8,128)(2,1)}, u32[]{:S(2)}, u32[]{:S(2)}) async-start(bf16[128,2,16,256]{3,2,1,0:T(8,128)(2,1)} %fusion.8), calls=%async_computation.3 | async-start | bytes 4194304 | tf_op jit(solution)/shard_map/all_to_all | solution.py:20
  138.3 1.5 constant_dynamic-slice_fusion.1
  139.8 28.6 %all-to-all-done.3.kv_ref = bf16[128,2,16,256]{3,2,1,0:T(8,128)(2,1)} async-done(((bf16[128,2,16,256]{3,2,1,0:T(8,128)(2,1)}), bf16[128,2,16,256]{3,2,1,0:T(8,128)(2,1)}, u32[]{:S(2)}, u32[]{:S(2)}) %all-to-all-start.3) | async-done | bytes 2097184 | tf_op jit(solution)/shard_map/all_to_all | solution.py:20
  168.4 4.2 %all-to-all-start.7 = ((bf16[4,2,16,256]{3,2,1,0:T(8,128)(2,1)}), bf16[4,2,16,256]{3,2,1,0:T(8,128)(2,1)S(1)}, u32[]{:S(2)}, u32[]{:S(2)}) async-start(bf16[4,2,16,256]{3,2,1,0:T(8,128)(2,1)} %constant_dynamic-slice_fusion.1), calls=%async_computation.7 | async-start | bytes 131072 | tf_op jit(solution)/shard_map/all_to_all | solution.py:182
  172.8 11.3 %shard_map.86 = (bf16[2,192,256]{2,1,0:T(8,128)(2,1)S(1)}, bf16[2,192,256]{2,1,0:T(8,128)(2,1)S(1)}, bf16[128,2,16,256]{3,2,1,0:T(8,128)(2,1)S(1)}) custom-call(s32[1,2048]{1,0:T(1,128)S(1)} %select_n.133.kpos_ref, bf16[2,192,1280]{2,1,0:T(8,128)(2,1)S(1)} %copy-done, bf16[2,192,1280]{2,1,0:T(8,128)(2,1)S(1)} %copy-done.1, ...), custom_call_target="tpu_custom_call" | custom-call | tf_op jit(solution)/shard_map/pallas_call | solution.py:89
  184.1 1.3 copy-done.5
  185.4 2.0 fusion.5
  187.4 0.6 copy-done.11
  188.0 4.7 %all-to-all-start.4 = ((bf16[128,2,16,256]{3,2,1,0:T(8,128)(2,1)}), bf16[128,2,16,256]{3,2,1,0:T(8,128)(2,1)}, u32[]{:S(2)}, u32[]{:S(2)}) async-start(bf16[128,2,16,256]{3,2,1,0:T(8,128)(2,1)} %fusion.5), calls=%async_computation.4 | async-start | bytes 4194304 | tf_op jit(solution)/shard_map/all_to_all | solution.py:20
  192.8 1.5 constant_dynamic-slice_fusion
  194.2 28.6 %all-to-all-done.4.kv_ref = bf16[128,2,16,256]{3,2,1,0:T(8,128)(2,1)} async-done(((bf16[128,2,16,256]{3,2,1,0:T(8,128)(2,1)}), bf16[128,2,16,256]{3,2,1,0:T(8,128)(2,1)}, u32[]{:S(2)}, u32[]{:S(2)}) %all-to-all-start.4) | async-done | bytes 2097184 | tf_op jit(solution)/shard_map/all_to_all | solution.py:20
  222.8 4.8 %all-to-all-start.8 = ((bf16[4,2,16,256]{3,2,1,0:T(8,128)(2,1)}), bf16[4,2,16,256]{3,2,1,0:T(8,128)(2,1)}, u32[]{:S(2)}, u32[]{:S(2)}) async-start(bf16[4,2,16,256]{3,2,1,0:T(8,128)(2,1)} %constant_dynamic-slice_fusion), calls=%async_computation.8 | async-start | bytes 131072 | tf_op jit(solution)/shard_map/all_to_all | solution.py:182
  227.8 11.3 %shard_map.87 = (bf16[2,192,256]{2,1,0:T(8,128)(2,1)S(1)}, bf16[2,192,256]{2,1,0:T(8,128)(2,1)S(1)}, bf16[128,2,16,256]{3,2,1,0:T(8,128)(2,1)S(1)}) custom-call(s32[1,2048]{1,0:T(1,128)S(1)} %select_n.133.kpos_ref, bf16[2,192,1280]{2,1,0:T(8,128)(2,1)S(1)} %copy-done, bf16[2,192,1280]{2,1,0:T(8,128)(2,1)S(1)} %copy-done.1, ...), custom_call_target="tpu_custom_call" | custom-call | tf_op jit(solution)/shard_map/pallas_call | solution.py:89
  239.1 1.3 copy-done.2
  240.4 2.1 fusion.2
  242.5 4.7 %all-to-all-start.5 = ((bf16[128,2,16,256]{3,2,1,0:T(8,128)(2,1)}), bf16[128,2,16,256]{3,2,1,0:T(8,128)(2,1)}, u32[]{:S(2)}, u32[]{:S(2)}) async-start(bf16[128,2,16,256]{3,2,1,0:T(8,128)(2,1)} %fusion.2), calls=%async_computation.5 | async-start | bytes 4194304 | tf_op jit(solution)/shard_map/all_to_all | solution.py:20
  247.2 0.8 constant_dynamic-update-slice_fusion.4
  248.0 1.5 constant_dynamic-update-slice_fusion.12
  249.4 1.5 constant_dynamic-slice_fusion.3
  250.9 26.4 %all-to-all-done.5.kv_ref = bf16[128,2,16,256]{3,2,1,0:T(8,128)(2,1)} async-done(((bf16[128,2,16,256]{3,2,1,0:T(8,128)(2,1)}), bf16[128,2,16,256]{3,2,1,0:T(8,128)(2,1)}, u32[]{:S(2)}, u32[]{:S(2)}) %all-to-all-start.5) | async-done | bytes 2097184 | tf_op jit(solution)/shard_map/all_to_all | solution.py:20
  277.3 4.8 %all-to-all-start.9 = ((bf16[4,2,16,256]{3,2,1,0:T(8,128)(2,1)}), bf16[4,2,16,256]{3,2,1,0:T(8,128)(2,1)}, u32[]{:S(2)}, u32[]{:S(2)}) async-start(bf16[4,2,16,256]{3,2,1,0:T(8,128)(2,1)} %constant_dynamic-slice_fusion.3), calls=%async_computation.9 | async-start | bytes 131072 | tf_op jit(solution)/shard_map/all_to_all | solution.py:182
  282.1 3.7 %fusion.24 = f32[3,4,2,16,1280]{4,0,3,2,1:T(4,128)} fusion(bf16[32,4,2,16,256]{4,3,2,1,0:T(8,128)(2,1)} %bitcast.49, pred[32,3]{0,1:T(4,128)(4,1)S(1)} %fusion.73), kind=kOutput, calls=%fused_computation.29 | convolution fusion | flops 6291455 | bytes 2621536 | tf_op jit(solution)/shard_map/dot_general | solution.py:152
  285.8 11.3 %shard_map.88 = (bf16[2,192,256]{2,1,0:T(8,128)(2,1)S(1)}, bf16[2,192,256]{2,1,0:T(8,128)(2,1)S(1)}, bf16[128,2,16,256]{3,2,1,0:T(8,128)(2,1)S(1)}) custom-call(s32[1,2048]{1,0:T(1,128)S(1)} %select_n.133.kpos_ref, bf16[2,192,1280]{2,1,0:T(8,128)(2,1)S(1)} %copy-done, bf16[2,192,1280]{2,1,0:T(8,128)(2,1)S(1)} %copy-done.1, ...), custom_call_target="tpu_custom_call" | custom-call | tf_op jit(solution)/shard_map/pallas_call | solution.py:89
  297.1 1.4 copy-done.6
  298.5 4.9 %all-to-all-start.10 = ((bf16[128,2,16,256]{3,2,1,0:T(8,128)(2,1)}), bf16[128,2,16,256]{3,2,1,0:T(8,128)(2,1)}, u32[]{:S(2)}, u32[]{:S(2)}) async-start(bf16[128,2,16,256]{3,2,1,0:T(8,128)(2,1)} %copy-done.6), calls=%async_computation.10 | async-start | bytes 4194304 | tf_op jit(solution)/shard_map/all_to_all | solution.py:20
  303.4 0.7 constant_dynamic-update-slice_fusion.3
  304.1 0.6 constant_dynamic-update-slice_fusion.11
  304.8 0.7 constant_dynamic-update-slice_fusion.2
  305.5 3.7 %fusion.27 = f32[3,4,2,16,1280]{4,0,3,2,1:T(4,128)} fusion(f32[3,4,2,16,1280]{4,0,3,2,1:T(4,128)} %fusion.24, bf16[32,4,2,16,256]{4,3,2,1,0:T(8,128)(2,1)} %bitcast.51, pred[32,3]{0,1:T(4,128)(4,1)S(1)} %fusion.73), kind=kOutput, calls=%fused_computation.30 | convolution fusion | flops 6291456 | bytes 2621536 | tf_op jit(solution)/shard_map/dot_general | solution.py:152
  309.2 1.5 constant_dynamic-update-slice_fusion.10
  310.6 0.7 constant_dynamic-update-slice_fusion.1
  311.3 3.7 %fusion.30 = f32[3,4,2,16,1280]{4,0,3,2,1:T(4,128)} fusion(f32[3,4,2,16,1280]{4,0,3,2,1:T(4,128)} %fusion.27, bf16[32,4,2,16,256]{4,3,2,1,0:T(8,128)(2,1)} %bitcast.52, pred[32,3]{0,1:T(4,128)(4,1)S(1)} %fusion.73), kind=kOutput, calls=%fused_computation.31 | convolution fusion | flops 6291456 | bytes 2621536 | tf_op jit(solution)/shard_map/dot_general | solution.py:152
  315.0 1.5 constant_dynamic-update-slice_fusion.13
  316.5 0.7 constant_dynamic-update-slice_fusion
  317.2 4.0 %fusion.33 = f32[3,4,2,16,1280]{4,0,3,2,1:T(4,128)} fusion(f32[3,4,2,16,1280]{4,0,3,2,1:T(4,128)} %fusion.30, bf16[32,4,2,16,256]{4,3,2,1,0:T(8,128)(2,1)} %bitcast.53, pred[32,3]{0,1:T(4,128)(4,1)S(1)} %fusion.73), kind=kOutput, calls=%fused_computation.32 | convolution fusion | flops 6291456 | bytes 2621536 | tf_op jit(solution)/shard_map/dot_general | solution.py:152
  321.3 12.4 %all-to-all-done.10 = bf16[128,2,16,256]{3,2,1,0:T(8,128)(2,1)} async-done(((bf16[128,2,16,256]{3,2,1,0:T(8,128)(2,1)}), bf16[128,2,16,256]{3,2,1,0:T(8,128)(2,1)}, u32[]{:S(2)}, u32[]{:S(2)}) %all-to-all-start.10) | async-done | bytes 2097184 | tf_op jit(solution)/shard_map/all_to_all | solution.py:20
  333.7 3.7 %fusion.36 = f32[3,4,2,16,1280]{4,0,3,2,1:T(4,128)} fusion(f32[3,4,2,16,1280]{4,0,3,2,1:T(4,128)} %fusion.33, bf16[32,4,2,16,256]{4,3,2,1,0:T(8,128)(2,1)} %bitcast.54, pred[32,3]{0,1:T(4,128)(4,1)S(1)} %fusion.73), kind=kOutput, calls=%fused_computation.33 | convolution fusion | flops 6291456 | bytes 2621536 | tf_op jit(solution)/shard_map/dot_general | solution.py:152
  337.3 2.2 fusion.81
  339.5 0.6 copy.132
  340.1 1.1 copy.135
  341.2 0.6 copy.131
  341.9 1.1 copy.134
  (101 shorter events, 1.6 us)
Async XLA Ops:
  1.9 21.1 %all-to-all-start = ((s32[128,1,96]{2,1,0:T(1,128)}), s32[128,1,96]{2,1,0:T(1,128)S(1)}, u32[]{:S(2)}, u32[]{:S(2)}) async-start(s32[128,1,96]{2,1,0:T(1,128)} %broadcast_in_dim.255), calls=%async_computation | async-start | bytes 131072 | tf_op jit(solution)/shard_map/all_to_all | solution.py:20
  23.7 2.0 copy-start.20
  23.9 1.8 copy-start.24
  25.7 5.4 %copy-start.32 = (s32[1,96]{1,0:T(1,128)S(1)}, s32[1,96]{1,0:T(1,128)}, u32[]{:S(2)}) copy-start(s32[1,96]{1,0:T(1,128)} %param.9) | copy-start | bytes 1156
  25.7 35.7 %copy-start = (bf16[2,192,1280]{2,1,0:T(8,128)(2,1)S(1)}, bf16[2,192,1280]{2,1,0:T(8,128)(2,1)}, u32[]{:S(2)}) copy-start(bf16[2,192,1280]{2,1,0:T(8,128)(2,1)} %q_ref.9) | copy-start | bytes 2949124
  25.7 35.7 %copy-start.1 = (bf16[2,192,1280]{2,1,0:T(8,128)(2,1)S(1)}, bf16[2,192,1280]{2,1,0:T(8,128)(2,1)}, u32[]{:S(2)}) copy-start(bf16[2,192,1280]{2,1,0:T(8,128)(2,1)} %do_ref.9) | copy-start | bytes 2949124
  25.7 35.7 %all-to-all-start.1 = ((bf16[128,2,16,256]{3,2,1,0:T(8,128)(2,1)}), bf16[128,2,16,256]{3,2,1,0:T(8,128)(2,1)}, u32[]{:S(2)}, u32[]{:S(2)}) async-start(bf16[128,2,16,256]{3,2,1,0:T(8,128)(2,1)} %fusion.13), calls=%async_computation.1 | async-start | bytes 4194304 | tf_op jit(solution)/shard_map/all_to_all | solution.py:20
  61.4 12.6 %copy-start.28 = (pred[128]{0:T(512)(128)(4,1)S(1)}, pred[128]{0:T(512)(128)(4,1)}, u32[]{:S(2)}) copy-start(pred[128]{0:T(512)(128)(4,1)} %fusion.79) | copy-start | bytes 388
  72.6 1.3 copy-start.3
  77.1 40.9 %copy-start.9 = (bf16[4,2,16,256]{3,0,2,1:T(4,128)(2,1)S(1)}, bf16[4,2,16,256]{3,0,2,1:T(4,128)(2,1)}, u32[]{:S(2)}) copy-start(bf16[4,2,16,256]{3,0,2,1:T(4,128)(2,1)} %get-tuple-element.45) | copy-start | bytes 196612
  77.1 40.9 %copy-start.8 = (bf16[4,2,16,256]{3,0,2,1:T(4,128)(2,1)S(1)}, bf16[4,2,16,256]{3,0,2,1:T(4,128)(2,1)}, u32[]{:S(2)}) copy-start(bf16[4,2,16,256]{3,0,2,1:T(4,128)(2,1)} %get-tuple-element.46) | copy-start | bytes 196612
  77.1 35.8 %all-to-all-start.2 = ((bf16[128,2,16,256]{3,2,1,0:T(8,128)(2,1)}), bf16[128,2,16,256]{3,2,1,0:T(8,128)(2,1)}, u32[]{:S(2)}, u32[]{:S(2)}) async-start(bf16[128,2,16,256]{3,2,1,0:T(8,128)(2,1)} %fusion.11), calls=%async_computation.2 | async-start | bytes 4194304 | tf_op jit(solution)/shard_map/all_to_all | solution.py:20
  112.9 19.9 %all-to-all-start.6 = ((bf16[4,2,16,256]{3,2,1,0:T(8,128)(2,1)}), bf16[4,2,16,256]{3,2,1,0:T(8,128)(2,1)S(1)}, u32[]{:S(2)}, u32[]{:S(2)}) async-start(bf16[4,2,16,256]{3,2,1,0:T(8,128)(2,1)} %constant_dynamic-slice_fusion.2), calls=%async_computation.6 | async-start | bytes 131072 | tf_op jit(solution)/shard_map/all_to_all | solution.py:182
  118.0 12.7 %copy-start.21 = (pred[128]{0:T(512)(128)(4,1)S(1)}, pred[128]{0:T(512)(128)(4,1)}, u32[]{:S(2)}) copy-start(pred[128]{0:T(512)(128)(4,1)} %copy-done.20) | copy-start | bytes 388
  118.0 12.7 %copy-start.25 = (pred[128]{0:T(512)(128)(4,1)S(1)}, pred[128]{0:T(512)(128)(4,1)}, u32[]{:S(2)}) copy-start(pred[128]{0:T(512)(128)(4,1)} %copy-done.24) | copy-start | bytes 388
  118.0 12.7 %copy-start.29 = (pred[128]{0:T(512)(128)(4,1)S(1)}, pred[128]{0:T(512)(128)(4,1)}, u32[]{:S(2)}) copy-start(pred[128]{0:T(512)(128)(4,1)} %fusion.79) | copy-start | bytes 388
  129.4 1.4 copy-start.4
  132.8 39.8 %copy-start.17 = (bf16[4,2,16,256]{3,0,2,1:T(4,128)(2,1)S(1)}, bf16[4,2,16,256]{3,0,2,1:T(4,128)(2,1)}, u32[]{:S(2)}) copy-start(bf16[4,2,16,256]{3,0,2,1:T(4,128)(2,1)} %get-tuple-element.49) | copy-start | bytes 196612
  132.8 39.9 %copy-start.16 = (bf16[4,2,16,256]{3,0,2,1:T(4,128)(2,1)S(1)}, bf16[4,2,16,256]{3,0,2,1:T(4,128)(2,1)}, u32[]{:S(2)}) copy-start(bf16[4,2,16,256]{3,0,2,1:T(4,128)(2,1)} %get-tuple-element.50) | copy-start | bytes 196612
  132.8 39.9 %copy-start.15 = (bf16[4,2,16,256]{3,0,2,1:T(4,128)(2,1)S(1)}, bf16[4,2,16,256]{3,0,2,1:T(4,128)(2,1)}, u32[]{:S(2)}) copy-start(bf16[4,2,16,256]{3,0,2,1:T(4,128)(2,1)} %get-tuple-element.51) | copy-start | bytes 196612
  132.8 0.6 copy-start.10
  133.5 35.0 %all-to-all-start.3 = ((bf16[128,2,16,256]{3,2,1,0:T(8,128)(2,1)}), bf16[128,2,16,256]{3,2,1,0:T(8,128)(2,1)}, u32[]{:S(2)}, u32[]{:S(2)}) async-start(bf16[128,2,16,256]{3,2,1,0:T(8,128)(2,1)} %fusion.8), calls=%async_computation.3 | async-start | bytes 4194304 | tf_op jit(solution)/shard_map/all_to_all | solution.py:20
  168.4 19.0 %all-to-all-start.7 = ((bf16[4,2,16,256]{3,2,1,0:T(8,128)(2,1)}), bf16[4,2,16,256]{3,2,1,0:T(8,128)(2,1)S(1)}, u32[]{:S(2)}, u32[]{:S(2)}) async-start(bf16[4,2,16,256]{3,2,1,0:T(8,128)(2,1)} %constant_dynamic-slice_fusion.1), calls=%async_computation.7 | async-start | bytes 131072 | tf_op jit(solution)/shard_map/all_to_all | solution.py:182
  172.7 12.7 %copy-start.22 = (pred[128]{0:T(512)(128)(4,1)S(1)}, pred[128]{0:T(512)(128)(4,1)}, u32[]{:S(2)}) copy-start(pred[128]{0:T(512)(128)(4,1)} %copy-done.20) | copy-start | bytes 388
  172.7 12.6 %copy-start.26 = (pred[128]{0:T(512)(128)(4,1)S(1)}, pred[128]{0:T(512)(128)(4,1)}, u32[]{:S(2)}) copy-start(pred[128]{0:T(512)(128)(4,1)} %copy-done.24) | copy-start | bytes 388
  172.7 12.6 %copy-start.30 = (pred[128]{0:T(512)(128)(4,1)S(1)}, pred[128]{0:T(512)(128)(4,1)}, u32[]{:S(2)}) copy-start(pred[128]{0:T(512)(128)(4,1)} %fusion.79) | copy-start | bytes 388
  184.1 1.3 copy-start.5
  187.4 40.2 %copy-start.7 = (bf16[4,2,16,256]{3,0,2,1:T(4,128)(2,1)S(1)}, bf16[4,2,16,256]{3,0,2,1:T(4,128)(2,1)}, u32[]{:S(2)}) copy-start(bf16[4,2,16,256]{3,0,2,1:T(4,128)(2,1)} %get-tuple-element.38) | copy-start | bytes 196612
  187.4 40.3 %copy-start.14 = (bf16[4,2,16,256]{3,0,2,1:T(4,128)(2,1)S(1)}, bf16[4,2,16,256]{3,0,2,1:T(4,128)(2,1)}, u32[]{:S(2)}) copy-start(bf16[4,2,16,256]{3,0,2,1:T(4,128)(2,1)} %get-tuple-element.47) | copy-start | bytes 196612
  187.4 40.3 %copy-start.13 = (bf16[4,2,16,256]{3,0,2,1:T(4,128)(2,1)S(1)}, bf16[4,2,16,256]{3,0,2,1:T(4,128)(2,1)}, u32[]{:S(2)}) copy-start(bf16[4,2,16,256]{3,0,2,1:T(4,128)(2,1)} %get-tuple-element.52) | copy-start | bytes 196612
  187.4 0.6 copy-start.11
  188.0 34.8 %all-to-all-start.4 = ((bf16[128,2,16,256]{3,2,1,0:T(8,128)(2,1)}), bf16[128,2,16,256]{3,2,1,0:T(8,128)(2,1)}, u32[]{:S(2)}, u32[]{:S(2)}) async-start(bf16[128,2,16,256]{3,2,1,0:T(8,128)(2,1)} %fusion.5), calls=%async_computation.4 | async-start | bytes 4194304 | tf_op jit(solution)/shard_map/all_to_all | solution.py:20
  222.8 19.6 %all-to-all-start.8 = ((bf16[4,2,16,256]{3,2,1,0:T(8,128)(2,1)}), bf16[4,2,16,256]{3,2,1,0:T(8,128)(2,1)}, u32[]{:S(2)}, u32[]{:S(2)}) async-start(bf16[4,2,16,256]{3,2,1,0:T(8,128)(2,1)} %constant_dynamic-slice_fusion), calls=%async_computation.8 | async-start | bytes 131072 | tf_op jit(solution)/shard_map/all_to_all | solution.py:182
  227.7 12.7 %copy-start.23 = (pred[128]{0:T(512)(128)(4,1)S(1)}, pred[128]{0:T(512)(128)(4,1)}, u32[]{:S(2)}) copy-start(pred[128]{0:T(512)(128)(4,1)} %copy-done.20) | copy-start | bytes 388
  227.7 12.7 %copy-start.27 = (pred[128]{0:T(512)(128)(4,1)S(1)}, pred[128]{0:T(512)(128)(4,1)}, u32[]{:S(2)}) copy-start(pred[128]{0:T(512)(128)(4,1)} %copy-done.24) | copy-start | bytes 388
  227.7 12.7 %copy-start.31 = (pred[128]{0:T(512)(128)(4,1)S(1)}, pred[128]{0:T(512)(128)(4,1)}, u32[]{:S(2)}) copy-start(pred[128]{0:T(512)(128)(4,1)} %fusion.79) | copy-start | bytes 388
  239.0 1.3 copy-start.2
  242.5 34.8 %all-to-all-start.5 = ((bf16[128,2,16,256]{3,2,1,0:T(8,128)(2,1)}), bf16[128,2,16,256]{3,2,1,0:T(8,128)(2,1)}, u32[]{:S(2)}, u32[]{:S(2)}) async-start(bf16[128,2,16,256]{3,2,1,0:T(8,128)(2,1)} %fusion.2), calls=%async_computation.5 | async-start | bytes 4194304 | tf_op jit(solution)/shard_map/all_to_all | solution.py:20
  277.3 21.2 %all-to-all-start.9 = ((bf16[4,2,16,256]{3,2,1,0:T(8,128)(2,1)}), bf16[4,2,16,256]{3,2,1,0:T(8,128)(2,1)}, u32[]{:S(2)}, u32[]{:S(2)}) async-start(bf16[4,2,16,256]{3,2,1,0:T(8,128)(2,1)} %constant_dynamic-slice_fusion.3), calls=%async_computation.9 | async-start | bytes 131072 | tf_op jit(solution)/shard_map/all_to_all | solution.py:182
  297.1 1.4 copy-start.6
  298.5 5.6 %copy-start.18 = (bf16[2,192,1280]{2,1,0:T(8,128)(2,1)S(1)}, bf16[2,192,1280]{2,1,0:T(8,128)(2,1)}, u32[]{:S(2)}) copy-start(bf16[2,192,1280]{2,1,0:T(8,128)(2,1)} %get-tuple-element.59) | copy-start | bytes 2949124
  298.5 5.6 %copy-start.12 = (bf16[4,2,16,256]{3,2,1,0:T(8,128)(2,1)S(1)}, bf16[4,2,16,256]{3,2,1,0:T(8,128)(2,1)}, u32[]{:S(2)}) copy-start(bf16[4,2,16,256]{3,2,1,0:T(8,128)(2,1)} %copy-done.11) | copy-start | bytes 196612
  298.5 35.1 %all-to-all-start.10 = ((bf16[128,2,16,256]{3,2,1,0:T(8,128)(2,1)}), bf16[128,2,16,256]{3,2,1,0:T(8,128)(2,1)}, u32[]{:S(2)}, u32[]{:S(2)}) async-start(bf16[128,2,16,256]{3,2,1,0:T(8,128)(2,1)} %copy-done.6), calls=%async_computation.10 | async-start | bytes 4194304 | tf_op jit(solution)/shard_map/all_to_all | solution.py:20
  317.2 20.1 %copy-start.19 = (bf16[2,192,1280]{2,1,0:T(8,128)(2,1)}, bf16[2,192,1280]{2,1,0:T(8,128)(2,1)S(1)}, u32[]{:S(2)}) copy-start(bf16[2,192,1280]{2,1,0:T(8,128)(2,1)S(1)} %constant_dynamic-update-slice_fusion.5) | copy-start | bytes 2949124

commit v6 on v4

--- a/solution.py
+++ b/solution.py
@@ -19,10 +19,13 @@
     return lax.all_to_all(operand, ("ctx", "mp"), split_axis=0, concat_axis=0, tiled=True)
 
 
-def attend_kernel(
-    kpos_ref, q_ref, do_ref, kv_ref, o_ref, dq_ref, dkv_ref, dk_acc, dv_acc,
-    *, factor, layer_count
-):
+def attend_kernel(*refs, factor, layer_count, mixed):
+    if mixed:
+        split_ref, kpos_ref, q_ref, do_ref, kv_ref, next_ref = refs[:6]
+        o_ref, dq_ref, dkv_ref, own_ref, dk_acc, dv_acc = refs[6:]
+    else:
+        kpos_ref, q_ref, do_ref, kv_ref = refs[:4]
+        o_ref, dq_ref, dkv_ref, dk_acc, dv_acc = refs[4:]
     layer_id = pl.program_id(1)
     q = q_ref[0]
     do = do_ref[0]
@@ -71,35 +74,60 @@
 
     @pl.when(layer_id == layer_count - 1)
     def _():
-        dkv_ref[:, 0] = dk_acc[...].astype(jnp.bfloat16).reshape(dkv_ref.shape[0], BLK, HD)
-        dkv_ref[:, 1] = dv_acc[...].astype(jnp.bfloat16).reshape(dkv_ref.shape[0], BLK, HD)
-
-
-def attend(kpos_rel, queries, douts, kv_rows, factor, head_offset):
+        slot_count = dkv_ref.shape[0]
+        dk_low = dk_acc[...].astype(jnp.bfloat16).reshape(slot_count, BLK, HD)
+        dv_low = dv_acc[...].astype(jnp.bfloat16).reshape(slot_count, BLK, HD)
+        if mixed:
+            own_count = own_ref.shape[0]
+            start_row = pl.multiple_of(split_ref[0] * BLK, own_count * BLK)
+            own_k = dk_acc[pl.ds(start_row, own_count * BLK), :].astype(jnp.bfloat16)
+            own_v = dv_acc[pl.ds(start_row, own_count * BLK), :].astype(jnp.bfloat16)
+            own_ref[:, 0] = own_k.reshape(own_count, BLK, HD)
+            own_ref[:, 1] = own_v.reshape(own_count, BLK, HD)
+            slot_ids = lax.broadcasted_iota(jnp.int32, (slot_count, BLK, HD), 0)
+            later = slot_ids >= split_ref[0]
+            dk_low = jnp.where(later, next_ref[:, 0], dk_low)
+            dv_low = jnp.where(later, next_ref[:, 1], dv_low)
+        dkv_ref[:, 0] = dk_low
+        dkv_ref[:, 1] = dv_low
+
+
+def attend(
+    kpos_rel, queries, douts, kv_rows, factor, head_offset, split=None, next_rows=None,
+    own_slots=None,
+):
     layer_count, tok_rows, _ = queries.shape
     slot_count, _, _, chunk_width = kv_rows.shape
     key_total = slot_count * BLK
     head_count = chunk_width // HD
-    kernel = functools.partial(attend_kernel, factor=factor, layer_count=layer_count)
+    mixed = next_rows is not None
+    kernel = functools.partial(
+        attend_kernel, factor=factor, layer_count=layer_count, mixed=mixed
+    )
     tok_in = pl.BlockSpec((1, tok_rows, HD), lambda h, l: (l, 0, h + head_offset))
     tok_out = pl.BlockSpec((1, tok_rows, HD), lambda h, l: (l, 0, h))
     kv_spec = pl.BlockSpec((slot_count, 2, BLK, HD), lambda h, l: (0, 0, 0, h))
     tok_shape = (layer_count, tok_rows, chunk_width)
+    in_specs = [pl.BlockSpec((1, key_total), lambda h, l: (0, 0)), tok_in, tok_in, kv_spec]
+    operands = [kpos_rel, queries, douts, kv_rows]
+    out_specs = [tok_out, tok_out, kv_spec]
+    out_shape = [
+        jax.ShapeDtypeStruct(tok_shape, jnp.bfloat16),
+        jax.ShapeDtypeStruct(tok_shape, jnp.bfloat16),
+        jax.ShapeDtypeStruct(kv_rows.shape, jnp.bfloat16),
+    ]
+    if mixed:
+        in_specs = [pl.BlockSpec(memory_space=pltpu.SMEM)] + in_specs + [kv_spec]
+        operands = [split] + operands + [next_rows]
+        own_count = own_slots
+        out_specs.append(pl.BlockSpec((own_count, 2, BLK, HD), lambda h, l: (0, 0, 0, h)))
+        out_shape.append(jax.ShapeDtypeStruct((own_count, 2, BLK, chunk_width), jnp.bfloat16))
     return pl.pallas_call(
         kernel,
         grid=(head_count, layer_count),
-        in_specs=[
-            pl.BlockSpec((1, key_total), lambda h, l: (0, 0)),
-            tok_in,
-            tok_in,
-            kv_spec,
-        ],
-        out_specs=[tok_out, tok_out, kv_spec],
-        out_shape=[
-            jax.ShapeDtypeStruct(tok_shape, jnp.bfloat16),
-            jax.ShapeDtypeStruct(tok_shape, jnp.bfloat16),
-            jax.ShapeDtypeStruct(kv_rows.shape, jnp.bfloat16),
-        ],
+        in_specs=in_specs,
+        out_specs=out_specs,
+        out_shape=out_shape,
         scratch_shapes=[
             pltpu.VMEM((key_total, HD), jnp.float32),
             pltpu.VMEM((key_total, HD), jnp.float32),
@@ -108,7 +136,7 @@
             dimension_semantics=("arbitrary", "arbitrary"),
             vmem_limit_bytes=48 * 1024 * 1024,
         ),
-    )(kpos_rel, queries, douts, kv_rows)
+    )(*operands)
 
 
 def on_device(queries, cache_keys, cache_values, douts, reads):
@@ -162,17 +190,18 @@
     key_live = jnp.repeat(slot_live, BLK)
     kpos_rel = jnp.where(key_live, key_pos - my_stretch * tok_rows, far_pos)
     kpos_rel = kpos_rel.reshape(1, -1).astype(jnp.int32)
-    src_ctx = jnp.arange(owner_count, dtype=jnp.int32) // mp_count
+    split = (my_stretch * mp_count).reshape(1).astype(jnp.int32)
     kv_first = exchange(outgoing(chunk_grids[0]))
-    out_first, dq_first, grads_first = attend(kpos_rel, queries, douts, kv_first, factor, 0)
-    later = (src_ctx >= my_stretch).reshape(owner_count, 1, 1, 1)
-    mixed = exchange(jnp.where(later, outgoing(chunk_grids[1]), grads_first))
-    own_grads = lax.dynamic_slice_in_dim(grads_first, my_stretch * mp_count, mp_count, 0)
+    out_first, dq_first, mixed_first, own_grads = attend(
+        kpos_rel, queries, douts, kv_first, factor, 0, split, outgoing(chunk_grids[1]),
+        mp_count,
+    )
+    kv_second = exchange(mixed_first)
     own_back = lax.all_to_all(own_grads, "mp", split_axis=0, concat_axis=0, tiled=True)
-    back_first = lax.dynamic_update_slice_in_dim(mixed, own_back, my_stretch * mp_count, 0)
+    back_first = lax.dynamic_update_slice_in_dim(kv_second, own_back, my_stretch * mp_count, 0)
     head_offset = chunk_width // HD
     out_second, dq_second, grads_second = attend(
-        kpos_rel, queries, douts, mixed, factor, head_offset
+        kpos_rel, queries, douts, kv_second, factor, head_offset
     )
     back_second = exchange(grads_second)
     summed = jnp.concatenate([absorb(back_first), absorb(back_second)], axis=-1)

time: 312 us -> 309 us (level)
  blocking collectives: 0 us -> 69.8 us
  waiting for transfers between devices: 186 us -> 124 us
  starting transfers between devices: 32.4 us -> 26.8 us
  other arithmetic: 13.3 us -> 9.57 us
    all_to_all x0 -> x1, blocking collectives: none -> 69.8 us  [exchange(): lax.all_to_all(operand, ('ctx', 'mp'), split_axis=0, concat_axis=0, tiled...]
    all_to_all x4 -> x3, waiting for transfers between devices: 186 us -> 124 us  [exchange(): lax.all_to_all(operand, ('ctx', 'mp'), split_axis=0, concat_axis=0, tiled...]
    select_n x1 -> x0, other arithmetic: 6.45 us -> none  [on_device(): mixed = exchange(jnp.where(later, outgoing(chunk_grids[1]), grads_first))]
    all_to_all x4 -> x3, starting transfers between devices: 27.5 us -> 21.9 us  [exchange(): lax.all_to_all(operand, ('ctx', 'mp'), split_axis=0, concat_axis=0, tiled...]
  transfers between devices with their start and end apart: 5 -> 4, of which waited for: 4 -> 3; matrix products, arithmetic and copies ran while one was open for 5% -> 4% of each run, Pallas kernels for 9% -> 9%
where the time goes in v6:
time: 309 us; the launch traced here: 308 us
  waiting for transfers between devices  124 us (40%)
  blocking collectives  69.8 us (23%)
  Pallas kernels  54.1 us (18%)
  starting transfers between devices  26.8 us (9%)
  matrix products  12 us (4%)
  local copies, waits for them, and re-layouts  11.3 us (4%)
  other arithmetic  9.57 us (3%)
    all_to_all x3, waiting for transfers between devices, exchange(): lax.all_to_all(operand, ('ctx', 'mp'), split_axis=0, concat_axis=0, tiled...  124 us
    all_to_all x1, blocking collectives, exchange(): lax.all_to_all(operand, ('ctx', 'mp'), split_axis=0, concat_axis=0, tiled...  69.8 us
    pallas_call x2, Pallas kernels, attend(): pl.pallas_call(kernel, grid=(head_count, layer_count), in_specs=in_specs,...  54.1 us
    all_to_all x3, starting transfers between devices, exchange(): lax.all_to_all(operand, ('ctx', 'mp'), split_axis=0, concat_axis=0, tiled...  21.9 us
    dot_general x2, matrix products, absorb(): lax.dot_general(picker_low, block_grid, (((0,), (0,)), ((), ())), preferr...  12 us
    select_n x1, other arithmetic, outgoing(): picked = jnp.where(hit, chunk_grid[block_id][None], picked)  6.29 us
  transfers between devices with their start and end apart: 4, of which 3 were waited for; matrix products, arithmetic and copies ran while one was open for 4% of the time, Pallas kernels for 9%

profile of v6, /device:TPU:1, one launch (start us, length us, event | category | flops | bytes accessed | tf_op | source)
XLA Modules:
  0.0 308.5 jit_solution(3290368518970111728)
XLA Ops:
  0.6 1.3 broadcast_in_dim.130
  1.9 11.5 %all-to-all-start = ((s32[128,1,96]{2,1,0:T(1,128)}), s32[128,1,96]{2,1,0:T(1,128)S(1)}, u32[]{:S(2)}, u32[]{:S(2)}) async-start(s32[128,1,96]{2,1,0:T(1,128)} %broadcast_in_dim.130), calls=%async_computation | async-start | bytes 131072 | tf_op jit(solution)/shard_map/all_to_all | solution.py:19
  13.4 1.4 reshape.165
  14.8 1.4 reshape.166
  16.2 0.6 fusion.14
  17.0 6.0 %all-to-all-done = s32[128,1,96]{2,1,0:T(1,128)S(1)} async-done(((s32[128,1,96]{2,1,0:T(1,128)}), s32[128,1,96]{2,1,0:T(1,128)S(1)}, u32[]{:S(2)}, u32[]{:S(2)}) %all-to-all-start) | async-done | bytes 49184 | tf_op jit(solution)/shard_map/all_to_all | solution.py:19
  23.0 0.1 fusion.27
  23.2 0.1 select_reduce_fusion.1
  23.3 0.1 broadcast_in_dim.132
  23.4 0.1 broadcast_in_dim.133
  23.5 0.1 broadcast_in_dim.146
  23.6 0.1 broadcast_in_dim.147
  23.7 0.1 broadcast_in_dim.139
  23.8 0.1 broadcast_in_dim.140
  23.9 6.3 %fusion.1 = (bf16[128,2,16,640]{3,2,1,0:T(8,128)(2,1)}, bf16[128,2,16,640]{3,2,1,0:T(8,128)(2,1)}) fusion(pred[128]{0:T(512)(128)(4,1)S(1)} %broadcast_in_dim.147, pred[128]{0:T(512)(128)(4,1)S(1)} %broadcast_in_dim.140, pred[128]{0:T(512)(128)(4,1)S(1)} %broadcast_in_dim.133, bf16[4,2,16,640]{3,2,1,0:T(8,128)(2,1)S(1)} %copy.68, ...), kind=kLoop, calls=%fused_computation.2 | loop fusion | flops 15728640 | bytes 11469184 | tf_op jit(solution)/shard_map/jit(_where)/select_n | solution.py:172
  30.2 0.0 copy-start.4
  30.2 0.0 copy-start
  30.2 0.0 copy-start.1
  30.2 5.4 %all-to-all-start.1 = ((bf16[128,2,16,640]{3,2,1,0:T(8,128)(2,1)}), bf16[128,2,16,640]{3,2,1,0:T(8,128)(2,1)}, u32[]{:S(2)}, u32[]{:S(2)}) async-start(bf16[128,2,16,640]{3,2,1,0:T(8,128)(2,1)} %get-tuple-element.31), calls=%async_computation.1 | async-start | bytes 10485760 | tf_op jit(solution)/shard_map/all_to_all | solution.py:19
  35.6 0.0 copy-done.4
  35.7 0.1 fusion.20
  35.8 0.1 select_reduce_fusion
  35.9 0.1 subtract_select_fusion
  36.0 0.1 select_n.68.refs_1_.refs_0_
  36.1 63.5 %all-to-all-done.1.refs_4_ = bf16[128,2,16,640]{3,2,1,0:T(8,128)(2,1)} async-done(((bf16[128,2,16,640]{3,2,1,0:T(8,128)(2,1)}), bf16[128,2,16,640]{3,2,1,0:T(8,128)(2,1)}, u32[]{:S(2)}, u32[]{:S(2)}) %all-to-all-start.1) | async-done | bytes 5242912 | tf_op jit(solution)/shard_map/all_to_all | solution.py:19
  99.6 0.0 copy-done
  99.6 0.0 copy-done.1
  99.6 27.6 %shard_map.84 = (bf16[2,192,640]{2,1,0:T(8,128)(2,1)S(1)}, bf16[2,192,640]{2,1,0:T(8,128)(2,1)S(1)}, bf16[128,2,16,640]{3,2,1,0:T(8,128)(2,1)}, bf16[4,2,16,640]{3,2,1,0:T(8,128)(2,1)}) custom-call(s32[1]{0:T(128)} %bitcast.refs_0_, s32[1,2048]{1,0:T(1,128)S(1)} %select_n.68.refs_1_.refs_0_, bf16[2,192,1280]{2,1,0:T(8,128)(2,1)S(1)} %copy-done, ...), custom_call_target="tpu_custom_call" | custom-call | tf_op jit(solution)/shard_map/pallas_call | solution.py:125
  127.2 69.8 %all_to_all.26.refs_3_ = bf16[128,2,16,640]{3,2,1,0:T(8,128)(2,1)} all-to-all(bf16[128,2,16,640]{3,2,1,0:T(8,128)(2,1)} %get-tuple-element.12), channel_id=1, replica_groups=mesh['ctx'=32,'mp'=4] {'ctx','mp'}, dimensions={0} | all-to-all | bytes 10485760 | tf_op jit(solution)/shard_map/all_to_all | solution.py:19
  197.0 4.9 %all-to-all-start.3 = ((bf16[4,2,16,640]{3,2,1,0:T(8,128)(2,1)}), bf16[4,2,16,640]{3,2,1,0:T(8,128)(2,1)}, u32[]{:S(2)}, u32[]{:S(2)}) async-start(bf16[4,2,16,640]{3,2,1,0:T(8,128)(2,1)} %get-tuple-element.16), calls=%async_computation.3 | async-start | bytes 327680 | tf_op jit(solution)/shard_map/all_to_all | solution.py:200
  201.9 26.5 %shard_map.85 = (bf16[2,192,640]{2,1,0:T(8,128)(2,1)S(1)}, bf16[2,192,640]{2,1,0:T(8,128)(2,1)S(1)}, bf16[128,2,16,640]{3,2,1,0:T(8,128)(2,1)}) custom-call(s32[1,2048]{1,0:T(1,128)S(1)} %select_n.68.refs_1_.refs_0_, bf16[2,192,1280]{2,1,0:T(8,128)(2,1)S(1)} %copy-done, bf16[2,192,1280]{2,1,0:T(8,128)(2,1)S(1)} %copy-done.1, ...), custom_call_target="tpu_custom_call" | custom-call | tf_op jit(solution)/shard_map/pallas_call | solution.py:125
  228.3 0.0 copy-start.2
  228.3 0.8 copy-done.2
  229.1 0.0 all-to-all-done.3
  229.1 0.0 copy-start.3
  229.1 5.0 %all-to-all-start.4 = ((bf16[128,2,16,640]{3,2,1,0:T(8,128)(2,1)}), bf16[128,2,16,640]{3,2,1,0:T(8,128)(2,1)}, u32[]{:S(2)}, u32[]{:S(2)}) async-start(bf16[128,2,16,640]{3,2,1,0:T(8,128)(2,1)} %get-tuple-element.17), calls=%async_computation.4 | async-start | bytes 10485760 | tf_op jit(solution)/shard_map/all_to_all | solution.py:19
  234.2 1.6 constant_dynamic-update-slice_fusion
  235.8 0.0 copy-done.3
  235.8 1.4 pad_maximum_fusion
  237.2 6.0 %fusion.6 = f32[3,4,2,16,640]{4,0,3,2,1:T(4,128)S(1)} fusion(bf16[32,4,2,16,640]{4,3,2,1,0:T(8,128)(2,1)} %bitcast.86, pred[32,3]{0,1:T(4,128)(4,1)S(1)} %fusion.24), kind=kOutput, calls=%fused_computation.8 | convolution fusion | flops 15728640 | bytes 6226016 | tf_op jit(solution)/shard_map/dot_general | solution.py:177
  243.2 54.6 %all-to-all-done.4 = bf16[128,2,16,640]{3,2,1,0:T(8,128)(2,1)} async-done(((bf16[128,2,16,640]{3,2,1,0:T(8,128)(2,1)}), bf16[128,2,16,640]{3,2,1,0:T(8,128)(2,1)}, u32[]{:S(2)}, u32[]{:S(2)}) %all-to-all-start.4) | async-done | bytes 5242912 | tf_op jit(solution)/shard_map/all_to_all | solution.py:19
  297.8 6.0 %fusion.4 = f32[3,4,2,16,640]{4,0,3,2,1:T(4,128)S(1)} fusion(bf16[32,4,2,16,640]{4,3,2,1,0:T(8,128)(2,1)} %bitcast.34, pred[32,3]{0,1:T(4,128)(4,1)S(1)} %fusion.24), kind=kOutput, calls=%fused_computation.6 | convolution fusion | flops 15728640 | bytes 6226016 | tf_op jit(solution)/shard_map/dot_general | solution.py:177
  303.8 0.7 maximum_bitcast_fusion
  304.5 0.5 fusion.28
  305.0 0.6 copy.72
  305.6 1.1 copy.75
  306.7 0.6 copy.71
  307.4 1.1 copy.74
  (13 shorter events, 0.2 us)
Async XLA Ops:
  1.9 21.1 %all-to-all-start = ((s32[128,1,96]{2,1,0:T(1,128)}), s32[128,1,96]{2,1,0:T(1,128)S(1)}, u32[]{:S(2)}, u32[]{:S(2)}) async-start(s32[128,1,96]{2,1,0:T(1,128)} %broadcast_in_dim.130), calls=%async_computation | async-start | bytes 131072 | tf_op jit(solution)/shard_map/all_to_all | solution.py:19
  30.2 5.5 %copy-start.4 = (s32[1,96]{1,0:T(1,128)S(1)}, s32[1,96]{1,0:T(1,128)}, u32[]{:S(2)}) copy-start(s32[1,96]{1,0:T(1,128)} %param.9) | copy-start | bytes 1156
  30.2 69.4 %copy-start = (bf16[2,192,1280]{2,1,0:T(8,128)(2,1)S(1)}, bf16[2,192,1280]{2,1,0:T(8,128)(2,1)}, u32[]{:S(2)}) copy-start(bf16[2,192,1280]{2,1,0:T(8,128)(2,1)} %refs_1_.1) | copy-start | bytes 2949124
  30.2 69.4 %copy-start.1 = (bf16[2,192,1280]{2,1,0:T(8,128)(2,1)S(1)}, bf16[2,192,1280]{2,1,0:T(8,128)(2,1)}, u32[]{:S(2)}) copy-start(bf16[2,192,1280]{2,1,0:T(8,128)(2,1)} %refs_2_.3) | copy-start | bytes 2949124
  30.2 69.4 %all-to-all-start.1 = ((bf16[128,2,16,640]{3,2,1,0:T(8,128)(2,1)}), bf16[128,2,16,640]{3,2,1,0:T(8,128)(2,1)}, u32[]{:S(2)}, u32[]{:S(2)}) async-start(bf16[128,2,16,640]{3,2,1,0:T(8,128)(2,1)} %get-tuple-element.31), calls=%async_computation.1 | async-start | bytes 10485760 | tf_op jit(solution)/shard_map/all_to_all | solution.py:19
  197.0 32.2 %all-to-all-start.3 = ((bf16[4,2,16,640]{3,2,1,0:T(8,128)(2,1)}), bf16[4,2,16,640]{3,2,1,0:T(8,128)(2,1)}, u32[]{:S(2)}, u32[]{:S(2)}) async-start(bf16[4,2,16,640]{3,2,1,0:T(8,128)(2,1)} %get-tuple-element.16), calls=%async_computation.3 | async-start | bytes 327680 | tf_op jit(solution)/shard_map/all_to_all | solution.py:200
  228.3 0.8 copy-start.2
  229.1 6.6 %copy-start.3 = (bf16[2,192,640]{2,1,0:T(8,128)(2,1)S(1)}, bf16[2,192,640]{2,1,0:T(8,128)(2,1)}, u32[]{:S(2)}) copy-start(bf16[2,192,640]{2,1,0:T(8,128)(2,1)} %copy-done.2) | copy-start | bytes 1474564
  229.1 68.7 %all-to-all-start.4 = ((bf16[128,2,16,640]{3,2,1,0:T(8,128)(2,1)}), bf16[128,2,16,640]{3,2,1,0:T(8,128)(2,1)}, u32[]{:S(2)}, u32[]{:S(2)}) async-start(bf16[128,2,16,640]{3,2,1,0:T(8,128)(2,1)} %get-tuple-element.17), calls=%async_computation.4 | async-start | bytes 10485760 | tf_op jit(solution)/shard_map/all_to_all | solution.py:19

commit v7 on v6

--- a/solution.py
+++ b/solution.py
@@ -162,8 +162,10 @@
         return cache_rows.reshape(per_owner, BLK, mp_count, head_width).transpose(0, 2, 1, 3)
 
     block_grid = jnp.stack([by_block(cache_keys), by_block(cache_values)], axis=2)
-    chunk_width = (head_width // HD // 2) * HD
-    chunk_grids = (block_grid[..., :chunk_width], block_grid[..., chunk_width:])
+    head_count = head_width // HD
+    outer_width = (2 * head_count // 5) * HD
+    bounds = (0, outer_width, head_width - outer_width, head_width)
+    chunk_grids = [block_grid[..., bounds[i]:bounds[i + 1]] for i in range(3)]
 
     def outgoing(chunk_grid):
         picked = jnp.zeros((ctx_count,) + chunk_grid.shape[1:], jnp.bfloat16)
@@ -191,23 +193,31 @@
     kpos_rel = jnp.where(key_live, key_pos - my_stretch * tok_rows, far_pos)
     kpos_rel = kpos_rel.reshape(1, -1).astype(jnp.int32)
     split = (my_stretch * mp_count).reshape(1).astype(jnp.int32)
+    offsets = [bound // HD for bound in bounds]
     kv_first = exchange(outgoing(chunk_grids[0]))
+    kv_middle = exchange(outgoing(chunk_grids[1]))
     out_first, dq_first, mixed_first, own_grads = attend(
-        kpos_rel, queries, douts, kv_first, factor, 0, split, outgoing(chunk_grids[1]),
-        mp_count,
-    )
-    kv_second = exchange(mixed_first)
+        kpos_rel, queries, douts, kv_first, factor, offsets[0], split,
+        outgoing(chunk_grids[2]), mp_count,
+    )
+    kv_middle, mixed_first = lax.optimization_barrier((kv_middle, mixed_first))
+    kv_last = exchange(mixed_first)
+    out_middle, dq_middle, grads_middle = attend(
+        kpos_rel, queries, douts, kv_middle, factor, offsets[1]
+    )
+    back_middle = exchange(grads_middle)
     own_back = lax.all_to_all(own_grads, "mp", split_axis=0, concat_axis=0, tiled=True)
-    back_first = lax.dynamic_update_slice_in_dim(kv_second, own_back, my_stretch * mp_count, 0)
-    head_offset = chunk_width // HD
-    out_second, dq_second, grads_second = attend(
-        kpos_rel, queries, douts, kv_second, factor, head_offset
-    )
-    back_second = exchange(grads_second)
-    summed = jnp.concatenate([absorb(back_first), absorb(back_second)], axis=-1)
+    back_first = lax.dynamic_update_slice_in_dim(kv_last, own_back, my_stretch * mp_count, 0)
+    out_last, dq_last, grads_last = attend(
+        kpos_rel, queries, douts, kv_last, factor, offsets[2]
+    )
+    back_last = exchange(grads_last)
+    summed = jnp.concatenate(
+        [absorb(back_first), absorb(back_middle), absorb(back_last)], axis=-1
+    )
     summed = summed.transpose(2, 0, 3, 1, 4).reshape(2, kv_rows, full_width)
-    attended = jnp.concatenate([out_first, out_second], axis=-1)
-    d_query = jnp.concatenate([dq_first, dq_second], axis=-1)
+    attended = jnp.concatenate([out_first, out_middle, out_last], axis=-1)
+    d_query = jnp.concatenate([dq_first, dq_middle, dq_last], axis=-1)
     return (attended, d_query, summed[0], summed[1])
 
 

time: 309 us -> 293 us (0.948)
  blocking collectives: 69.8 us -> 0 us
  waiting for transfers between devices: 124 us -> 158 us
  starting transfers between devices: 26.8 us -> 43.1 us
    all_to_all x1 -> x0, blocking collectives: 69.8 us -> none  [exchange(): lax.all_to_all(operand, ('ctx', 'mp'), split_axis=0, concat_axis=0, tiled...]
    all_to_all x3 -> x6, waiting for transfers between devices: 124 us -> 154 us  [exchange(): lax.all_to_all(operand, ('ctx', 'mp'), split_axis=0, concat_axis=0, tiled...]
    all_to_all x3 -> x6, starting transfers between devices: 21.9 us -> 38.8 us  [exchange(): lax.all_to_all(operand, ('ctx', 'mp'), split_axis=0, concat_axis=0, tiled...]
    all_to_all x1, waiting for transfers between devices: 0.01 us -> 3.57 us  [on_device(): lax.all_to_all(own_grads, 'mp', split_axis=0, concat_axis=0, tiled=True)]
    pallas_call x2 -> x3, Pallas kernels: 54.1 us -> 55.6 us  [attend(): pl.pallas_call(kernel, grid=(head_count, layer_count), in_specs=in_specs,...]
    dot_general x2 -> x3, matrix products: 12 us -> 12.1 us  [absorb(): lax.dot_general(picker_low, block_grid, (((0,), (0,)), ((), ())), preferr...]
    select_n x1 -> x2, other arithmetic: 6.29 us -> 6.27 us  [outgoing(): picked = jnp.where(hit, chunk_grid[block_id][None], picked)]
  transfers between devices with their start and end apart: 4 -> 7, of which waited for: 3 -> 7; matrix products, arithmetic and copies ran while one was open for 4% -> 5% of each run, Pallas kernels for 9% -> 19%
where the time goes in v7:
time: 293 us; the launch traced here: 292 us
  waiting for transfers between devices  158 us (54%)
  Pallas kernels  55.6 us (19%)
  starting transfers between devices  43.1 us (15%)
  local copies, waits for them, and re-layouts  13 us (4%)
  matrix products  12.1 us (4%)
  other arithmetic  9.65 us (3%)
    all_to_all x6, waiting for transfers between devices, exchange(): lax.all_to_all(operand, ('ctx', 'mp'), split_axis=0, concat_axis=0, tiled...  154 us
    pallas_call x3, Pallas kernels, attend(): pl.pallas_call(kernel, grid=(head_count, layer_count), in_specs=in_specs,...  55.6 us
    all_to_all x6, starting transfers between devices, exchange(): lax.all_to_all(operand, ('ctx', 'mp'), split_axis=0, concat_axis=0, tiled...  38.8 us
    dot_general x3, matrix products, absorb(): lax.dot_general(picker_low, block_grid, (((0,), (0,)), ((), ())), preferr...  12.1 us
    select_n x2, other arithmetic, outgoing(): picked = jnp.where(hit, chunk_grid[block_id][None], picked)  6.27 us
  transfers between devices with their start and end apart: 7, of which 7 were waited for; matrix products, arithmetic and copies ran while one was open for 5% of the time, Pallas kernels for 19%

profile of v7, /device:TPU:1, one launch (start us, length us, event | category | flops | bytes accessed | tf_op | source)
XLA Modules:
  0.0 292.1 jit_solution(34827810359330400)
XLA Ops:
  0.6 1.3 broadcast_in_dim.181
  1.9 11.5 %all-to-all-start = ((s32[128,1,96]{2,1,0:T(1,128)}), s32[128,1,96]{2,1,0:T(1,128)S(1)}, u32[]{:S(2)}, u32[]{:S(2)}) async-start(s32[128,1,96]{2,1,0:T(1,128)} %broadcast_in_dim.181), calls=%async_computation | async-start | bytes 131072 | tf_op jit(solution)/shard_map/all_to_all | solution.py:19
  13.4 1.4 reshape.175
  14.8 1.4 reshape.176
  16.2 0.6 fusion.20
  17.1 5.9 %all-to-all-done = s32[128,1,96]{2,1,0:T(1,128)S(1)} async-done(((s32[128,1,96]{2,1,0:T(1,128)}), s32[128,1,96]{2,1,0:T(1,128)S(1)}, u32[]{:S(2)}, u32[]{:S(2)}) %all-to-all-start) | async-done | bytes 49184 | tf_op jit(solution)/shard_map/all_to_all | solution.py:19
  23.0 0.1 fusion.38
  23.2 0.1 select_reduce_fusion.1
  23.3 0.1 broadcast_in_dim.183
  23.4 0.1 broadcast_in_dim.184
  23.5 0.1 broadcast_in_dim.197
  23.6 0.1 broadcast_in_dim.198
  23.7 0.1 broadcast_in_dim.190
  23.8 0.1 broadcast_in_dim.191
  23.9 4.5 %fusion.1 = (bf16[128,2,16,512]{3,2,1,0:T(8,128)(2,1)}, bf16[128,2,16,512]{3,2,1,0:T(8,128)(2,1)}) fusion(pred[128]{0:T(512)(128)(4,1)S(1)} %broadcast_in_dim.198, pred[128]{0:T(512)(128)(4,1)S(1)} %broadcast_in_dim.191, pred[128]{0:T(512)(128)(4,1)S(1)} %broadcast_in_dim.184, bf16[4,2,16,512]{3,2,1,0:T(8,128)(2,1)S(1)} %copy.84, ...), kind=kLoop, calls=%fused_computation.2 | loop fusion | flops 12582912 | bytes 9175424 | tf_op jit(solution)/shard_map/jit(_where)/select_n | solution.py:174
  28.4 5.3 %all-to-all-start.1 = ((bf16[128,2,16,512]{3,2,1,0:T(8,128)(2,1)}), bf16[128,2,16,512]{3,2,1,0:T(8,128)(2,1)}, u32[]{:S(2)}, u32[]{:S(2)}) async-start(bf16[128,2,16,512]{3,2,1,0:T(8,128)(2,1)} %get-tuple-element.44), calls=%async_computation.1 | async-start | bytes 8388608 | tf_op jit(solution)/shard_map/all_to_all | solution.py:19
  33.7 0.1 fusion.27
  33.8 1.8 fusion.9
  35.6 0.0 copy-start.9
  35.6 0.0 copy-start
  35.6 0.0 copy-start.1
  35.6 50.8 %all-to-all-done.1.refs_4_ = bf16[128,2,16,512]{3,2,1,0:T(8,128)(2,1)} async-done(((bf16[128,2,16,512]{3,2,1,0:T(8,128)(2,1)}), bf16[128,2,16,512]{3,2,1,0:T(8,128)(2,1)}, u32[]{:S(2)}, u32[]{:S(2)}) %all-to-all-start.1) | async-done | bytes 4194336 | tf_op jit(solution)/shard_map/all_to_all | solution.py:19
  86.4 5.5 %all-to-all-start.2 = ((bf16[128,2,16,256]{3,2,1,0:T(8,128)(2,1)}), bf16[128,2,16,256]{3,2,1,0:T(8,128)(2,1)}, u32[]{:S(2)}, u32[]{:S(2)}) async-start(bf16[128,2,16,256]{3,2,1,0:T(8,128)(2,1)} %fusion.9), calls=%async_computation.2 | async-start | bytes 4194304 | tf_op jit(solution)/shard_map/all_to_all | solution.py:19
  91.9 0.0 copy-done.9
  91.9 0.1 fusion.30
  92.0 0.1 select_reduce_fusion
  92.2 0.1 subtract_select_fusion
  92.3 0.1 select_n.81.refs_1_.refs_0_
  92.4 0.0 copy-done
  92.4 0.0 copy-done.1
  92.4 22.6 %shard_map.84 = (bf16[2,192,512]{2,1,0:T(8,128)(2,1)S(1)}, bf16[2,192,512]{2,1,0:T(8,128)(2,1)S(1)}, bf16[128,2,16,512]{3,2,1,0:T(8,128)(2,1)}, bf16[4,2,16,512]{3,2,1,0:T(8,128)(2,1)}) custom-call(s32[1]{0:T(128)} %bitcast.refs_0_, s32[1,2048]{1,0:T(1,128)S(1)} %select_n.81.refs_1_.refs_0_, bf16[2,192,1280]{2,1,0:T(8,128)(2,1)S(1)} %copy-done, ...), custom_call_target="tpu_custom_call" | custom-call | tf_op jit(solution)/shard_map/pallas_call | solution.py:125
  115.0 7.1 %all-to-all-done.2.refs_3_ = bf16[128,2,16,256]{3,2,1,0:T(8,128)(2,1)} async-done(((bf16[128,2,16,256]{3,2,1,0:T(8,128)(2,1)}), bf16[128,2,16,256]{3,2,1,0:T(8,128)(2,1)}, u32[]{:S(2)}, u32[]{:S(2)}) %all-to-all-start.2) | async-done | bytes 2097184 | tf_op jit(solution)/shard_map/all_to_all | solution.py:19
  122.1 4.3 %all-to-all-start.4 = ((bf16[4,2,16,512]{3,2,1,0:T(8,128)(2,1)}), bf16[4,2,16,512]{3,2,1,0:T(8,128)(2,1)S(1)}, u32[]{:S(2)}, u32[]{:S(2)}) async-start(bf16[4,2,16,512]{3,2,1,0:T(8,128)(2,1)} %get-tuple-element.25), calls=%async_computation.4 | async-start | bytes 262144 | tf_op jit(solution)/shard_map/all_to_all | solution.py:209
  126.4 3.6 %all-to-all-done.4 = bf16[4,2,16,512]{3,2,1,0:T(8,128)(2,1)S(1)} async-done(((bf16[4,2,16,512]{3,2,1,0:T(8,128)(2,1)}), bf16[4,2,16,512]{3,2,1,0:T(8,128)(2,1)S(1)}, u32[]{:S(2)}, u32[]{:S(2)}) %all-to-all-start.4) | async-done | bytes 131104 | tf_op jit(solution)/shard_map/all_to_all | solution.py:209
  130.0 0.7 copy-done.7
  130.6 5.6 %all-to-all-start.3 = ((bf16[128,2,16,512]{3,2,1,0:T(8,128)(2,1)}), bf16[128,2,16,512]{3,2,1,0:T(8,128)(2,1)}, u32[]{:S(2)}, u32[]{:S(2)}) async-start(bf16[128,2,16,512]{3,2,1,0:T(8,128)(2,1)} %get-tuple-element.20), calls=%async_computation.3 | async-start | bytes 8388608 | tf_op jit(solution)/shard_map/all_to_all | solution.py:19
  136.2 11.3 %shard_map.85 = (bf16[2,192,256]{2,1,0:T(8,128)(2,1)S(1)}, bf16[2,192,256]{2,1,0:T(8,128)(2,1)S(1)}, bf16[128,2,16,256]{3,2,1,0:T(8,128)(2,1)S(1)}) custom-call(s32[1,2048]{1,0:T(1,128)S(1)} %select_n.81.refs_1_.refs_0_, bf16[2,192,1280]{2,1,0:T(8,128)(2,1)S(1)} %copy-done, bf16[2,192,1280]{2,1,0:T(8,128)(2,1)S(1)} %copy-done.1, ...), custom_call_target="tpu_custom_call" | custom-call | tf_op jit(solution)/shard_map/pallas_call | solution.py:125
  147.5 0.0 copy-start.2
  147.5 1.4 copy-done.2
  148.9 0.7 copy-done.3
  149.6 0.7 copy-done.5
  150.3 38.7 %all-to-all-done.3.refs_3_ = bf16[128,2,16,512]{3,2,1,0:T(8,128)(2,1)} async-done(((bf16[128,2,16,512]{3,2,1,0:T(8,128)(2,1)}), bf16[128,2,16,512]{3,2,1,0:T(8,128)(2,1)}, u32[]{:S(2)}, u32[]{:S(2)}) %all-to-all-start.3) | async-done | bytes 4194336 | tf_op jit(solution)/shard_map/all_to_all | solution.py:19
  188.9 5.5 %all-to-all-start.5 = ((bf16[128,2,16,256]{3,2,1,0:T(8,128)(2,1)}), bf16[128,2,16,256]{3,2,1,0:T(8,128)(2,1)}, u32[]{:S(2)}, u32[]{:S(2)}) async-start(bf16[128,2,16,256]{3,2,1,0:T(8,128)(2,1)} %copy-done.2), calls=%async_computation.5 | async-start | bytes 4194304 | tf_op jit(solution)/shard_map/all_to_all | solution.py:19
  194.4 21.7 %shard_map.86 = (bf16[2,192,512]{2,1,0:T(8,128)(2,1)S(1)}, bf16[2,192,512]{2,1,0:T(8,128)(2,1)S(1)}, bf16[128,2,16,512]{3,2,1,0:T(8,128)(2,1)}) custom-call(s32[1,2048]{1,0:T(1,128)S(1)} %select_n.81.refs_1_.refs_0_, bf16[2,192,1280]{2,1,0:T(8,128)(2,1)S(1)} %copy-done, bf16[2,192,1280]{2,1,0:T(8,128)(2,1)S(1)} %copy-done.1, ...), custom_call_target="tpu_custom_call" | custom-call | tf_op jit(solution)/shard_map/pallas_call | solution.py:125
  216.0 8.6 %all-to-all-done.5 = bf16[128,2,16,256]{3,2,1,0:T(8,128)(2,1)} async-done(((bf16[128,2,16,256]{3,2,1,0:T(8,128)(2,1)}), bf16[128,2,16,256]{3,2,1,0:T(8,128)(2,1)}, u32[]{:S(2)}, u32[]{:S(2)}) %all-to-all-start.5) | async-done | bytes 2097184 | tf_op jit(solution)/shard_map/all_to_all | solution.py:19
  224.6 5.5 %all-to-all-start.6 = ((bf16[128,2,16,512]{3,2,1,0:T(8,128)(2,1)}), bf16[128,2,16,512]{3,2,1,0:T(8,128)(2,1)}, u32[]{:S(2)}, u32[]{:S(2)}) async-start(bf16[128,2,16,512]{3,2,1,0:T(8,128)(2,1)} %get-tuple-element.27), calls=%async_computation.6 | async-start | bytes 8388608 | tf_op jit(solution)/shard_map/all_to_all | solution.py:19
  230.2 0.0 copy-start.8
  230.2 0.0 copy-start.4
  230.2 0.0 copy-start.6
  230.2 2.9 fusion.10
  233.1 0.0 copy-done.8
  233.1 0.7 constant_dynamic-update-slice_fusion
  233.8 0.0 copy-done.4
  233.8 0.0 copy-done.6
  233.8 1.4 pad_maximum_fusion
  235.2 4.6 %fusion.6 = f32[3,4,2,16,512]{4,0,3,2,1:T(4,128)S(1)} fusion(bf16[32,4,2,16,512]{4,3,2,1,0:T(8,128)(2,1)} %bitcast.38, pred[32,3]{0,1:T(4,128)(4,1)S(1)} %fusion.34), kind=kOutput, calls=%fused_computation.8 | convolution fusion | flops 12582912 | bytes 4980832 | tf_op jit(solution)/shard_map/dot_general | solution.py:179
  239.8 43.1 %all-to-all-done.6 = bf16[128,2,16,512]{3,2,1,0:T(8,128)(2,1)} async-done(((bf16[128,2,16,512]{3,2,1,0:T(8,128)(2,1)}), bf16[128,2,16,512]{3,2,1,0:T(8,128)(2,1)}, u32[]{:S(2)}, u32[]{:S(2)}) %all-to-all-start.6) | async-done | bytes 4194336 | tf_op jit(solution)/shard_map/all_to_all | solution.py:19
  282.9 4.6 %fusion.4 = f32[3,4,2,16,512]{4,0,3,2,1:T(4,128)S(1)} fusion(bf16[32,4,2,16,512]{4,3,2,1,0:T(8,128)(2,1)} %bitcast.41, pred[32,3]{0,1:T(4,128)(4,1)S(1)} %fusion.34), kind=kOutput, calls=%fused_computation.6 | convolution fusion | flops 12582912 | bytes 4980832 | tf_op jit(solution)/shard_map/dot_general | solution.py:179
  287.5 0.7 maximum_bitcast_fusion
  288.2 0.5 fusion.39
  288.6 0.6 copy.92
  289.3 1.1 copy.95
  290.4 0.6 copy.91
  291.0 1.1 copy.94
  (19 shorter events, 0.3 us)
Async XLA Ops:
  1.9 21.1 %all-to-all-start = ((s32[128,1,96]{2,1,0:T(1,128)}), s32[128,1,96]{2,1,0:T(1,128)S(1)}, u32[]{:S(2)}, u32[]{:S(2)}) async-start(s32[128,1,96]{2,1,0:T(1,128)} %broadcast_in_dim.181), calls=%async_computation | async-start | bytes 131072 | tf_op jit(solution)/shard_map/all_to_all | solution.py:19
  28.4 58.0 %all-to-all-start.1 = ((bf16[128,2,16,512]{3,2,1,0:T(8,128)(2,1)}), bf16[128,2,16,512]{3,2,1,0:T(8,128)(2,1)}, u32[]{:S(2)}, u32[]{:S(2)}) async-start(bf16[128,2,16,512]{3,2,1,0:T(8,128)(2,1)} %get-tuple-element.44), calls=%async_computation.1 | async-start | bytes 8388608 | tf_op jit(solution)/shard_map/all_to_all | solution.py:19
  35.6 56.3 %copy-start.9 = (s32[1,96]{1,0:T(1,128)S(1)}, s32[1,96]{1,0:T(1,128)}, u32[]{:S(2)}) copy-start(s32[1,96]{1,0:T(1,128)} %param.9) | copy-start | bytes 1156
  35.6 56.8 %copy-start = (bf16[2,192,1280]{2,1,0:T(8,128)(2,1)S(1)}, bf16[2,192,1280]{2,1,0:T(8,128)(2,1)}, u32[]{:S(2)}) copy-start(bf16[2,192,1280]{2,1,0:T(8,128)(2,1)} %refs_1_.3) | copy-start | bytes 2949124
  35.6 56.8 %copy-start.1 = (bf16[2,192,1280]{2,1,0:T(8,128)(2,1)S(1)}, bf16[2,192,1280]{2,1,0:T(8,128)(2,1)}, u32[]{:S(2)}) copy-start(bf16[2,192,1280]{2,1,0:T(8,128)(2,1)} %refs_2_.5) | copy-start | bytes 2949124
  86.4 35.7 %all-to-all-start.2 = ((bf16[128,2,16,256]{3,2,1,0:T(8,128)(2,1)}), bf16[128,2,16,256]{3,2,1,0:T(8,128)(2,1)}, u32[]{:S(2)}, u32[]{:S(2)}) async-start(bf16[128,2,16,256]{3,2,1,0:T(8,128)(2,1)} %fusion.9), calls=%async_computation.2 | async-start | bytes 4194304 | tf_op jit(solution)/shard_map/all_to_all | solution.py:19
  122.1 7.8 %all-to-all-start.4 = ((bf16[4,2,16,512]{3,2,1,0:T(8,128)(2,1)}), bf16[4,2,16,512]{3,2,1,0:T(8,128)(2,1)S(1)}, u32[]{:S(2)}, u32[]{:S(2)}) async-start(bf16[4,2,16,512]{3,2,1,0:T(8,128)(2,1)} %get-tuple-element.25), calls=%async_computation.4 | async-start | bytes 262144 | tf_op jit(solution)/shard_map/all_to_all | solution.py:209
  130.0 0.7 copy-start.7
  130.6 58.3 %all-to-all-start.3 = ((bf16[128,2,16,512]{3,2,1,0:T(8,128)(2,1)}), bf16[128,2,16,512]{3,2,1,0:T(8,128)(2,1)}, u32[]{:S(2)}, u32[]{:S(2)}) async-start(bf16[128,2,16,512]{3,2,1,0:T(8,128)(2,1)} %get-tuple-element.20), calls=%async_computation.3 | async-start | bytes 8388608 | tf_op jit(solution)/shard_map/all_to_all | solution.py:19
  147.5 1.4 copy-start.2
  148.9 0.7 copy-start.3
  149.6 0.7 copy-start.5
  188.9 35.7 %all-to-all-start.5 = ((bf16[128,2,16,256]{3,2,1,0:T(8,128)(2,1)}), bf16[128,2,16,256]{3,2,1,0:T(8,128)(2,1)}, u32[]{:S(2)}, u32[]{:S(2)}) async-start(bf16[128,2,16,256]{3,2,1,0:T(8,128)(2,1)} %copy-done.2), calls=%async_computation.5 | async-start | bytes 4194304 | tf_op jit(solution)/shard_map/all_to_all | solution.py:19
  224.6 58.2 %all-to-all-start.6 = ((bf16[128,2,16,512]{3,2,1,0:T(8,128)(2,1)}), bf16[128,2,16,512]{3,2,1,0:T(8,128)(2,1)}, u32[]{:S(2)}, u32[]{:S(2)}) async-start(bf16[128,2,16,512]{3,2,1,0:T(8,128)(2,1)} %get-tuple-element.27), calls=%async_computation.6 | async-start | bytes 8388608 | tf_op jit(solution)/shard_map/all_to_all | solution.py:19
  230.2 2.9 %copy-start.8 = (bf16[4,2,16,512]{3,2,1,0:T(8,128)(2,1)S(1)}, bf16[4,2,16,512]{3,2,1,0:T(8,128)(2,1)}, u32[]{:S(2)}) copy-start(bf16[4,2,16,512]{3,2,1,0:T(8,128)(2,1)} %copy-done.7) | copy-start | bytes 393220
  230.2 3.6 %copy-start.4 = (bf16[2,192,256]{2,1,0:T(8,128)(2,1)S(1)}, bf16[2,192,256]{2,1,0:T(8,128)(2,1)}, u32[]{:S(2)}) copy-start(bf16[2,192,256]{2,1,0:T(8,128)(2,1)} %copy-done.3) | copy-start | bytes 589828
  230.2 3.6 %copy-start.6 = (bf16[2,192,256]{2,1,0:T(8,128)(2,1)S(1)}, bf16[2,192,256]{2,1,0:T(8,128)(2,1)}, u32[]{:S(2)}) copy-start(bf16[2,192,256]{2,1,0:T(8,128)(2,1)} %copy-done.5) | copy-start | bytes 589828

commit v8 on v7

--- a/solution.py
+++ b/solution.py
@@ -206,7 +206,9 @@
         kpos_rel, queries, douts, kv_middle, factor, offsets[1]
     )
     back_middle = exchange(grads_middle)
-    own_back = lax.all_to_all(own_grads, "mp", split_axis=0, concat_axis=0, tiled=True)
+    gathered = lax.all_gather(own_grads, "mp", axis=0, tiled=True)
+    gathered = gathered.reshape((mp_count, mp_count) + own_grads.shape[1:])
+    own_back = lax.dynamic_index_in_dim(gathered, my_mp, 1, keepdims=False)
     back_first = lax.dynamic_update_slice_in_dim(kv_last, own_back, my_stretch * mp_count, 0)
     out_last, dq_last, grads_last = attend(
         kpos_rel, queries, douts, kv_last, factor, offsets[2]

time: 293 us -> 292 us (level)
  blocking collectives: 0 us -> 50.3 us
  waiting for transfers between devices: 158 us -> 111 us
  starting transfers between devices: 43.1 us -> 38.9 us
    all_gather x0 -> x1, blocking collectives: none -> 50.3 us  [on_device(): gathered = lax.all_gather(own_grads, 'mp', axis=0, tiled=True)]
    all_to_all x6, waiting for transfers between devices: 154 us -> 111 us  [exchange(): lax.all_to_all(operand, ('ctx', 'mp'), split_axis=0, concat_axis=0, tiled...]
    all_to_all x1 -> x0, starting transfers between devices: 4.26 us -> none  [on_device(): lax.all_to_all(own_grads, 'mp', split_axis=0, concat_axis=0, tiled=True)]
    all_to_all x1 -> x0, waiting for transfers between devices: 3.57 us -> none  [on_device(): lax.all_to_all(own_grads, 'mp', split_axis=0, concat_axis=0, tiled=True)]
  transfers between devices with their start and end apart: 7 -> 6, of which waited for: 7 -> 5; matrix products, arithmetic and copies ran while one was open for 5% -> 5% of each run, Pallas kernels for 19% -> 19%
where the time goes in v8:
time: 292 us; the launch traced here: 291 us
  waiting for transfers between devices  111 us (38%)
  Pallas kernels  55.6 us (19%)
  blocking collectives  50.3 us (17%)
  starting transfers between devices  38.9 us (13%)
  local copies, waits for them, and re-layouts  12.4 us (4%)
  matrix products  12 us (4%)
  other arithmetic  9.67 us (3%)
    all_to_all x6, waiting for transfers between devices, exchange(): lax.all_to_all(operand, ('ctx', 'mp'), split_axis=0, concat_axis=0, tiled...  111 us
    pallas_call x3, Pallas kernels, attend(): pl.pallas_call(kernel, grid=(head_count, layer_count), in_specs=in_specs,...  55.6 us
    all_gather x1, blocking collectives, on_device(): gathered = lax.all_gather(own_grads, 'mp', axis=0, tiled=True)  50.3 us
    all_to_all x6, starting transfers between devices, exchange(): lax.all_to_all(operand, ('ctx', 'mp'), split_axis=0, concat_axis=0, tiled...  38.9 us
    dot_general x3, matrix products, absorb(): lax.dot_general(picker_low, block_grid, (((0,), (0,)), ((), ())), preferr...  12 us
    select_n x2, other arithmetic, outgoing(): picked = jnp.where(hit, chunk_grid[block_id][None], picked)  6.29 us
  transfers between devices with their start and end apart: 6, of which 5 were waited for; matrix products, arithmetic and copies ran while one was open for 5% of the time, Pallas kernels for 19%

profile of v8, /device:TPU:1, one launch (start us, length us, event | category | flops | bytes accessed | tf_op | source)
XLA Modules:
  0.0 290.9 jit_solution(16772438904379356548)
XLA Ops:
  0.6 1.3 broadcast_in_dim.181
  1.9 11.5 %all-to-all-start = ((s32[128,1,96]{2,1,0:T(1,128)}), s32[128,1,96]{2,1,0:T(1,128)S(1)}, u32[]{:S(2)}, u32[]{:S(2)}) async-start(s32[128,1,96]{2,1,0:T(1,128)} %broadcast_in_dim.181), calls=%async_computation | async-start | bytes 131072 | tf_op jit(solution)/shard_map/all_to_all | solution.py:19
  13.4 1.4 reshape.178
  14.8 1.4 reshape.179
  16.2 0.6 fusion.20
  17.1 5.9 %all-to-all-done = s32[128,1,96]{2,1,0:T(1,128)S(1)} async-done(((s32[128,1,96]{2,1,0:T(1,128)}), s32[128,1,96]{2,1,0:T(1,128)S(1)}, u32[]{:S(2)}, u32[]{:S(2)}) %all-to-all-start) | async-done | bytes 49184 | tf_op jit(solution)/shard_map/all_to_all | solution.py:19
  23.0 0.1 fusion.38
  23.2 0.1 select_reduce_fusion.1
  23.3 0.1 broadcast_in_dim.183
  23.4 0.1 broadcast_in_dim.184
  23.5 0.1 broadcast_in_dim.197
  23.6 0.1 broadcast_in_dim.198
  23.7 0.1 broadcast_in_dim.190
  23.8 0.1 broadcast_in_dim.191
  23.9 4.5 %fusion.1 = (bf16[128,2,16,512]{3,2,1,0:T(8,128)(2,1)}, bf16[128,2,16,512]{3,2,1,0:T(8,128)(2,1)}) fusion(pred[128]{0:T(512)(128)(4,1)S(1)} %broadcast_in_dim.198, pred[128]{0:T(512)(128)(4,1)S(1)} %broadcast_in_dim.191, pred[128]{0:T(512)(128)(4,1)S(1)} %broadcast_in_dim.184, bf16[4,2,16,512]{3,2,1,0:T(8,128)(2,1)S(1)} %copy.107, ...), kind=kLoop, calls=%fused_computation.2 | loop fusion | flops 12582912 | bytes 9175424 | tf_op jit(solution)/shard_map/jit(_where)/select_n | solution.py:174
  28.4 5.3 %all-to-all-start.1 = ((bf16[128,2,16,512]{3,2,1,0:T(8,128)(2,1)}), bf16[128,2,16,512]{3,2,1,0:T(8,128)(2,1)}, u32[]{:S(2)}, u32[]{:S(2)}) async-start(bf16[128,2,16,512]{3,2,1,0:T(8,128)(2,1)} %get-tuple-element.44), calls=%async_computation.1 | async-start | bytes 8388608 | tf_op jit(solution)/shard_map/all_to_all | solution.py:19
  33.7 0.1 fusion.27
  33.9 1.8 fusion.9
  35.6 0.0 copy-start.9
  35.6 0.0 copy-start
  35.6 0.0 copy-start.1
  35.6 50.8 %all-to-all-done.1.refs_4_ = bf16[128,2,16,512]{3,2,1,0:T(8,128)(2,1)} async-done(((bf16[128,2,16,512]{3,2,1,0:T(8,128)(2,1)}), bf16[128,2,16,512]{3,2,1,0:T(8,128)(2,1)}, u32[]{:S(2)}, u32[]{:S(2)}) %all-to-all-start.1) | async-done | bytes 4194336 | tf_op jit(solution)/shard_map/all_to_all | solution.py:19
  86.4 5.5 %all-to-all-start.2 = ((bf16[128,2,16,256]{3,2,1,0:T(8,128)(2,1)}), bf16[128,2,16,256]{3,2,1,0:T(8,128)(2,1)}, u32[]{:S(2)}, u32[]{:S(2)}) async-start(bf16[128,2,16,256]{3,2,1,0:T(8,128)(2,1)} %fusion.9), calls=%async_computation.2 | async-start | bytes 4194304 | tf_op jit(solution)/shard_map/all_to_all | solution.py:19
  91.9 0.0 copy-done.9
  92.0 0.1 fusion.30
  92.1 0.1 select_reduce_fusion
  92.2 0.1 subtract_select_fusion
  92.3 0.1 select_n.85.refs_1_.refs_0_
  92.4 0.0 copy-done
  92.4 0.0 copy-done.1
  92.4 22.6 %shard_map.84 = (bf16[2,192,512]{2,1,0:T(8,128)(2,1)S(1)}, bf16[2,192,512]{2,1,0:T(8,128)(2,1)S(1)}, bf16[128,2,16,512]{3,2,1,0:T(8,128)(2,1)}, bf16[4,2,16,512]{3,2,1,0:T(8,128)(2,1)S(1)}) custom-call(s32[1]{0:T(128)} %bitcast.refs_0_, s32[1,2048]{1,0:T(1,128)S(1)} %select_n.85.refs_1_.refs_0_, bf16[2,192,1280]{2,1,0:T(8,128)(2,1)S(1)} %copy-done, ...), custom_call_target="tpu_custom_call" | custom-call | tf_op jit(solution)/shard_map/pallas_call | solution.py:125
  115.0 0.0 copy-start.7
  115.0 7.1 %all-to-all-done.2.refs_3_ = bf16[128,2,16,256]{3,2,1,0:T(8,128)(2,1)} async-done(((bf16[128,2,16,256]{3,2,1,0:T(8,128)(2,1)}), bf16[128,2,16,256]{3,2,1,0:T(8,128)(2,1)}, u32[]{:S(2)}, u32[]{:S(2)}) %all-to-all-start.2) | async-done | bytes 2097184 | tf_op jit(solution)/shard_map/all_to_all | solution.py:19
  122.1 0.0 copy-done.7
  122.1 5.5 %all-to-all-start.3 = ((bf16[128,2,16,512]{3,2,1,0:T(8,128)(2,1)}), bf16[128,2,16,512]{3,2,1,0:T(8,128)(2,1)}, u32[]{:S(2)}, u32[]{:S(2)}) async-start(bf16[128,2,16,512]{3,2,1,0:T(8,128)(2,1)} %get-tuple-element.20), calls=%async_computation.3 | async-start | bytes 8388608 | tf_op jit(solution)/shard_map/all_to_all | solution.py:19
  127.7 11.3 %shard_map.85 = (bf16[2,192,256]{2,1,0:T(8,128)(2,1)S(1)}, bf16[2,192,256]{2,1,0:T(8,128)(2,1)S(1)}, bf16[128,2,16,256]{3,2,1,0:T(8,128)(2,1)S(1)}) custom-call(s32[1,2048]{1,0:T(1,128)S(1)} %select_n.85.refs_1_.refs_0_, bf16[2,192,1280]{2,1,0:T(8,128)(2,1)S(1)} %copy-done, bf16[2,192,1280]{2,1,0:T(8,128)(2,1)S(1)} %copy-done.1, ...), custom_call_target="tpu_custom_call" | custom-call | tf_op jit(solution)/shard_map/pallas_call | solution.py:125
  139.0 0.0 copy-start.2
  139.0 1.4 copy-done.2
  140.4 0.0 copy-start.3
  140.4 0.7 copy-done.3
  141.1 0.7 copy-done.5
  141.7 38.7 %all-to-all-done.3.refs_3_ = bf16[128,2,16,512]{3,2,1,0:T(8,128)(2,1)} async-done(((bf16[128,2,16,512]{3,2,1,0:T(8,128)(2,1)}), bf16[128,2,16,512]{3,2,1,0:T(8,128)(2,1)}, u32[]{:S(2)}, u32[]{:S(2)}) %all-to-all-start.3) | async-done | bytes 4194336 | tf_op jit(solution)/shard_map/all_to_all | solution.py:19
  180.4 5.5 %all-to-all-start.4 = ((bf16[128,2,16,256]{3,2,1,0:T(8,128)(2,1)}), bf16[128,2,16,256]{3,2,1,0:T(8,128)(2,1)}, u32[]{:S(2)}, u32[]{:S(2)}) async-start(bf16[128,2,16,256]{3,2,1,0:T(8,128)(2,1)} %copy-done.2), calls=%async_computation.4 | async-start | bytes 4194304 | tf_op jit(solution)/shard_map/all_to_all | solution.py:19
  185.9 21.7 %shard_map.86 = (bf16[2,192,512]{2,1,0:T(8,128)(2,1)S(1)}, bf16[2,192,512]{2,1,0:T(8,128)(2,1)S(1)}, bf16[128,2,16,512]{3,2,1,0:T(8,128)(2,1)}) custom-call(s32[1,2048]{1,0:T(1,128)S(1)} %select_n.85.refs_1_.refs_0_, bf16[2,192,1280]{2,1,0:T(8,128)(2,1)S(1)} %copy-done, bf16[2,192,1280]{2,1,0:T(8,128)(2,1)S(1)} %copy-done.1, ...), custom_call_target="tpu_custom_call" | custom-call | tf_op jit(solution)/shard_map/pallas_call | solution.py:125
  207.5 8.6 %all-to-all-done.4 = bf16[128,2,16,256]{3,2,1,0:T(8,128)(2,1)} async-done(((bf16[128,2,16,256]{3,2,1,0:T(8,128)(2,1)}), bf16[128,2,16,256]{3,2,1,0:T(8,128)(2,1)}, u32[]{:S(2)}, u32[]{:S(2)}) %all-to-all-start.4) | async-done | bytes 2097184 | tf_op jit(solution)/shard_map/all_to_all | solution.py:19
  216.1 5.6 %all-to-all-start.5 = ((bf16[128,2,16,512]{3,2,1,0:T(8,128)(2,1)}), bf16[128,2,16,512]{3,2,1,0:T(8,128)(2,1)}, u32[]{:S(2)}, u32[]{:S(2)}) async-start(bf16[128,2,16,512]{3,2,1,0:T(8,128)(2,1)} %get-tuple-element.27), calls=%async_computation.5 | async-start | bytes 8388608 | tf_op jit(solution)/shard_map/all_to_all | solution.py:19
  221.8 0.0 copy-start.4
  221.8 0.0 copy-start.6
  221.8 0.0 copy-done.8
  221.8 50.3 %all_gather.3 = bf16[16,2,16,512]{3,2,1,0:T(8,128)(2,1)S(1)} all-gather(bf16[4,2,16,512]{3,2,1,0:T(8,128)(2,1)S(1)} %copy-done.8), channel_id=1, replica_groups=mesh['ctx'=32,'mp'=4] {'mp'}, dimensions={0}, use_global_device_ids=true | all-gather | bytes 655360 | tf_op jit(solution)/shard_map/all_gather | solution.py:209
  272.1 2.8 fusion.10
  274.9 0.7 bitcast_dynamic-update-slice_fusion
  275.6 0.0 copy-done.4
  275.6 0.0 copy-done.6
  275.6 1.4 pad_maximum_fusion
  277.0 4.6 %fusion.6 = f32[3,4,2,16,512]{4,0,3,2,1:T(4,128)S(1)} fusion(bf16[32,4,2,16,512]{4,3,2,1,0:T(8,128)(2,1)} %bitcast.40, pred[32,3]{0,1:T(4,128)(4,1)S(1)} %fusion.34), kind=kOutput, calls=%fused_computation.8 | convolution fusion | flops 12582912 | bytes 4980832 | tf_op jit(solution)/shard_map/dot_general | solution.py:179
  281.6 0.0 all-to-all-done.5
  281.6 4.6 %fusion.4 = f32[3,4,2,16,512]{4,0,3,2,1:T(4,128)S(1)} fusion(bf16[32,4,2,16,512]{4,3,2,1,0:T(8,128)(2,1)} %bitcast.43, pred[32,3]{0,1:T(4,128)(4,1)S(1)} %fusion.34), kind=kOutput, calls=%fused_computation.6 | convolution fusion | flops 12582912 | bytes 4980832 | tf_op jit(solution)/shard_map/dot_general | solution.py:179
  286.2 0.7 maximum_bitcast_fusion
  286.9 0.5 fusion.39
  287.3 0.6 copy.116
  288.0 1.1 copy.120
  289.1 0.6 copy.115
  289.7 1.1 copy.119
  (18 shorter events, 0.3 us)
Async XLA Ops:
  1.9 21.1 %all-to-all-start = ((s32[128,1,96]{2,1,0:T(1,128)}), s32[128,1,96]{2,1,0:T(1,128)S(1)}, u32[]{:S(2)}, u32[]{:S(2)}) async-start(s32[128,1,96]{2,1,0:T(1,128)} %broadcast_in_dim.181), calls=%async_computation | async-start | bytes 131072 | tf_op jit(solution)/shard_map/all_to_all | solution.py:19
  28.4 58.0 %all-to-all-start.1 = ((bf16[128,2,16,512]{3,2,1,0:T(8,128)(2,1)}), bf16[128,2,16,512]{3,2,1,0:T(8,128)(2,1)}, u32[]{:S(2)}, u32[]{:S(2)}) async-start(bf16[128,2,16,512]{3,2,1,0:T(8,128)(2,1)} %get-tuple-element.44), calls=%async_computation.1 | async-start | bytes 8388608 | tf_op jit(solution)/shard_map/all_to_all | solution.py:19
  35.6 56.3 %copy-start.9 = (s32[1,96]{1,0:T(1,128)S(1)}, s32[1,96]{1,0:T(1,128)}, u32[]{:S(2)}) copy-start(s32[1,96]{1,0:T(1,128)} %param.9) | copy-start | bytes 1156
  35.6 56.8 %copy-start = (bf16[2,192,1280]{2,1,0:T(8,128)(2,1)S(1)}, bf16[2,192,1280]{2,1,0:T(8,128)(2,1)}, u32[]{:S(2)}) copy-start(bf16[2,192,1280]{2,1,0:T(8,128)(2,1)} %refs_1_.3) | copy-start | bytes 2949124
  35.6 56.8 %copy-start.1 = (bf16[2,192,1280]{2,1,0:T(8,128)(2,1)S(1)}, bf16[2,192,1280]{2,1,0:T(8,128)(2,1)}, u32[]{:S(2)}) copy-start(bf16[2,192,1280]{2,1,0:T(8,128)(2,1)} %refs_2_.5) | copy-start | bytes 2949124
  86.4 35.7 %all-to-all-start.2 = ((bf16[128,2,16,256]{3,2,1,0:T(8,128)(2,1)}), bf16[128,2,16,256]{3,2,1,0:T(8,128)(2,1)}, u32[]{:S(2)}, u32[]{:S(2)}) async-start(bf16[128,2,16,256]{3,2,1,0:T(8,128)(2,1)} %fusion.9), calls=%async_computation.2 | async-start | bytes 4194304 | tf_op jit(solution)/shard_map/all_to_all | solution.py:19
  115.0 7.1 %copy-start.7 = (bf16[4,2,16,512]{3,2,1,0:T(8,128)(2,1)}, bf16[4,2,16,512]{3,2,1,0:T(8,128)(2,1)S(1)}, u32[]{:S(2)}) copy-start(bf16[4,2,16,512]{3,2,1,0:T(8,128)(2,1)S(1)} %get-tuple-element.25) | copy-start | bytes 393220
  122.1 58.2 %all-to-all-start.3 = ((bf16[128,2,16,512]{3,2,1,0:T(8,128)(2,1)}), bf16[128,2,16,512]{3,2,1,0:T(8,128)(2,1)}, u32[]{:S(2)}, u32[]{:S(2)}) async-start(bf16[128,2,16,512]{3,2,1,0:T(8,128)(2,1)} %get-tuple-element.20), calls=%async_computation.3 | async-start | bytes 8388608 | tf_op jit(solution)/shard_map/all_to_all | solution.py:19
  139.0 1.4 copy-start.2
  140.4 0.7 copy-start.3
  141.1 0.7 copy-start.5
  180.4 35.7 %all-to-all-start.4 = ((bf16[128,2,16,256]{3,2,1,0:T(8,128)(2,1)}), bf16[128,2,16,256]{3,2,1,0:T(8,128)(2,1)}, u32[]{:S(2)}, u32[]{:S(2)}) async-start(bf16[128,2,16,256]{3,2,1,0:T(8,128)(2,1)} %copy-done.2), calls=%async_computation.4 | async-start | bytes 4194304 | tf_op jit(solution)/shard_map/all_to_all | solution.py:19
  216.1 5.7 %copy-start.8 = (bf16[4,2,16,512]{3,2,1,0:T(8,128)(2,1)S(1)}, bf16[4,2,16,512]{3,2,1,0:T(8,128)(2,1)}, u32[]{:S(2)}) copy-start(bf16[4,2,16,512]{3,2,1,0:T(8,128)(2,1)} %copy-done.7) | copy-start | bytes 393220
  216.1 65.5 %all-to-all-start.5 = ((bf16[128,2,16,512]{3,2,1,0:T(8,128)(2,1)}), bf16[128,2,16,512]{3,2,1,0:T(8,128)(2,1)}, u32[]{:S(2)}, u32[]{:S(2)}) async-start(bf16[128,2,16,512]{3,2,1,0:T(8,128)(2,1)} %get-tuple-element.27), calls=%async_computation.5 | async-start | bytes 8388608 | tf_op jit(solution)/shard_map/all_to_all | solution.py:19
  221.8 53.8 %copy-start.4 = (bf16[2,192,256]{2,1,0:T(8,128)(2,1)S(1)}, bf16[2,192,256]{2,1,0:T(8,128)(2,1)}, u32[]{:S(2)}) copy-start(bf16[2,192,256]{2,1,0:T(8,128)(2,1)} %copy-done.3) | copy-start | bytes 589828
  221.8 53.8 %copy-start.6 = (bf16[2,192,256]{2,1,0:T(8,128)(2,1)S(1)}, bf16[2,192,256]{2,1,0:T(8,128)(2,1)}, u32[]{:S(2)}) copy-start(bf16[2,192,256]{2,1,0:T(8,128)(2,1)} %copy-done.5) | copy-start | bytes 589828

commit v9 on v8

--- a/solution.py
+++ b/solution.py
@@ -206,17 +206,27 @@
         kpos_rel, queries, douts, kv_middle, factor, offsets[1]
     )
     back_middle = exchange(grads_middle)
+    own_row = jnp.arange(ctx_count, dtype=jnp.int32)[:, None] == my_stretch
+    picker_others = jnp.where(own_row, jnp.zeros_like(picker_low), picker_low)
+    first_rows = kv_last.reshape((ctx_count, mp_count) + kv_last.shape[1:])
+    first_main = lax.dot_general(
+        picker_others, first_rows, (((0,), (0,)), ((), ())), preferred_element_type=jnp.float32
+    )
+    middle_sum = absorb(back_middle)
+    own_grads, first_main, middle_sum = lax.optimization_barrier(
+        (own_grads, first_main, middle_sum)
+    )
     gathered = lax.all_gather(own_grads, "mp", axis=0, tiled=True)
     gathered = gathered.reshape((mp_count, mp_count) + own_grads.shape[1:])
     own_back = lax.dynamic_index_in_dim(gathered, my_mp, 1, keepdims=False)
-    back_first = lax.dynamic_update_slice_in_dim(kv_last, own_back, my_stretch * mp_count, 0)
+    own_pick = lax.dynamic_index_in_dim(picker_low, my_stretch, 0, keepdims=False)
+    own_pick = own_pick.astype(jnp.float32).reshape(per_owner, 1, 1, 1, 1)
+    first_sum = first_main + own_pick * own_back.astype(jnp.float32)[None]
     out_last, dq_last, grads_last = attend(
         kpos_rel, queries, douts, kv_last, factor, offsets[2]
     )
     back_last = exchange(grads_last)
-    summed = jnp.concatenate(
-        [absorb(back_first), absorb(back_middle), absorb(back_last)], axis=-1
-    )
+    summed = jnp.concatenate([first_sum, middle_sum, absorb(back_last)], axis=-1)
     summed = summed.transpose(2, 0, 3, 1, 4).reshape(2, kv_rows, full_width)
     attended = jnp.concatenate([out_first, out_middle, out_last], axis=-1)
     d_query = jnp.concatenate([dq_first, dq_middle, dq_last], axis=-1)

time: 292 us -> 286 us (0.979)
  blocking collectives: 50.3 us -> 42 us
    all_gather x1, blocking collectives: 50.3 us -> 42 us  [on_device(): gathered = lax.all_gather(own_grads, 'mp', axis=0, tiled=True)]
    dot_general x0 -> x1, matrix products: none -> 4.68 us  [on_device(): lax.dot_general(picker_others, first_rows, (((0,), (0,)), ((), ())), pref...]
    dot_general x3 -> x2, matrix products: 12 us -> 7.53 us  [absorb(): lax.dot_general(picker_low, block_grid, (((0,), (0,)), ((), ())), preferr...]
  transfers between devices with their start and end apart: 6 -> 6, of which waited for: 5 -> 6; matrix products, arithmetic and copies ran while one was open for 5% -> 6% of each run, Pallas kernels for 19% -> 20%
where the time goes in v9:
time: 286 us; the launch traced here: 285 us
  waiting for transfers between devices  112 us (39%)
  Pallas kernels  55.6 us (19%)
  blocking collectives  42 us (15%)
  starting transfers between devices  38.8 us (14%)
  matrix products  12.2 us (4%)
  local copies, waits for them, and re-layouts  11.9 us (4%)
  other arithmetic  11.4 us (4%)
    all_to_all x6, waiting for transfers between devices, exchange(): lax.all_to_all(operand, ('ctx', 'mp'), split_axis=0, concat_axis=0, tiled...  112 us
    pallas_call x3, Pallas kernels, attend(): pl.pallas_call(kernel, grid=(head_count, layer_count), in_specs=in_specs,...  55.6 us
    all_gather x1, blocking collectives, on_device(): gathered = lax.all_gather(own_grads, 'mp', axis=0, tiled=True)  42 us
    all_to_all x6, starting transfers between devices, exchange(): lax.all_to_all(operand, ('ctx', 'mp'), split_axis=0, concat_axis=0, tiled...  38.8 us
    dot_general x2, matrix products, absorb(): lax.dot_general(picker_low, block_grid, (((0,), (0,)), ((), ())), preferr...  7.53 us
    select_n x2, other arithmetic, outgoing(): picked = jnp.where(hit, chunk_grid[block_id][None], picked)  6.3 us
  transfers between devices with their start and end apart: 6, of which 6 were waited for; matrix products, arithmetic and copies ran while one was open for 6% of the time, Pallas kernels for 20%

profile of v9, /device:TPU:1, one launch (start us, length us, event | category | flops | bytes accessed | tf_op | source)
XLA Modules:
  0.0 284.5 jit_solution(4406503826654029180)
XLA Ops:
  0.6 1.3 broadcast_in_dim.194
  1.9 11.5 %all-to-all-start = ((s32[128,1,96]{2,1,0:T(1,128)}), s32[128,1,96]{2,1,0:T(1,128)S(1)}, u32[]{:S(2)}, u32[]{:S(2)}) async-start(s32[128,1,96]{2,1,0:T(1,128)} %broadcast_in_dim.194), calls=%async_computation | async-start | bytes 131072 | tf_op jit(solution)/shard_map/all_to_all | solution.py:19
  13.4 1.4 reshape.198
  14.8 1.4 reshape.199
  16.2 0.6 fusion.20
  17.1 5.9 %all-to-all-done = s32[128,1,96]{2,1,0:T(1,128)S(1)} async-done(((s32[128,1,96]{2,1,0:T(1,128)}), s32[128,1,96]{2,1,0:T(1,128)S(1)}, u32[]{:S(2)}, u32[]{:S(2)}) %all-to-all-start) | async-done | bytes 49184 | tf_op jit(solution)/shard_map/all_to_all | solution.py:19
  23.0 0.1 fusion.47
  23.2 0.1 select_reduce_fusion.1
  23.3 0.7 fusion.46
  24.0 0.2 slice_reduce_fusion.2
  24.2 0.1 broadcast_in_dim.196
  24.2 0.1 broadcast_in_dim.197
  24.4 0.1 broadcast_in_dim.203
  24.4 0.1 broadcast_in_dim.204
  24.6 0.1 broadcast_in_dim.210
  24.6 0.1 broadcast_in_dim.211
  24.8 4.5 %fusion.1 = (bf16[128,2,16,512]{3,2,1,0:T(8,128)(2,1)}, bf16[128,2,16,512]{3,2,1,0:T(8,128)(2,1)}) fusion(pred[128]{0:T(512)(128)(4,1)S(1)} %broadcast_in_dim.211, pred[128]{0:T(512)(128)(4,1)S(1)} %broadcast_in_dim.204, pred[128]{0:T(512)(128)(4,1)S(1)} %broadcast_in_dim.197, bf16[4,2,16,512]{3,2,1,0:T(8,128)(2,1)S(1)} %copy.120, ...), kind=kLoop, calls=%fused_computation.2 | loop fusion | flops 12582912 | bytes 9175424 | tf_op jit(solution)/shard_map/jit(_where)/select_n | solution.py:174
  29.3 5.3 %all-to-all-start.1 = ((bf16[128,2,16,512]{3,2,1,0:T(8,128)(2,1)}), bf16[128,2,16,512]{3,2,1,0:T(8,128)(2,1)}, u32[]{:S(2)}, u32[]{:S(2)}) async-start(bf16[128,2,16,512]{3,2,1,0:T(8,128)(2,1)} %get-tuple-element.53), calls=%async_computation.1 | async-start | bytes 8388608 | tf_op jit(solution)/shard_map/all_to_all | solution.py:19
  34.6 0.1 fusion.27
  34.8 1.8 fusion.9
  36.5 0.0 copy-start.9
  36.5 0.0 copy-start
  36.5 0.0 copy-start.1
  36.5 50.8 %all-to-all-done.1.refs_4_ = bf16[128,2,16,512]{3,2,1,0:T(8,128)(2,1)} async-done(((bf16[128,2,16,512]{3,2,1,0:T(8,128)(2,1)}), bf16[128,2,16,512]{3,2,1,0:T(8,128)(2,1)}, u32[]{:S(2)}, u32[]{:S(2)}) %all-to-all-start.1) | async-done | bytes 4194336 | tf_op jit(solution)/shard_map/all_to_all | solution.py:19
  87.3 5.5 %all-to-all-start.2 = ((bf16[128,2,16,256]{3,2,1,0:T(8,128)(2,1)}), bf16[128,2,16,256]{3,2,1,0:T(8,128)(2,1)}, u32[]{:S(2)}, u32[]{:S(2)}) async-start(bf16[128,2,16,256]{3,2,1,0:T(8,128)(2,1)} %fusion.9), calls=%async_computation.2 | async-start | bytes 4194304 | tf_op jit(solution)/shard_map/all_to_all | solution.py:19
  92.8 0.0 copy-done.9
  92.8 0.1 fusion.30
  93.0 0.1 select_reduce_fusion
  93.1 0.1 subtract_select_fusion
  93.2 0.1 select_n.90.refs_1_.refs_0_
  93.3 0.0 copy-done
  93.3 0.0 copy-done.1
  93.3 22.6 %shard_map.84 = (bf16[2,192,512]{2,1,0:T(8,128)(2,1)S(1)}, bf16[2,192,512]{2,1,0:T(8,128)(2,1)S(1)}, bf16[128,2,16,512]{3,2,1,0:T(8,128)(2,1)}, bf16[4,2,16,512]{3,2,1,0:T(8,128)(2,1)S(1)}) custom-call(s32[1]{0:T(128)} %bitcast.refs_0_, s32[1,2048]{1,0:T(1,128)S(1)} %select_n.90.refs_1_.refs_0_, bf16[2,192,1280]{2,1,0:T(8,128)(2,1)S(1)} %copy-done, ...), custom_call_target="tpu_custom_call" | custom-call | tf_op jit(solution)/shard_map/pallas_call | solution.py:125
  115.9 0.0 copy-start.7
  115.9 7.1 %all-to-all-done.2.refs_3_ = bf16[128,2,16,256]{3,2,1,0:T(8,128)(2,1)} async-done(((bf16[128,2,16,256]{3,2,1,0:T(8,128)(2,1)}), bf16[128,2,16,256]{3,2,1,0:T(8,128)(2,1)}, u32[]{:S(2)}, u32[]{:S(2)}) %all-to-all-start.2) | async-done | bytes 2097184 | tf_op jit(solution)/shard_map/all_to_all | solution.py:19
  123.0 0.0 copy-done.7
  123.0 5.5 %all-to-all-start.3 = ((bf16[128,2,16,512]{3,2,1,0:T(8,128)(2,1)}), bf16[128,2,16,512]{3,2,1,0:T(8,128)(2,1)}, u32[]{:S(2)}, u32[]{:S(2)}) async-start(bf16[128,2,16,512]{3,2,1,0:T(8,128)(2,1)} %get-tuple-element.23), calls=%async_computation.3 | async-start | bytes 8388608 | tf_op jit(solution)/shard_map/all_to_all | solution.py:19
  128.6 11.3 %shard_map.85 = (bf16[2,192,256]{2,1,0:T(8,128)(2,1)S(1)}, bf16[2,192,256]{2,1,0:T(8,128)(2,1)S(1)}, bf16[128,2,16,256]{3,2,1,0:T(8,128)(2,1)S(1)}) custom-call(s32[1,2048]{1,0:T(1,128)S(1)} %select_n.90.refs_1_.refs_0_, bf16[2,192,1280]{2,1,0:T(8,128)(2,1)S(1)} %copy-done, bf16[2,192,1280]{2,1,0:T(8,128)(2,1)S(1)} %copy-done.1, ...), custom_call_target="tpu_custom_call" | custom-call | tf_op jit(solution)/shard_map/pallas_call | solution.py:125
  139.9 0.0 copy-start.2
  139.9 1.4 copy-done.2
  141.2 0.7 copy-done.3
  141.9 0.7 copy-done.5
  142.6 38.7 %all-to-all-done.3.refs_3_ = bf16[128,2,16,512]{3,2,1,0:T(8,128)(2,1)} async-done(((bf16[128,2,16,512]{3,2,1,0:T(8,128)(2,1)}), bf16[128,2,16,512]{3,2,1,0:T(8,128)(2,1)}, u32[]{:S(2)}, u32[]{:S(2)}) %all-to-all-start.3) | async-done | bytes 4194336 | tf_op jit(solution)/shard_map/all_to_all | solution.py:19
  181.3 5.5 %all-to-all-start.4 = ((bf16[128,2,16,256]{3,2,1,0:T(8,128)(2,1)}), bf16[128,2,16,256]{3,2,1,0:T(8,128)(2,1)}, u32[]{:S(2)}, u32[]{:S(2)}) async-start(bf16[128,2,16,256]{3,2,1,0:T(8,128)(2,1)} %copy-done.2), calls=%async_computation.4 | async-start | bytes 4194304 | tf_op jit(solution)/shard_map/all_to_all | solution.py:19
  186.8 21.7 %shard_map.86 = (bf16[2,192,512]{2,1,0:T(8,128)(2,1)S(1)}, bf16[2,192,512]{2,1,0:T(8,128)(2,1)S(1)}, bf16[128,2,16,512]{3,2,1,0:T(8,128)(2,1)}) custom-call(s32[1,2048]{1,0:T(1,128)S(1)} %select_n.90.refs_1_.refs_0_, bf16[2,192,1280]{2,1,0:T(8,128)(2,1)S(1)} %copy-done, bf16[2,192,1280]{2,1,0:T(8,128)(2,1)S(1)} %copy-done.1, ...), custom_call_target="tpu_custom_call" | custom-call | tf_op jit(solution)/shard_map/pallas_call | solution.py:125
  208.4 8.6 %all-to-all-done.4 = bf16[128,2,16,256]{3,2,1,0:T(8,128)(2,1)} async-done(((bf16[128,2,16,256]{3,2,1,0:T(8,128)(2,1)}), bf16[128,2,16,256]{3,2,1,0:T(8,128)(2,1)}, u32[]{:S(2)}, u32[]{:S(2)}) %all-to-all-start.4) | async-done | bytes 2097184 | tf_op jit(solution)/shard_map/all_to_all | solution.py:19
  217.0 5.5 %all-to-all-start.5 = ((bf16[128,2,16,512]{3,2,1,0:T(8,128)(2,1)}), bf16[128,2,16,512]{3,2,1,0:T(8,128)(2,1)}, u32[]{:S(2)}, u32[]{:S(2)}) async-start(bf16[128,2,16,512]{3,2,1,0:T(8,128)(2,1)} %get-tuple-element.33), calls=%async_computation.5 | async-start | bytes 8388608 | tf_op jit(solution)/shard_map/all_to_all | solution.py:19
  222.5 0.7 bitcast_convert_fusion.1
  223.2 2.9 %fusion.10 = f32[3,4,2,16,256]{4,0,3,2,1:T(4,128)S(1)} fusion(bf16[32,4,2,16,256]{4,3,2,1,0:T(8,128)(2,1)} %bitcast.36, s32[32]{0:T(128)S(1)} %select_reduce_fusion.1, pred[32]{0:T(512)(128)(4,1)S(1)} %get-tuple-element.37), kind=kOutput, calls=%fused_computation.14 | convolution fusion | flops 6291648 | bytes 2490528 | tf_op jit(solution)/shard_map/dot_general | solution.py:179
  226.1 4.7 %fusion.6 = f32[3,4,2,16,512]{4,0,3,2,1:T(4,128)S(1)} fusion(bf16[32,4,2,16,512]{4,3,2,1,0:T(8,128)(2,1)} %bitcast.34, pred[32]{0:T(512)(128)(4,1)S(1)} %iota_compare_fusion.2, s32[32]{0:T(128)S(1)} %select_reduce_fusion.1, pred[32]{0:T(512)(128)(4,1)S(1)} %get-tuple-element.37), kind=kOutput, calls=%fused_computation.8 | convolution fusion | flops 12583296 | bytes 4980928 | tf_op jit(solution)/shard_map/dot_general | solution.py:212
  230.8 0.0 copy-done.8
  230.8 42.0 %all_gather.3 = bf16[16,2,16,512]{3,2,1,0:T(8,128)(2,1)S(1)} all-gather(bf16[4,2,16,512]{3,2,1,0:T(8,128)(2,1)S(1)} %copy-done.8), channel_id=1, replica_groups=mesh['ctx'=32,'mp'=4] {'mp'}, dimensions={0}, use_global_device_ids=true | all-gather | bytes 655360 | tf_op jit(solution)/shard_map/all_gather | solution.py:219
  272.9 0.3 multiply_add_fusion
  273.2 0.0 copy-done.4
  273.2 0.0 copy-done.6
  273.3 1.4 pad_maximum_fusion
  274.6 0.6 all-to-all-done.5
  275.2 4.6 %fusion.4 = f32[3,4,2,16,512]{4,0,3,2,1:T(4,128)S(1)} fusion(bf16[32,4,2,16,512]{4,3,2,1,0:T(8,128)(2,1)} %bitcast.41, s32[32]{0:T(128)S(1)} %select_reduce_fusion.1, pred[32]{0:T(512)(128)(4,1)S(1)} %get-tuple-element.37), kind=kOutput, calls=%fused_computation.6 | convolution fusion | flops 12583104 | bytes 4980896 | tf_op jit(solution)/shard_map/dot_general | solution.py:179
  279.9 0.7 maximum_bitcast_fusion
  280.6 0.5 fusion.48
  281.0 0.6 copy.131
  281.7 1.1 copy.140
  282.8 0.6 copy.132
  283.4 1.1 copy.141
  (21 shorter events, 0.3 us)
Async XLA Ops:
  1.9 21.1 %all-to-all-start = ((s32[128,1,96]{2,1,0:T(1,128)}), s32[128,1,96]{2,1,0:T(1,128)S(1)}, u32[]{:S(2)}, u32[]{:S(2)}) async-start(s32[128,1,96]{2,1,0:T(1,128)} %broadcast_in_dim.194), calls=%async_computation | async-start | bytes 131072 | tf_op jit(solution)/shard_map/all_to_all | solution.py:19
  29.3 58.0 %all-to-all-start.1 = ((bf16[128,2,16,512]{3,2,1,0:T(8,128)(2,1)}), bf16[128,2,16,512]{3,2,1,0:T(8,128)(2,1)}, u32[]{:S(2)}, u32[]{:S(2)}) async-start(bf16[128,2,16,512]{3,2,1,0:T(8,128)(2,1)} %get-tuple-element.53), calls=%async_computation.1 | async-start | bytes 8388608 | tf_op jit(solution)/shard_map/all_to_all | solution.py:19
  36.5 56.3 %copy-start.9 = (s32[1,96]{1,0:T(1,128)S(1)}, s32[1,96]{1,0:T(1,128)}, u32[]{:S(2)}) copy-start(s32[1,96]{1,0:T(1,128)} %param.9) | copy-start | bytes 1156
  36.5 56.8 %copy-start = (bf16[2,192,1280]{2,1,0:T(8,128)(2,1)S(1)}, bf16[2,192,1280]{2,1,0:T(8,128)(2,1)}, u32[]{:S(2)}) copy-start(bf16[2,192,1280]{2,1,0:T(8,128)(2,1)} %refs_1_.3) | copy-start | bytes 2949124
  36.5 56.8 %copy-start.1 = (bf16[2,192,1280]{2,1,0:T(8,128)(2,1)S(1)}, bf16[2,192,1280]{2,1,0:T(8,128)(2,1)}, u32[]{:S(2)}) copy-start(bf16[2,192,1280]{2,1,0:T(8,128)(2,1)} %refs_2_.5) | copy-start | bytes 2949124
  87.3 35.7 %all-to-all-start.2 = ((bf16[128,2,16,256]{3,2,1,0:T(8,128)(2,1)}), bf16[128,2,16,256]{3,2,1,0:T(8,128)(2,1)}, u32[]{:S(2)}, u32[]{:S(2)}) async-start(bf16[128,2,16,256]{3,2,1,0:T(8,128)(2,1)} %fusion.9), calls=%async_computation.2 | async-start | bytes 4194304 | tf_op jit(solution)/shard_map/all_to_all | solution.py:19
  115.9 7.1 %copy-start.7 = (bf16[4,2,16,512]{3,2,1,0:T(8,128)(2,1)}, bf16[4,2,16,512]{3,2,1,0:T(8,128)(2,1)S(1)}, u32[]{:S(2)}) copy-start(bf16[4,2,16,512]{3,2,1,0:T(8,128)(2,1)S(1)} %get-tuple-element.31) | copy-start | bytes 393220
  123.0 58.2 %all-to-all-start.3 = ((bf16[128,2,16,512]{3,2,1,0:T(8,128)(2,1)}), bf16[128,2,16,512]{3,2,1,0:T(8,128)(2,1)}, u32[]{:S(2)}, u32[]{:S(2)}) async-start(bf16[128,2,16,512]{3,2,1,0:T(8,128)(2,1)} %get-tuple-element.23), calls=%async_computation.3 | async-start | bytes 8388608 | tf_op jit(solution)/shard_map/all_to_all | solution.py:19
  139.9 1.4 copy-start.2
  141.2 0.7 copy-start.3
  141.9 0.7 copy-start.5
  181.3 35.7 %all-to-all-start.4 = ((bf16[128,2,16,256]{3,2,1,0:T(8,128)(2,1)}), bf16[128,2,16,256]{3,2,1,0:T(8,128)(2,1)}, u32[]{:S(2)}, u32[]{:S(2)}) async-start(bf16[128,2,16,256]{3,2,1,0:T(8,128)(2,1)} %copy-done.2), calls=%async_computation.4 | async-start | bytes 4194304 | tf_op jit(solution)/shard_map/all_to_all | solution.py:19
  217.0 58.2 %all-to-all-start.5 = ((bf16[128,2,16,512]{3,2,1,0:T(8,128)(2,1)}), bf16[128,2,16,512]{3,2,1,0:T(8,128)(2,1)}, u32[]{:S(2)}, u32[]{:S(2)}) async-start(bf16[128,2,16,512]{3,2,1,0:T(8,128)(2,1)} %get-tuple-element.33), calls=%async_computation.5 | async-start | bytes 8388608 | tf_op jit(solution)/shard_map/all_to_all | solution.py:19
  226.1 4.7 %copy-start.8 = (bf16[4,2,16,512]{3,2,1,0:T(8,128)(2,1)S(1)}, bf16[4,2,16,512]{3,2,1,0:T(8,128)(2,1)}, u32[]{:S(2)}) copy-start(bf16[4,2,16,512]{3,2,1,0:T(8,128)(2,1)} %copy-done.7) | copy-start | bytes 393220
  230.8 42.4 %copy-start.4 = (bf16[2,192,256]{2,1,0:T(8,128)(2,1)S(1)}, bf16[2,192,256]{2,1,0:T(8,128)(2,1)}, u32[]{:S(2)}) copy-start(bf16[2,192,256]{2,1,0:T(8,128)(2,1)} %copy-done.3) | copy-start | bytes 589828
  230.8 42.4 %copy-start.6 = (bf16[2,192,256]{2,1,0:T(8,128)(2,1)S(1)}, bf16[2,192,256]{2,1,0:T(8,128)(2,1)}, u32[]{:S(2)}) copy-start(bf16[2,192,256]{2,1,0:T(8,128)(2,1)} %copy-done.5) | copy-start | bytes 589828

commit v10 on v9

--- a/solution.py
+++ b/solution.py
@@ -226,7 +226,12 @@
         kpos_rel, queries, douts, kv_last, factor, offsets[2]
     )
     back_last = exchange(grads_last)
-    summed = jnp.concatenate([first_sum, middle_sum, absorb(back_last)], axis=-1)
+    last_rows = back_last.reshape((ctx_count, mp_count) + back_last.shape[1:]).astype(jnp.float32)
+    last_sum = jnp.stack([
+        jnp.sum(jnp.where(picker[:, block_id].reshape(ctx_count, 1, 1, 1, 1), last_rows, 0.0), axis=0)
+        for block_id in range(per_owner)
+    ])
+    summed = jnp.concatenate([first_sum, middle_sum, last_sum], axis=-1)
     summed = summed.transpose(2, 0, 3, 1, 4).reshape(2, kv_rows, full_width)
     attended = jnp.concatenate([out_first, out_middle, out_last], axis=-1)
     d_query = jnp.concatenate([dq_first, dq_middle, dq_last], axis=-1)

time: 286 us -> 287 us (level)
  other arithmetic: 11.4 us -> 16.5 us
  matrix products: 12.2 us -> 7.57 us
    dot_general x2 -> x1, matrix products: 7.53 us -> 2.89 us  [absorb(): lax.dot_general(picker_low, block_grid, (((0,), (0,)), ((), ())), preferr...]
    reduce_sum x0 -> x1, other arithmetic: none -> 4.57 us  [on_device(): jnp.sum(jnp.where(picker[:, block_id].reshape(ctx_count, 1, 1, 1, 1), las...]
  transfers between devices with their start and end apart: 6 -> 6, of which waited for: 6 -> 6; matrix products, arithmetic and copies ran while one was open for 6% -> 6% of each run, Pallas kernels for 20% -> 19%
where the time goes in v10:
time: 287 us; the launch traced here: 286 us
  waiting for transfers between devices  112 us (39%)
  Pallas kernels  55.6 us (19%)
  blocking collectives  42 us (15%)
  starting transfers between devices  38.7 us (13%)
  other arithmetic  16.5 us (6%)
  local copies, waits for them, and re-layouts  12.9 us (4%)
  matrix products  7.57 us (3%)
    all_to_all x6, waiting for transfers between devices, exchange(): lax.all_to_all(operand, ('ctx', 'mp'), split_axis=0, concat_axis=0, tiled...  112 us
    pallas_call x3, Pallas kernels, attend(): pl.pallas_call(kernel, grid=(head_count, layer_count), in_specs=in_specs,...  55.6 us
    all_gather x1, blocking collectives, on_device(): gathered = lax.all_gather(own_grads, 'mp', axis=0, tiled=True)  42 us
    all_to_all x6, starting transfers between devices, exchange(): lax.all_to_all(operand, ('ctx', 'mp'), split_axis=0, concat_axis=0, tiled...  38.7 us
    select_n x2, other arithmetic, outgoing(): picked = jnp.where(hit, chunk_grid[block_id][None], picked)  6.31 us
  transfers between devices with their start and end apart: 6, of which 6 were waited for; matrix products, arithmetic and copies ran while one was open for 6% of the time, Pallas kernels for 19%

profile of v10, /device:TPU:1, one launch (start us, length us, event | category | flops | bytes accessed | tf_op | source)
XLA Modules:
  0.0 286.1 jit_solution(15390478754597893064)
XLA Ops:
  0.6 1.3 broadcast_in_dim.218
  1.9 11.5 %all-to-all-start = ((s32[128,1,96]{2,1,0:T(1,128)}), s32[128,1,96]{2,1,0:T(1,128)S(1)}, u32[]{:S(2)}, u32[]{:S(2)}) async-start(s32[128,1,96]{2,1,0:T(1,128)} %broadcast_in_dim.218), calls=%async_computation | async-start | bytes 131072 | tf_op jit(solution)/shard_map/all_to_all | solution.py:19
  13.4 1.4 reshape.198
  14.8 1.4 reshape.199
  16.2 0.6 fusion.21
  17.1 5.9 %all-to-all-done = s32[128,1,96]{2,1,0:T(1,128)S(1)} async-done(((s32[128,1,96]{2,1,0:T(1,128)}), s32[128,1,96]{2,1,0:T(1,128)S(1)}, u32[]{:S(2)}, u32[]{:S(2)}) %all-to-all-start) | async-done | bytes 49184 | tf_op jit(solution)/shard_map/all_to_all | solution.py:19
  23.0 0.1 fusion.46
  23.2 0.1 select_reduce_fusion.1
  23.3 0.7 fusion.45
  24.0 0.2 slice_reduce_fusion.2
  24.2 0.0 copy-start.13
  24.2 0.0 copy-start.11
  24.2 0.6 copy-done.9
  24.8 0.1 broadcast_in_dim.220
  24.8 0.1 broadcast_in_dim.221
  24.9 0.0 copy-done.13
  25.0 0.1 broadcast_in_dim.227
  25.0 0.1 broadcast_in_dim.228
  25.1 0.0 copy-done.11
  25.2 0.1 broadcast_in_dim.234
  25.2 0.1 broadcast_in_dim.235
  25.3 4.5 %fusion.4 = (bf16[128,2,16,512]{3,2,1,0:T(8,128)(2,1)}, bf16[128,2,16,512]{3,2,1,0:T(8,128)(2,1)}) fusion(pred[128]{0:T(512)(128)(4,1)S(1)} %broadcast_in_dim.235, pred[128]{0:T(512)(128)(4,1)S(1)} %broadcast_in_dim.228, pred[128]{0:T(512)(128)(4,1)S(1)} %broadcast_in_dim.221, bf16[4,2,16,512]{3,2,1,0:T(8,128)(2,1)S(1)} %copy.110, ...), kind=kLoop, calls=%fused_computation.8 | loop fusion | flops 12582912 | bytes 9175424 | tf_op jit(solution)/shard_map/jit(_where)/select_n | solution.py:174
  29.9 5.3 %all-to-all-start.1 = ((bf16[128,2,16,512]{3,2,1,0:T(8,128)(2,1)}), bf16[128,2,16,512]{3,2,1,0:T(8,128)(2,1)}, u32[]{:S(2)}, u32[]{:S(2)}) async-start(bf16[128,2,16,512]{3,2,1,0:T(8,128)(2,1)} %get-tuple-element.56), calls=%async_computation.1 | async-start | bytes 8388608 | tf_op jit(solution)/shard_map/all_to_all | solution.py:19
  35.2 0.1 fusion.28
  35.3 1.8 fusion.10
  37.1 50.8 %all-to-all-done.1.refs_4_ = bf16[128,2,16,512]{3,2,1,0:T(8,128)(2,1)} async-done(((bf16[128,2,16,512]{3,2,1,0:T(8,128)(2,1)}), bf16[128,2,16,512]{3,2,1,0:T(8,128)(2,1)}, u32[]{:S(2)}, u32[]{:S(2)}) %all-to-all-start.1) | async-done | bytes 4194336 | tf_op jit(solution)/shard_map/all_to_all | solution.py:19
  87.9 5.5 %all-to-all-start.2 = ((bf16[128,2,16,256]{3,2,1,0:T(8,128)(2,1)}), bf16[128,2,16,256]{3,2,1,0:T(8,128)(2,1)}, u32[]{:S(2)}, u32[]{:S(2)}) async-start(bf16[128,2,16,256]{3,2,1,0:T(8,128)(2,1)} %fusion.10), calls=%async_computation.2 | async-start | bytes 4194304 | tf_op jit(solution)/shard_map/all_to_all | solution.py:19
  93.4 0.0 copy-done.15
  93.4 0.1 fusion.31
  93.5 0.1 select_reduce_fusion
  93.7 0.1 subtract_select_fusion
  93.8 0.1 select_n.100.refs_1_.refs_0_
  93.9 0.0 copy-done
  93.9 0.0 copy-done.1
  93.9 22.6 %shard_map.84 = (bf16[2,192,512]{2,1,0:T(8,128)(2,1)S(1)}, bf16[2,192,512]{2,1,0:T(8,128)(2,1)S(1)}, bf16[128,2,16,512]{3,2,1,0:T(8,128)(2,1)}, bf16[4,2,16,512]{3,2,1,0:T(8,128)(2,1)S(1)}) custom-call(s32[1]{0:T(128)} %bitcast.refs_0_, s32[1,2048]{1,0:T(1,128)S(1)} %select_n.100.refs_1_.refs_0_, bf16[2,192,1280]{2,1,0:T(8,128)(2,1)S(1)} %copy-done, ...), custom_call_target="tpu_custom_call" | custom-call | tf_op jit(solution)/shard_map/pallas_call | solution.py:125
  116.5 7.1 %all-to-all-done.2.refs_3_ = bf16[128,2,16,256]{3,2,1,0:T(8,128)(2,1)} async-done(((bf16[128,2,16,256]{3,2,1,0:T(8,128)(2,1)}), bf16[128,2,16,256]{3,2,1,0:T(8,128)(2,1)}, u32[]{:S(2)}, u32[]{:S(2)}) %all-to-all-start.2) | async-done | bytes 2097184 | tf_op jit(solution)/shard_map/all_to_all | solution.py:19
  123.6 5.5 %all-to-all-start.3 = ((bf16[128,2,16,512]{3,2,1,0:T(8,128)(2,1)}), bf16[128,2,16,512]{3,2,1,0:T(8,128)(2,1)}, u32[]{:S(2)}, u32[]{:S(2)}) async-start(bf16[128,2,16,512]{3,2,1,0:T(8,128)(2,1)} %get-tuple-element.23), calls=%async_computation.3 | async-start | bytes 8388608 | tf_op jit(solution)/shard_map/all_to_all | solution.py:19
  129.2 11.3 %shard_map.85 = (bf16[2,192,256]{2,1,0:T(8,128)(2,1)S(1)}, bf16[2,192,256]{2,1,0:T(8,128)(2,1)S(1)}, bf16[128,2,16,256]{3,2,1,0:T(8,128)(2,1)S(1)}) custom-call(s32[1,2048]{1,0:T(1,128)S(1)} %select_n.100.refs_1_.refs_0_, bf16[2,192,1280]{2,1,0:T(8,128)(2,1)S(1)} %copy-done, bf16[2,192,1280]{2,1,0:T(8,128)(2,1)S(1)} %copy-done.1, ...), custom_call_target="tpu_custom_call" | custom-call | tf_op jit(solution)/shard_map/pallas_call | solution.py:125
  140.5 1.3 copy-done.2
  141.7 0.7 copy-done.3
  142.4 0.7 copy-done.5
  143.1 38.8 %all-to-all-done.3.refs_3_ = bf16[128,2,16,512]{3,2,1,0:T(8,128)(2,1)} async-done(((bf16[128,2,16,512]{3,2,1,0:T(8,128)(2,1)}), bf16[128,2,16,512]{3,2,1,0:T(8,128)(2,1)}, u32[]{:S(2)}, u32[]{:S(2)}) %all-to-all-start.3) | async-done | bytes 4194336 | tf_op jit(solution)/shard_map/all_to_all | solution.py:19
  181.9 5.5 %all-to-all-start.4 = ((bf16[128,2,16,256]{3,2,1,0:T(8,128)(2,1)}), bf16[128,2,16,256]{3,2,1,0:T(8,128)(2,1)}, u32[]{:S(2)}, u32[]{:S(2)}) async-start(bf16[128,2,16,256]{3,2,1,0:T(8,128)(2,1)} %copy-done.2), calls=%async_computation.4 | async-start | bytes 4194304 | tf_op jit(solution)/shard_map/all_to_all | solution.py:19
  187.3 21.7 %shard_map.86 = (bf16[2,192,512]{2,1,0:T(8,128)(2,1)S(1)}, bf16[2,192,512]{2,1,0:T(8,128)(2,1)S(1)}, bf16[128,2,16,512]{3,2,1,0:T(8,128)(2,1)}) custom-call(s32[1,2048]{1,0:T(1,128)S(1)} %select_n.100.refs_1_.refs_0_, bf16[2,192,1280]{2,1,0:T(8,128)(2,1)S(1)} %copy-done, bf16[2,192,1280]{2,1,0:T(8,128)(2,1)S(1)} %copy-done.1, ...), custom_call_target="tpu_custom_call" | custom-call | tf_op jit(solution)/shard_map/pallas_call | solution.py:125
  209.0 8.6 %all-to-all-done.4 = bf16[128,2,16,256]{3,2,1,0:T(8,128)(2,1)} async-done(((bf16[128,2,16,256]{3,2,1,0:T(8,128)(2,1)}), bf16[128,2,16,256]{3,2,1,0:T(8,128)(2,1)}, u32[]{:S(2)}, u32[]{:S(2)}) %all-to-all-start.4) | async-done | bytes 2097184 | tf_op jit(solution)/shard_map/all_to_all | solution.py:19
  217.6 5.5 %all-to-all-start.5 = ((bf16[128,2,16,512]{3,2,1,0:T(8,128)(2,1)}), bf16[128,2,16,512]{3,2,1,0:T(8,128)(2,1)}, u32[]{:S(2)}, u32[]{:S(2)}) async-start(bf16[128,2,16,512]{3,2,1,0:T(8,128)(2,1)} %get-tuple-element.33), calls=%async_computation.5 | async-start | bytes 8388608 | tf_op jit(solution)/shard_map/all_to_all | solution.py:19
  223.1 0.7 bitcast_convert_fusion.1
  223.8 2.9 %fusion.11 = f32[3,4,2,16,256]{4,0,3,2,1:T(4,128)S(1)} fusion(bf16[32,4,2,16,256]{4,3,2,1,0:T(8,128)(2,1)} %bitcast.36, s32[32]{0:T(128)S(1)} %select_reduce_fusion.1, pred[32]{0:T(512)(128)(4,1)S(1)} %get-tuple-element.40), kind=kOutput, calls=%fused_computation.18 | convolution fusion | flops 6291648 | bytes 2490528 | tf_op jit(solution)/shard_map/dot_general | solution.py:179
  226.7 4.7 %fusion.7 = f32[3,4,2,16,512]{4,0,3,2,1:T(4,128)S(1)} fusion(bf16[32,4,2,16,512]{4,3,2,1,0:T(8,128)(2,1)} %bitcast.34, pred[32]{0:T(512)(128)(4,1)S(1)} %iota_compare_fusion.2, s32[32]{0:T(128)S(1)} %select_reduce_fusion.1, pred[32]{0:T(512)(128)(4,1)S(1)} %get-tuple-element.40), kind=kOutput, calls=%fused_computation.12 | convolution fusion | flops 12583296 | bytes 4980928 | tf_op jit(solution)/shard_map/dot_general | solution.py:212
  231.4 42.0 %all_gather.3 = bf16[16,2,16,512]{3,2,1,0:T(8,128)(2,1)S(1)} all-gather(bf16[4,2,16,512]{3,2,1,0:T(8,128)(2,1)S(1)} %copy-done.8), channel_id=1, replica_groups=mesh['ctx'=32,'mp'=4] {'mp'}, dimensions={0}, use_global_device_ids=true | all-gather | bytes 655360 | tf_op jit(solution)/shard_map/all_gather | solution.py:219
  273.5 0.3 multiply_add_fusion
  273.9 1.4 pad_maximum_fusion
  275.3 0.6 all-to-all-done.5
  275.8 0.0 copy-done.12
  275.8 4.6 %fusion = (f32[4,2,16,512]{3,2,1,0:T(8,128)S(1)}, f32[4,2,16,512]{3,2,1,0:T(8,128)S(1)}, f32[4,2,16,512]{3,2,1,0:T(8,128)S(1)}) fusion(bf16[32,4,2,16,512]{4,3,2,1,0:T(8,128)(2,1)} %bitcast.41, pred[32]{0:T(512)(128)(4,1)S(1)} %copy-done.12, pred[32]{0:T(512)(128)(4,1)S(1)} %copy-done.14, pred[32]{0:T(512)(128)(4,1)S(1)} %copy-done.10), kind=kLoop, calls=%fused_computation.3 | loop fusion | flops 14483456 | bytes 4980832 | tf_op jit(solution)/shard_map/reduce_sum | solution.py:231
  280.4 0.2 stack.24
  280.6 0.2 stack.25
  280.8 0.2 stack.26
  281.0 1.2 maximum_bitcast_fusion
  282.1 0.5 fusion.47
  282.6 0.6 copy.119
  283.2 1.1 copy.126
  284.4 0.6 copy.120
  285.0 1.1 copy.127
  (36 shorter events, 0.3 us)
Async XLA Ops:
  1.9 21.1 %all-to-all-start = ((s32[128,1,96]{2,1,0:T(1,128)}), s32[128,1,96]{2,1,0:T(1,128)S(1)}, u32[]{:S(2)}, u32[]{:S(2)}) async-start(s32[128,1,96]{2,1,0:T(1,128)} %broadcast_in_dim.218), calls=%async_computation | async-start | bytes 131072 | tf_op jit(solution)/shard_map/all_to_all | solution.py:19
  24.2 0.6 copy-start.9
  24.2 0.8 copy-start.13
  24.2 1.0 copy-start.11
  29.9 58.0 %all-to-all-start.1 = ((bf16[128,2,16,512]{3,2,1,0:T(8,128)(2,1)}), bf16[128,2,16,512]{3,2,1,0:T(8,128)(2,1)}, u32[]{:S(2)}, u32[]{:S(2)}) async-start(bf16[128,2,16,512]{3,2,1,0:T(8,128)(2,1)} %get-tuple-element.56), calls=%async_computation.1 | async-start | bytes 8388608 | tf_op jit(solution)/shard_map/all_to_all | solution.py:19
  37.1 56.3 %copy-start.15 = (s32[1,96]{1,0:T(1,128)S(1)}, s32[1,96]{1,0:T(1,128)}, u32[]{:S(2)}) copy-start(s32[1,96]{1,0:T(1,128)} %param.9) | copy-start | bytes 1156
  37.1 56.8 %copy-start = (bf16[2,192,1280]{2,1,0:T(8,128)(2,1)S(1)}, bf16[2,192,1280]{2,1,0:T(8,128)(2,1)}, u32[]{:S(2)}) copy-start(bf16[2,192,1280]{2,1,0:T(8,128)(2,1)} %refs_1_.3) | copy-start | bytes 2949124
  37.1 56.8 %copy-start.1 = (bf16[2,192,1280]{2,1,0:T(8,128)(2,1)S(1)}, bf16[2,192,1280]{2,1,0:T(8,128)(2,1)}, u32[]{:S(2)}) copy-start(bf16[2,192,1280]{2,1,0:T(8,128)(2,1)} %refs_2_.5) | copy-start | bytes 2949124
  87.9 35.7 %all-to-all-start.2 = ((bf16[128,2,16,256]{3,2,1,0:T(8,128)(2,1)}), bf16[128,2,16,256]{3,2,1,0:T(8,128)(2,1)}, u32[]{:S(2)}, u32[]{:S(2)}) async-start(bf16[128,2,16,256]{3,2,1,0:T(8,128)(2,1)} %fusion.10), calls=%async_computation.2 | async-start | bytes 4194304 | tf_op jit(solution)/shard_map/all_to_all | solution.py:19
  116.5 7.1 %copy-start.7 = (bf16[4,2,16,512]{3,2,1,0:T(8,128)(2,1)}, bf16[4,2,16,512]{3,2,1,0:T(8,128)(2,1)S(1)}, u32[]{:S(2)}) copy-start(bf16[4,2,16,512]{3,2,1,0:T(8,128)(2,1)S(1)} %get-tuple-element.31) | copy-start | bytes 393220
  123.6 58.2 %all-to-all-start.3 = ((bf16[128,2,16,512]{3,2,1,0:T(8,128)(2,1)}), bf16[128,2,16,512]{3,2,1,0:T(8,128)(2,1)}, u32[]{:S(2)}, u32[]{:S(2)}) async-start(bf16[128,2,16,512]{3,2,1,0:T(8,128)(2,1)} %get-tuple-element.23), calls=%async_computation.3 | async-start | bytes 8388608 | tf_op jit(solution)/shard_map/all_to_all | solution.py:19
  140.4 1.3 copy-start.2
  141.7 0.7 copy-start.3
  142.4 0.7 copy-start.5
  181.9 35.7 %all-to-all-start.4 = ((bf16[128,2,16,256]{3,2,1,0:T(8,128)(2,1)}), bf16[128,2,16,256]{3,2,1,0:T(8,128)(2,1)}, u32[]{:S(2)}, u32[]{:S(2)}) async-start(bf16[128,2,16,256]{3,2,1,0:T(8,128)(2,1)} %copy-done.2), calls=%async_computation.4 | async-start | bytes 4194304 | tf_op jit(solution)/shard_map/all_to_all | solution.py:19
  217.6 58.2 %all-to-all-start.5 = ((bf16[128,2,16,512]{3,2,1,0:T(8,128)(2,1)}), bf16[128,2,16,512]{3,2,1,0:T(8,128)(2,1)}, u32[]{:S(2)}, u32[]{:S(2)}) async-start(bf16[128,2,16,512]{3,2,1,0:T(8,128)(2,1)} %get-tuple-element.33), calls=%async_computation.5 | async-start | bytes 8388608 | tf_op jit(solution)/shard_map/all_to_all | solution.py:19
  226.7 4.7 %copy-start.8 = (bf16[4,2,16,512]{3,2,1,0:T(8,128)(2,1)S(1)}, bf16[4,2,16,512]{3,2,1,0:T(8,128)(2,1)}, u32[]{:S(2)}) copy-start(bf16[4,2,16,512]{3,2,1,0:T(8,128)(2,1)} %copy-done.7) | copy-start | bytes 393220
  231.4 42.5 %copy-start.4 = (bf16[2,192,256]{2,1,0:T(8,128)(2,1)S(1)}, bf16[2,192,256]{2,1,0:T(8,128)(2,1)}, u32[]{:S(2)}) copy-start(bf16[2,192,256]{2,1,0:T(8,128)(2,1)} %copy-done.3) | copy-start | bytes 589828
  231.4 42.5 %copy-start.6 = (bf16[2,192,256]{2,1,0:T(8,128)(2,1)S(1)}, bf16[2,192,256]{2,1,0:T(8,128)(2,1)}, u32[]{:S(2)}) copy-start(bf16[2,192,256]{2,1,0:T(8,128)(2,1)} %copy-done.5) | copy-start | bytes 589828
  273.5 2.4 copy-start.10
  273.5 2.4 copy-start.12
  273.5 2.3 copy-start.14

commit v11 on v9

--- a/solution.py
+++ b/solution.py
@@ -226,8 +226,10 @@
         kpos_rel, queries, douts, kv_last, factor, offsets[2]
     )
     back_last = exchange(grads_last)
-    summed = jnp.concatenate([first_sum, middle_sum, absorb(back_last)], axis=-1)
-    summed = summed.transpose(2, 0, 3, 1, 4).reshape(2, kv_rows, full_width)
+    early = [part.transpose(2, 0, 3, 1, 4) for part in (first_sum, middle_sum)]
+    early = lax.optimization_barrier(early)
+    late = absorb(back_last).transpose(2, 0, 3, 1, 4)
+    summed = jnp.concatenate(early + [late], axis=-1).reshape(2, kv_rows, full_width)
     attended = jnp.concatenate([out_first, out_middle, out_last], axis=-1)
     d_query = jnp.concatenate([dq_first, dq_middle, dq_last], axis=-1)
     return (attended, d_query, summed[0], summed[1])

time: 286 us -> 286 us (level)
  no operation moved by 1% of the time
where the time goes in v11:
time: 286 us; the launch traced here: 285 us
  waiting for transfers between devices  112 us (39%)
  Pallas kernels  55.6 us (19%)
  blocking collectives  42 us (15%)
  starting transfers between devices  38.8 us (14%)
  matrix products  12.2 us (4%)
  local copies, waits for them, and re-layouts  11.9 us (4%)
  other arithmetic  11.4 us (4%)
    all_to_all x6, waiting for transfers between devices, exchange(): lax.all_to_all(operand, ('ctx', 'mp'), split_axis=0, concat_axis=0, tiled...  112 us
    pallas_call x3, Pallas kernels, attend(): pl.pallas_call(kernel, grid=(head_count, layer_count), in_specs=in_specs,...  55.6 us
    all_gather x1, blocking collectives, on_device(): gathered = lax.all_gather(own_grads, 'mp', axis=0, tiled=True)  42 us
    all_to_all x6, starting transfers between devices, exchange(): lax.all_to_all(operand, ('ctx', 'mp'), split_axis=0, concat_axis=0, tiled...  38.8 us
    dot_general x2, matrix products, absorb(): lax.dot_general(picker_low, block_grid, (((0,), (0,)), ((), ())), preferr...  7.53 us
    select_n x2, other arithmetic, outgoing(): picked = jnp.where(hit, chunk_grid[block_id][None], picked)  6.3 us
  transfers between devices with their start and end apart: 6, of which 6 were waited for; matrix products, arithmetic and copies ran while one was open for 6% of the time, Pallas kernels for 20%

profile of v11, /device:TPU:1, one launch (start us, length us, event | category | flops | bytes accessed | tf_op | source)
XLA Modules:
  0.0 284.5 jit_solution(4406503826654029180)
XLA Ops:
  0.6 1.3 broadcast_in_dim.194
  1.9 11.5 %all-to-all-start = ((s32[128,1,96]{2,1,0:T(1,128)}), s32[128,1,96]{2,1,0:T(1,128)S(1)}, u32[]{:S(2)}, u32[]{:S(2)}) async-start(s32[128,1,96]{2,1,0:T(1,128)} %broadcast_in_dim.194), calls=%async_computation | async-start | bytes 131072 | tf_op jit(solution)/shard_map/all_to_all | solution.py:19
  13.4 1.4 reshape.198
  14.8 1.4 reshape.199
  16.2 0.6 fusion.23
  17.1 5.9 %all-to-all-done = s32[128,1,96]{2,1,0:T(1,128)S(1)} async-done(((s32[128,1,96]{2,1,0:T(1,128)}), s32[128,1,96]{2,1,0:T(1,128)S(1)}, u32[]{:S(2)}, u32[]{:S(2)}) %all-to-all-start) | async-done | bytes 49184 | tf_op jit(solution)/shard_map/all_to_all | solution.py:19
  23.0 0.1 fusion.50
  23.2 0.1 select_reduce_fusion.1
  23.3 0.7 fusion.49
  24.0 0.2 slice_reduce_fusion.2
  24.2 0.1 broadcast_in_dim.196
  24.2 0.1 broadcast_in_dim.197
  24.4 0.1 broadcast_in_dim.203
  24.4 0.1 broadcast_in_dim.204
  24.6 0.1 broadcast_in_dim.210
  24.6 0.1 broadcast_in_dim.211
  24.8 4.5 %fusion.1 = (bf16[128,2,16,512]{3,2,1,0:T(8,128)(2,1)}, bf16[128,2,16,512]{3,2,1,0:T(8,128)(2,1)}) fusion(pred[128]{0:T(512)(128)(4,1)S(1)} %broadcast_in_dim.211, pred[128]{0:T(512)(128)(4,1)S(1)} %broadcast_in_dim.204, pred[128]{0:T(512)(128)(4,1)S(1)} %broadcast_in_dim.197, bf16[4,2,16,512]{3,2,1,0:T(8,128)(2,1)S(1)} %copy.120, ...), kind=kLoop, calls=%fused_computation.2 | loop fusion | flops 12582912 | bytes 9175424 | tf_op jit(solution)/shard_map/jit(_where)/select_n | solution.py:174
  29.3 5.3 %all-to-all-start.1 = ((bf16[128,2,16,512]{3,2,1,0:T(8,128)(2,1)}), bf16[128,2,16,512]{3,2,1,0:T(8,128)(2,1)}, u32[]{:S(2)}, u32[]{:S(2)}) async-start(bf16[128,2,16,512]{3,2,1,0:T(8,128)(2,1)} %get-tuple-element.57), calls=%async_computation.1 | async-start | bytes 8388608 | tf_op jit(solution)/shard_map/all_to_all | solution.py:19
  34.6 0.1 fusion.30
  34.8 1.8 fusion.9
  36.5 0.0 copy-start.9
  36.5 0.0 copy-start
  36.5 0.0 copy-start.1
  36.5 50.8 %all-to-all-done.1.refs_4_ = bf16[128,2,16,512]{3,2,1,0:T(8,128)(2,1)} async-done(((bf16[128,2,16,512]{3,2,1,0:T(8,128)(2,1)}), bf16[128,2,16,512]{3,2,1,0:T(8,128)(2,1)}, u32[]{:S(2)}, u32[]{:S(2)}) %all-to-all-start.1) | async-done | bytes 4194336 | tf_op jit(solution)/shard_map/all_to_all | solution.py:19
  87.3 5.5 %all-to-all-start.2 = ((bf16[128,2,16,256]{3,2,1,0:T(8,128)(2,1)}), bf16[128,2,16,256]{3,2,1,0:T(8,128)(2,1)}, u32[]{:S(2)}, u32[]{:S(2)}) async-start(bf16[128,2,16,256]{3,2,1,0:T(8,128)(2,1)} %fusion.9), calls=%async_computation.2 | async-start | bytes 4194304 | tf_op jit(solution)/shard_map/all_to_all | solution.py:19
  92.8 0.0 copy-done.9
  92.8 0.1 fusion.33
  93.0 0.1 select_reduce_fusion
  93.1 0.1 subtract_select_fusion
  93.2 0.1 select_n.90.refs_1_.refs_0_
  93.3 0.0 copy-done
  93.3 0.0 copy-done.1
  93.3 22.6 %shard_map.84 = (bf16[2,192,512]{2,1,0:T(8,128)(2,1)S(1)}, bf16[2,192,512]{2,1,0:T(8,128)(2,1)S(1)}, bf16[128,2,16,512]{3,2,1,0:T(8,128)(2,1)}, bf16[4,2,16,512]{3,2,1,0:T(8,128)(2,1)S(1)}) custom-call(s32[1]{0:T(128)} %bitcast.refs_0_, s32[1,2048]{1,0:T(1,128)S(1)} %select_n.90.refs_1_.refs_0_, bf16[2,192,1280]{2,1,0:T(8,128)(2,1)S(1)} %copy-done, ...), custom_call_target="tpu_custom_call" | custom-call | tf_op jit(solution)/shard_map/pallas_call | solution.py:125
  115.9 0.0 copy-start.7
  115.9 7.1 %all-to-all-done.2.refs_3_ = bf16[128,2,16,256]{3,2,1,0:T(8,128)(2,1)} async-done(((bf16[128,2,16,256]{3,2,1,0:T(8,128)(2,1)}), bf16[128,2,16,256]{3,2,1,0:T(8,128)(2,1)}, u32[]{:S(2)}, u32[]{:S(2)}) %all-to-all-start.2) | async-done | bytes 2097184 | tf_op jit(solution)/shard_map/all_to_all | solution.py:19
  123.0 0.0 copy-done.7
  123.0 5.5 %all-to-all-start.3 = ((bf16[128,2,16,512]{3,2,1,0:T(8,128)(2,1)}), bf16[128,2,16,512]{3,2,1,0:T(8,128)(2,1)}, u32[]{:S(2)}, u32[]{:S(2)}) async-start(bf16[128,2,16,512]{3,2,1,0:T(8,128)(2,1)} %get-tuple-element.25), calls=%async_computation.3 | async-start | bytes 8388608 | tf_op jit(solution)/shard_map/all_to_all | solution.py:19
  128.6 11.3 %shard_map.85 = (bf16[2,192,256]{2,1,0:T(8,128)(2,1)S(1)}, bf16[2,192,256]{2,1,0:T(8,128)(2,1)S(1)}, bf16[128,2,16,256]{3,2,1,0:T(8,128)(2,1)S(1)}) custom-call(s32[1,2048]{1,0:T(1,128)S(1)} %select_n.90.refs_1_.refs_0_, bf16[2,192,1280]{2,1,0:T(8,128)(2,1)S(1)} %copy-done, bf16[2,192,1280]{2,1,0:T(8,128)(2,1)S(1)} %copy-done.1, ...), custom_call_target="tpu_custom_call" | custom-call | tf_op jit(solution)/shard_map/pallas_call | solution.py:125
  139.9 0.0 copy-start.2
  139.9 1.4 copy-done.2
  141.2 0.7 copy-done.3
  141.9 0.7 copy-done.5
  142.6 38.7 %all-to-all-done.3.refs_3_ = bf16[128,2,16,512]{3,2,1,0:T(8,128)(2,1)} async-done(((bf16[128,2,16,512]{3,2,1,0:T(8,128)(2,1)}), bf16[128,2,16,512]{3,2,1,0:T(8,128)(2,1)}, u32[]{:S(2)}, u32[]{:S(2)}) %all-to-all-start.3) | async-done | bytes 4194336 | tf_op jit(solution)/shard_map/all_to_all | solution.py:19
  181.3 5.5 %all-to-all-start.4 = ((bf16[128,2,16,256]{3,2,1,0:T(8,128)(2,1)}), bf16[128,2,16,256]{3,2,1,0:T(8,128)(2,1)}, u32[]{:S(2)}, u32[]{:S(2)}) async-start(bf16[128,2,16,256]{3,2,1,0:T(8,128)(2,1)} %copy-done.2), calls=%async_computation.4 | async-start | bytes 4194304 | tf_op jit(solution)/shard_map/all_to_all | solution.py:19
  186.8 21.7 %shard_map.86 = (bf16[2,192,512]{2,1,0:T(8,128)(2,1)S(1)}, bf16[2,192,512]{2,1,0:T(8,128)(2,1)S(1)}, bf16[128,2,16,512]{3,2,1,0:T(8,128)(2,1)}) custom-call(s32[1,2048]{1,0:T(1,128)S(1)} %select_n.90.refs_1_.refs_0_, bf16[2,192,1280]{2,1,0:T(8,128)(2,1)S(1)} %copy-done, bf16[2,192,1280]{2,1,0:T(8,128)(2,1)S(1)} %copy-done.1, ...), custom_call_target="tpu_custom_call" | custom-call | tf_op jit(solution)/shard_map/pallas_call | solution.py:125
  208.4 8.6 %all-to-all-done.4 = bf16[128,2,16,256]{3,2,1,0:T(8,128)(2,1)} async-done(((bf16[128,2,16,256]{3,2,1,0:T(8,128)(2,1)}), bf16[128,2,16,256]{3,2,1,0:T(8,128)(2,1)}, u32[]{:S(2)}, u32[]{:S(2)}) %all-to-all-start.4) | async-done | bytes 2097184 | tf_op jit(solution)/shard_map/all_to_all | solution.py:19
  217.0 5.5 %all-to-all-start.5 = ((bf16[128,2,16,512]{3,2,1,0:T(8,128)(2,1)}), bf16[128,2,16,512]{3,2,1,0:T(8,128)(2,1)}, u32[]{:S(2)}, u32[]{:S(2)}) async-start(bf16[128,2,16,512]{3,2,1,0:T(8,128)(2,1)} %get-tuple-element.37), calls=%async_computation.5 | async-start | bytes 8388608 | tf_op jit(solution)/shard_map/all_to_all | solution.py:19
  222.5 0.7 bitcast_convert_fusion.1
  223.2 2.9 %fusion.10 = f32[3,4,2,16,256]{4,0,3,2,1:T(4,128)S(1)} fusion(bf16[32,4,2,16,256]{4,3,2,1,0:T(8,128)(2,1)} %bitcast.36, s32[32]{0:T(128)S(1)} %select_reduce_fusion.1, pred[32]{0:T(512)(128)(4,1)S(1)} %get-tuple-element.41), kind=kOutput, calls=%fused_computation.14 | convolution fusion | flops 6291648 | bytes 2490528 | tf_op jit(solution)/shard_map/dot_general | solution.py:179
  226.1 4.7 %fusion.6 = f32[3,4,2,16,512]{4,0,3,2,1:T(4,128)S(1)} fusion(bf16[32,4,2,16,512]{4,3,2,1,0:T(8,128)(2,1)} %bitcast.34, pred[32]{0:T(512)(128)(4,1)S(1)} %iota_compare_fusion.2, s32[32]{0:T(128)S(1)} %select_reduce_fusion.1, pred[32]{0:T(512)(128)(4,1)S(1)} %get-tuple-element.41), kind=kOutput, calls=%fused_computation.8 | convolution fusion | flops 12583296 | bytes 4980928 | tf_op jit(solution)/shard_map/dot_general | solution.py:212
  230.8 0.0 copy-done.8
  230.8 42.0 %all_gather.3 = bf16[16,2,16,512]{3,2,1,0:T(8,128)(2,1)S(1)} all-gather(bf16[4,2,16,512]{3,2,1,0:T(8,128)(2,1)S(1)} %copy-done.8), channel_id=1, replica_groups=mesh['ctx'=32,'mp'=4] {'mp'}, dimensions={0}, use_global_device_ids=true | all-gather | bytes 655360 | tf_op jit(solution)/shard_map/all_gather | solution.py:219
  272.9 0.3 add_bitcast_fusion
  273.2 0.0 copy-done.4
  273.2 0.0 copy-done.6
  273.3 1.4 pad_maximum_fusion.1
  274.6 0.6 all-to-all-done.5
  275.2 4.6 %fusion.12 = f32[2,3,16,4,512]{4,1,2,0,3:T(4,128)S(1)} fusion(bf16[32,4,2,16,512]{4,3,2,1,0:T(8,128)(2,1)} %bitcast.43, s32[32]{0:T(128)S(1)} %select_reduce_fusion.1, pred[32]{0:T(512)(128)(4,1)S(1)} %get-tuple-element.41), kind=kOutput, calls=%fused_computation.16 | convolution fusion | flops 12583104 | bytes 4980896 | tf_op jit(solution)/shard_map/dot_general | solution.py:179
  279.9 0.7 pad_maximum_fusion
  280.6 0.5 fusion.51
  281.0 0.6 copy.131
  281.7 1.1 copy.140
  282.8 0.6 copy.132
  283.4 1.1 copy.141
  (21 shorter events, 0.3 us)
Async XLA Ops:
  1.9 21.1 %all-to-all-start = ((s32[128,1,96]{2,1,0:T(1,128)}), s32[128,1,96]{2,1,0:T(1,128)S(1)}, u32[]{:S(2)}, u32[]{:S(2)}) async-start(s32[128,1,96]{2,1,0:T(1,128)} %broadcast_in_dim.194), calls=%async_computation | async-start | bytes 131072 | tf_op jit(solution)/shard_map/all_to_all | solution.py:19
  29.3 58.0 %all-to-all-start.1 = ((bf16[128,2,16,512]{3,2,1,0:T(8,128)(2,1)}), bf16[128,2,16,512]{3,2,1,0:T(8,128)(2,1)}, u32[]{:S(2)}, u32[]{:S(2)}) async-start(bf16[128,2,16,512]{3,2,1,0:T(8,128)(2,1)} %get-tuple-element.57), calls=%async_computation.1 | async-start | bytes 8388608 | tf_op jit(solution)/shard_map/all_to_all | solution.py:19
  36.5 56.3 %copy-start.9 = (s32[1,96]{1,0:T(1,128)S(1)}, s32[1,96]{1,0:T(1,128)}, u32[]{:S(2)}) copy-start(s32[1,96]{1,0:T(1,128)} %param.9) | copy-start | bytes 1156
  36.5 56.8 %copy-start = (bf16[2,192,1280]{2,1,0:T(8,128)(2,1)S(1)}, bf16[2,192,1280]{2,1,0:T(8,128)(2,1)}, u32[]{:S(2)}) copy-start(bf16[2,192,1280]{2,1,0:T(8,128)(2,1)} %refs_1_.3) | copy-start | bytes 2949124
  36.5 56.8 %copy-start.1 = (bf16[2,192,1280]{2,1,0:T(8,128)(2,1)S(1)}, bf16[2,192,1280]{2,1,0:T(8,128)(2,1)}, u32[]{:S(2)}) copy-start(bf16[2,192,1280]{2,1,0:T(8,128)(2,1)} %refs_2_.5) | copy-start | bytes 2949124
  87.3 35.7 %all-to-all-start.2 = ((bf16[128,2,16,256]{3,2,1,0:T(8,128)(2,1)}), bf16[128,2,16,256]{3,2,1,0:T(8,128)(2,1)}, u32[]{:S(2)}, u32[]{:S(2)}) async-start(bf16[128,2,16,256]{3,2,1,0:T(8,128)(2,1)} %fusion.9), calls=%async_computation.2 | async-start | bytes 4194304 | tf_op jit(solution)/shard_map/all_to_all | solution.py:19
  115.9 7.1 %copy-start.7 = (bf16[4,2,16,512]{3,2,1,0:T(8,128)(2,1)}, bf16[4,2,16,512]{3,2,1,0:T(8,128)(2,1)S(1)}, u32[]{:S(2)}) copy-start(bf16[4,2,16,512]{3,2,1,0:T(8,128)(2,1)S(1)} %get-tuple-element.33) | copy-start | bytes 393220
  123.0 58.2 %all-to-all-start.3 = ((bf16[128,2,16,512]{3,2,1,0:T(8,128)(2,1)}), bf16[128,2,16,512]{3,2,1,0:T(8,128)(2,1)}, u32[]{:S(2)}, u32[]{:S(2)}) async-start(bf16[128,2,16,512]{3,2,1,0:T(8,128)(2,1)} %get-tuple-element.25), calls=%async_computation.3 | async-start | bytes 8388608 | tf_op jit(solution)/shard_map/all_to_all | solution.py:19
  139.9 1.4 copy-start.2
  141.2 0.7 copy-start.3
  141.9 0.7 copy-start.5
  181.3 35.7 %all-to-all-start.4 = ((bf16[128,2,16,256]{3,2,1,0:T(8,128)(2,1)}), bf16[128,2,16,256]{3,2,1,0:T(8,128)(2,1)}, u32[]{:S(2)}, u32[]{:S(2)}) async-start(bf16[128,2,16,256]{3,2,1,0:T(8,128)(2,1)} %copy-done.2), calls=%async_computation.4 | async-start | bytes 4194304 | tf_op jit(solution)/shard_map/all_to_all | solution.py:19
  217.0 58.2 %all-to-all-start.5 = ((bf16[128,2,16,512]{3,2,1,0:T(8,128)(2,1)}), bf16[128,2,16,512]{3,2,1,0:T(8,128)(2,1)}, u32[]{:S(2)}, u32[]{:S(2)}) async-start(bf16[128,2,16,512]{3,2,1,0:T(8,128)(2,1)} %get-tuple-element.37), calls=%async_computation.5 | async-start | bytes 8388608 | tf_op jit(solution)/shard_map/all_to_all | solution.py:19
  226.1 4.7 %copy-start.8 = (bf16[4,2,16,512]{3,2,1,0:T(8,128)(2,1)S(1)}, bf16[4,2,16,512]{3,2,1,0:T(8,128)(2,1)}, u32[]{:S(2)}) copy-start(bf16[4,2,16,512]{3,2,1,0:T(8,128)(2,1)} %copy-done.7) | copy-start | bytes 393220
  230.8 42.4 %copy-start.4 = (bf16[2,192,256]{2,1,0:T(8,128)(2,1)S(1)}, bf16[2,192,256]{2,1,0:T(8,128)(2,1)}, u32[]{:S(2)}) copy-start(bf16[2,192,256]{2,1,0:T(8,128)(2,1)} %copy-done.3) | copy-start | bytes 589828
  230.8 42.4 %copy-start.6 = (bf16[2,192,256]{2,1,0:T(8,128)(2,1)S(1)}, bf16[2,192,256]{2,1,0:T(8,128)(2,1)}, u32[]{:S(2)}) copy-start(bf16[2,192,256]{2,1,0:T(8,128)(2,1)} %copy-done.5) | copy-start | bytes 589828

commit v12 on v9

--- a/solution.py
+++ b/solution.py
@@ -150,8 +150,8 @@
     my_stretch = lax.axis_index("ctx")
     my_mp = lax.axis_index("mp")
     factor = 1.0 / math.sqrt(HD)
-    spread = jnp.broadcast_to(reads, (owner_count, reads.shape[1]))
-    all_lists = exchange(spread).reshape(ctx_count, mp_count, -1)[:, 0, :]
+    spread = jnp.broadcast_to(reads, (ctx_count, reads.shape[1]))
+    all_lists = lax.all_to_all(spread, "ctx", split_axis=0, concat_axis=0, tiled=True)
     owner_hit = (all_lists >= 0) & (all_lists // per_owner == my_owner)
     chosen = jnp.sum(jnp.where(owner_hit, all_lists - my_owner * per_owner, 0), axis=1)
     wanted = jnp.any(owner_hit, axis=1)

time: 286 us -> 286 us (level)
    all_to_all x0 -> x1, starting transfers between devices: none -> 11.3 us  [on_device(): lax.all_to_all(spread, 'ctx', split_axis=0, concat_axis=0, tiled=True)]
    all_to_all x6 -> x5, starting transfers between devices: 38.8 us -> 28.7 us  [exchange(): lax.all_to_all(operand, ('ctx', 'mp'), split_axis=0, concat_axis=0, tiled...]
    all_to_all x6 -> x5, waiting for transfers between devices: 112 us -> 106 us  [exchange(): lax.all_to_all(operand, ('ctx', 'mp'), split_axis=0, concat_axis=0, tiled...]
    all_to_all x0 -> x1, waiting for transfers between devices: none -> 4.93 us  [on_device(): lax.all_to_all(spread, 'ctx', split_axis=0, concat_axis=0, tiled=True)]
where the time goes in v12:
time: 286 us; the launch traced here: 285 us
  waiting for transfers between devices  111 us (39%)
  Pallas kernels  55.6 us (19%)
  blocking collectives  42 us (15%)
  starting transfers between devices  40 us (14%)
  matrix products  12.2 us (4%)
  local copies, waits for them, and re-layouts  11.8 us (4%)
  other arithmetic  11.4 us (4%)
    all_to_all x5, waiting for transfers between devices, exchange(): lax.all_to_all(operand, ('ctx', 'mp'), split_axis=0, concat_axis=0, tiled...  106 us
    pallas_call x3, Pallas kernels, attend(): pl.pallas_call(kernel, grid=(head_count, layer_count), in_specs=in_specs,...  55.6 us
    all_gather x1, blocking collectives, on_device(): gathered = lax.all_gather(own_grads, 'mp', axis=0, tiled=True)  42 us
    all_to_all x5, starting transfers between devices, exchange(): lax.all_to_all(operand, ('ctx', 'mp'), split_axis=0, concat_axis=0, tiled...  28.7 us
    all_to_all x1, starting transfers between devices, on_device(): lax.all_to_all(spread, 'ctx', split_axis=0, concat_axis=0, tiled=True)  11.3 us
    dot_general x2, matrix products, absorb(): lax.dot_general(picker_low, block_grid, (((0,), (0,)), ((), ())), preferr...  7.53 us
    select_n x2, other arithmetic, outgoing(): picked = jnp.where(hit, chunk_grid[block_id][None], picked)  6.31 us
  transfers between devices with their start and end apart: 6, of which 6 were waited for; matrix products, arithmetic and copies ran while one was open for 6% of the time, Pallas kernels for 20%

profile of v12, /device:TPU:1, one launch (start us, length us, event | category | flops | bytes accessed | tf_op | source)
XLA Modules:
  0.0 284.7 jit_solution(4135639252795088496)
XLA Ops:
  0.6 1.3 broadcast_in_dim.194
  1.9 11.3 %all-to-all-start = ((s32[32,1,96]{2,1,0:T(1,128)}), s32[32,1,96]{2,1,0:T(1,128)S(1)}, u32[]{:S(2)}, u32[]{:S(2)}) async-start(s32[32,1,96]{2,1,0:T(1,128)} %broadcast_in_dim.194), calls=%async_computation | async-start | bytes 32768 | tf_op jit(solution)/shard_map/all_to_all | solution.py:154
  13.2 1.4 reshape.193
  14.6 1.4 reshape.194
  16.0 0.6 fusion.20
  16.9 4.9 %all-to-all-done = s32[32,1,96]{2,1,0:T(1,128)S(1)} async-done(((s32[32,1,96]{2,1,0:T(1,128)}), s32[32,1,96]{2,1,0:T(1,128)S(1)}, u32[]{:S(2)}, u32[]{:S(2)}) %all-to-all-start) | async-done | bytes 12320 | tf_op jit(solution)/shard_map/all_to_all | solution.py:154
  21.8 0.1 fusion.47
  21.9 0.1 select_reduce_fusion.1
  22.0 0.7 fusion.46
  22.7 0.2 slice_reduce_fusion.2
  22.9 0.1 broadcast_in_dim.196
  23.0 0.1 broadcast_in_dim.197
  23.1 0.1 broadcast_in_dim.203
  23.2 0.1 broadcast_in_dim.204
  23.3 0.1 broadcast_in_dim.210
  23.4 0.1 broadcast_in_dim.211
  23.5 4.5 %fusion.1 = (bf16[128,2,16,512]{3,2,1,0:T(8,128)(2,1)}, bf16[128,2,16,512]{3,2,1,0:T(8,128)(2,1)}) fusion(pred[128]{0:T(512)(128)(4,1)S(1)} %broadcast_in_dim.211, pred[128]{0:T(512)(128)(4,1)S(1)} %broadcast_in_dim.204, pred[128]{0:T(512)(128)(4,1)S(1)} %broadcast_in_dim.197, bf16[4,2,16,512]{3,2,1,0:T(8,128)(2,1)S(1)} %copy.98, ...), kind=kLoop, calls=%fused_computation.2 | loop fusion | flops 12582912 | bytes 9175424 | tf_op jit(solution)/shard_map/jit(_where)/select_n | solution.py:174
  28.1 6.7 %all-to-all-start.1 = ((bf16[128,2,16,512]{3,2,1,0:T(8,128)(2,1)}), bf16[128,2,16,512]{3,2,1,0:T(8,128)(2,1)}, u32[]{:S(2)}, u32[]{:S(2)}) async-start(bf16[128,2,16,512]{3,2,1,0:T(8,128)(2,1)} %get-tuple-element.51), calls=%async_computation.1 | async-start | bytes 8388608 | tf_op jit(solution)/shard_map/all_to_all | solution.py:19
  34.7 0.1 fusion.27
  34.9 1.8 fusion.9
  36.7 0.0 copy-start.9
  36.7 0.0 copy-start
  36.7 0.0 copy-start.1
  36.7 50.8 %all-to-all-done.1.refs_4_ = bf16[128,2,16,512]{3,2,1,0:T(8,128)(2,1)} async-done(((bf16[128,2,16,512]{3,2,1,0:T(8,128)(2,1)}), bf16[128,2,16,512]{3,2,1,0:T(8,128)(2,1)}, u32[]{:S(2)}, u32[]{:S(2)}) %all-to-all-start.1) | async-done | bytes 4194336 | tf_op jit(solution)/shard_map/all_to_all | solution.py:19
  87.4 5.5 %all-to-all-start.2 = ((bf16[128,2,16,256]{3,2,1,0:T(8,128)(2,1)}), bf16[128,2,16,256]{3,2,1,0:T(8,128)(2,1)}, u32[]{:S(2)}, u32[]{:S(2)}) async-start(bf16[128,2,16,256]{3,2,1,0:T(8,128)(2,1)} %fusion.9), calls=%async_computation.2 | async-start | bytes 4194304 | tf_op jit(solution)/shard_map/all_to_all | solution.py:19
  92.9 0.0 copy-done.9
  93.0 0.1 fusion.30
  93.1 0.1 select_reduce_fusion
  93.2 0.1 subtract_select_fusion
  93.3 0.1 select_n.90.refs_1_.refs_0_
  93.4 0.0 copy-done
  93.4 0.0 copy-done.1
  93.4 22.6 %shard_map.84 = (bf16[2,192,512]{2,1,0:T(8,128)(2,1)S(1)}, bf16[2,192,512]{2,1,0:T(8,128)(2,1)S(1)}, bf16[128,2,16,512]{3,2,1,0:T(8,128)(2,1)}, bf16[4,2,16,512]{3,2,1,0:T(8,128)(2,1)S(1)}) custom-call(s32[1]{0:T(128)} %bitcast.refs_0_, s32[1,2048]{1,0:T(1,128)S(1)} %select_n.90.refs_1_.refs_0_, bf16[2,192,1280]{2,1,0:T(8,128)(2,1)S(1)} %copy-done, ...), custom_call_target="tpu_custom_call" | custom-call | tf_op jit(solution)/shard_map/pallas_call | solution.py:125
  116.1 0.0 copy-start.7
  116.1 7.1 %all-to-all-done.2.refs_3_ = bf16[128,2,16,256]{3,2,1,0:T(8,128)(2,1)} async-done(((bf16[128,2,16,256]{3,2,1,0:T(8,128)(2,1)}), bf16[128,2,16,256]{3,2,1,0:T(8,128)(2,1)}, u32[]{:S(2)}, u32[]{:S(2)}) %all-to-all-start.2) | async-done | bytes 2097184 | tf_op jit(solution)/shard_map/all_to_all | solution.py:19
  123.2 0.0 copy-done.7
  123.2 5.5 %all-to-all-start.3 = ((bf16[128,2,16,512]{3,2,1,0:T(8,128)(2,1)}), bf16[128,2,16,512]{3,2,1,0:T(8,128)(2,1)}, u32[]{:S(2)}, u32[]{:S(2)}) async-start(bf16[128,2,16,512]{3,2,1,0:T(8,128)(2,1)} %get-tuple-element.23), calls=%async_computation.3 | async-start | bytes 8388608 | tf_op jit(solution)/shard_map/all_to_all | solution.py:19
  128.7 11.3 %shard_map.85 = (bf16[2,192,256]{2,1,0:T(8,128)(2,1)S(1)}, bf16[2,192,256]{2,1,0:T(8,128)(2,1)S(1)}, bf16[128,2,16,256]{3,2,1,0:T(8,128)(2,1)S(1)}) custom-call(s32[1,2048]{1,0:T(1,128)S(1)} %select_n.90.refs_1_.refs_0_, bf16[2,192,1280]{2,1,0:T(8,128)(2,1)S(1)} %copy-done, bf16[2,192,1280]{2,1,0:T(8,128)(2,1)S(1)} %copy-done.1, ...), custom_call_target="tpu_custom_call" | custom-call | tf_op jit(solution)/shard_map/pallas_call | solution.py:125
  140.0 0.0 copy-start.2
  140.0 1.4 copy-done.2
  141.4 0.7 copy-done.3
  142.0 0.7 copy-done.5
  142.7 38.7 %all-to-all-done.3.refs_3_ = bf16[128,2,16,512]{3,2,1,0:T(8,128)(2,1)} async-done(((bf16[128,2,16,512]{3,2,1,0:T(8,128)(2,1)}), bf16[128,2,16,512]{3,2,1,0:T(8,128)(2,1)}, u32[]{:S(2)}, u32[]{:S(2)}) %all-to-all-start.3) | async-done | bytes 4194336 | tf_op jit(solution)/shard_map/all_to_all | solution.py:19
  181.4 5.5 %all-to-all-start.4 = ((bf16[128,2,16,256]{3,2,1,0:T(8,128)(2,1)}), bf16[128,2,16,256]{3,2,1,0:T(8,128)(2,1)}, u32[]{:S(2)}, u32[]{:S(2)}) async-start(bf16[128,2,16,256]{3,2,1,0:T(8,128)(2,1)} %copy-done.2), calls=%async_computation.4 | async-start | bytes 4194304 | tf_op jit(solution)/shard_map/all_to_all | solution.py:19
  186.9 21.7 %shard_map.86 = (bf16[2,192,512]{2,1,0:T(8,128)(2,1)S(1)}, bf16[2,192,512]{2,1,0:T(8,128)(2,1)S(1)}, bf16[128,2,16,512]{3,2,1,0:T(8,128)(2,1)}) custom-call(s32[1,2048]{1,0:T(1,128)S(1)} %select_n.90.refs_1_.refs_0_, bf16[2,192,1280]{2,1,0:T(8,128)(2,1)S(1)} %copy-done, bf16[2,192,1280]{2,1,0:T(8,128)(2,1)S(1)} %copy-done.1, ...), custom_call_target="tpu_custom_call" | custom-call | tf_op jit(solution)/shard_map/pallas_call | solution.py:125
  208.6 8.6 %all-to-all-done.4 = bf16[128,2,16,256]{3,2,1,0:T(8,128)(2,1)} async-done(((bf16[128,2,16,256]{3,2,1,0:T(8,128)(2,1)}), bf16[128,2,16,256]{3,2,1,0:T(8,128)(2,1)}, u32[]{:S(2)}, u32[]{:S(2)}) %all-to-all-start.4) | async-done | bytes 2097184 | tf_op jit(solution)/shard_map/all_to_all | solution.py:19
  217.1 5.5 %all-to-all-start.5 = ((bf16[128,2,16,512]{3,2,1,0:T(8,128)(2,1)}), bf16[128,2,16,512]{3,2,1,0:T(8,128)(2,1)}, u32[]{:S(2)}, u32[]{:S(2)}) async-start(bf16[128,2,16,512]{3,2,1,0:T(8,128)(2,1)} %get-tuple-element.33), calls=%async_computation.5 | async-start | bytes 8388608 | tf_op jit(solution)/shard_map/all_to_all | solution.py:19
  222.7 0.7 bitcast_convert_fusion.1
  223.4 2.9 %fusion.10 = f32[3,4,2,16,256]{4,0,3,2,1:T(4,128)S(1)} fusion(bf16[32,4,2,16,256]{4,3,2,1,0:T(8,128)(2,1)} %bitcast.35, s32[32]{0:T(128)S(1)} %select_reduce_fusion.1, pred[32]{0:T(512)(128)(4,1)S(1)} %get-tuple-element.37), kind=kOutput, calls=%fused_computation.14 | convolution fusion | flops 6291648 | bytes 2490528 | tf_op jit(solution)/shard_map/dot_general | solution.py:179
  226.3 4.7 %fusion.6 = f32[3,4,2,16,512]{4,0,3,2,1:T(4,128)S(1)} fusion(bf16[32,4,2,16,512]{4,3,2,1,0:T(8,128)(2,1)} %bitcast.33, pred[32]{0:T(512)(128)(4,1)S(1)} %iota_compare_fusion.2, s32[32]{0:T(128)S(1)} %select_reduce_fusion.1, pred[32]{0:T(512)(128)(4,1)S(1)} %get-tuple-element.37), kind=kOutput, calls=%fused_computation.8 | convolution fusion | flops 12583296 | bytes 4980928 | tf_op jit(solution)/shard_map/dot_general | solution.py:212
  231.0 0.0 copy-done.8
  231.0 42.0 %all_gather.3 = bf16[16,2,16,512]{3,2,1,0:T(8,128)(2,1)S(1)} all-gather(bf16[4,2,16,512]{3,2,1,0:T(8,128)(2,1)S(1)} %copy-done.8), channel_id=1, replica_groups=mesh['ctx'=32,'mp'=4] {'mp'}, dimensions={0}, use_global_device_ids=true | all-gather | bytes 655360 | tf_op jit(solution)/shard_map/all_gather | solution.py:219
  273.0 0.3 multiply_add_fusion
  273.4 0.0 copy-done.4
  273.4 0.0 copy-done.6
  273.4 1.4 pad_maximum_fusion
  274.8 0.6 all-to-all-done.5
  275.4 4.6 %fusion.4 = f32[3,4,2,16,512]{4,0,3,2,1:T(4,128)S(1)} fusion(bf16[32,4,2,16,512]{4,3,2,1,0:T(8,128)(2,1)} %bitcast.40, s32[32]{0:T(128)S(1)} %select_reduce_fusion.1, pred[32]{0:T(512)(128)(4,1)S(1)} %get-tuple-element.37), kind=kOutput, calls=%fused_computation.6 | convolution fusion | flops 12583104 | bytes 4980896 | tf_op jit(solution)/shard_map/dot_general | solution.py:179
  280.0 0.7 maximum_bitcast_fusion
  280.7 0.5 fusion.48
  281.2 0.6 copy.109
  281.8 1.1 copy.118
  282.9 0.6 copy.110
  283.6 1.1 copy.119
  (21 shorter events, 0.3 us)
Async XLA Ops:
  1.9 19.9 %all-to-all-start = ((s32[32,1,96]{2,1,0:T(1,128)}), s32[32,1,96]{2,1,0:T(1,128)S(1)}, u32[]{:S(2)}, u32[]{:S(2)}) async-start(s32[32,1,96]{2,1,0:T(1,128)} %broadcast_in_dim.194), calls=%async_computation | async-start | bytes 32768 | tf_op jit(solution)/shard_map/all_to_all | solution.py:154
  28.1 59.4 %all-to-all-start.1 = ((bf16[128,2,16,512]{3,2,1,0:T(8,128)(2,1)}), bf16[128,2,16,512]{3,2,1,0:T(8,128)(2,1)}, u32[]{:S(2)}, u32[]{:S(2)}) async-start(bf16[128,2,16,512]{3,2,1,0:T(8,128)(2,1)} %get-tuple-element.51), calls=%async_computation.1 | async-start | bytes 8388608 | tf_op jit(solution)/shard_map/all_to_all | solution.py:19
  36.7 56.3 %copy-start.9 = (s32[1,96]{1,0:T(1,128)S(1)}, s32[1,96]{1,0:T(1,128)}, u32[]{:S(2)}) copy-start(s32[1,96]{1,0:T(1,128)} %param.9) | copy-start | bytes 1156
  36.7 56.8 %copy-start = (bf16[2,192,1280]{2,1,0:T(8,128)(2,1)S(1)}, bf16[2,192,1280]{2,1,0:T(8,128)(2,1)}, u32[]{:S(2)}) copy-start(bf16[2,192,1280]{2,1,0:T(8,128)(2,1)} %refs_1_.3) | copy-start | bytes 2949124
  36.7 56.8 %copy-start.1 = (bf16[2,192,1280]{2,1,0:T(8,128)(2,1)S(1)}, bf16[2,192,1280]{2,1,0:T(8,128)(2,1)}, u32[]{:S(2)}) copy-start(bf16[2,192,1280]{2,1,0:T(8,128)(2,1)} %refs_2_.5) | copy-start | bytes 2949124
  87.4 35.7 %all-to-all-start.2 = ((bf16[128,2,16,256]{3,2,1,0:T(8,128)(2,1)}), bf16[128,2,16,256]{3,2,1,0:T(8,128)(2,1)}, u32[]{:S(2)}, u32[]{:S(2)}) async-start(bf16[128,2,16,256]{3,2,1,0:T(8,128)(2,1)} %fusion.9), calls=%async_computation.2 | async-start | bytes 4194304 | tf_op jit(solution)/shard_map/all_to_all | solution.py:19
  116.1 7.1 %copy-start.7 = (bf16[4,2,16,512]{3,2,1,0:T(8,128)(2,1)}, bf16[4,2,16,512]{3,2,1,0:T(8,128)(2,1)S(1)}, u32[]{:S(2)}) copy-start(bf16[4,2,16,512]{3,2,1,0:T(8,128)(2,1)S(1)} %get-tuple-element.31) | copy-start | bytes 393220
  123.2 58.2 %all-to-all-start.3 = ((bf16[128,2,16,512]{3,2,1,0:T(8,128)(2,1)}), bf16[128,2,16,512]{3,2,1,0:T(8,128)(2,1)}, u32[]{:S(2)}, u32[]{:S(2)}) async-start(bf16[128,2,16,512]{3,2,1,0:T(8,128)(2,1)} %get-tuple-element.23), calls=%async_computation.3 | async-start | bytes 8388608 | tf_op jit(solution)/shard_map/all_to_all | solution.py:19
  140.0 1.4 copy-start.2
  141.4 0.7 copy-start.3
  142.0 0.7 copy-start.5
  181.4 35.7 %all-to-all-start.4 = ((bf16[128,2,16,256]{3,2,1,0:T(8,128)(2,1)}), bf16[128,2,16,256]{3,2,1,0:T(8,128)(2,1)}, u32[]{:S(2)}, u32[]{:S(2)}) async-start(bf16[128,2,16,256]{3,2,1,0:T(8,128)(2,1)} %copy-done.2), calls=%async_computation.4 | async-start | bytes 4194304 | tf_op jit(solution)/shard_map/all_to_all | solution.py:19
  217.1 58.2 %all-to-all-start.5 = ((bf16[128,2,16,512]{3,2,1,0:T(8,128)(2,1)}), bf16[128,2,16,512]{3,2,1,0:T(8,128)(2,1)}, u32[]{:S(2)}, u32[]{:S(2)}) async-start(bf16[128,2,16,512]{3,2,1,0:T(8,128)(2,1)} %get-tuple-element.33), calls=%async_computation.5 | async-start | bytes 8388608 | tf_op jit(solution)/shard_map/all_to_all | solution.py:19
  226.3 4.7 %copy-start.8 = (bf16[4,2,16,512]{3,2,1,0:T(8,128)(2,1)S(1)}, bf16[4,2,16,512]{3,2,1,0:T(8,128)(2,1)}, u32[]{:S(2)}) copy-start(bf16[4,2,16,512]{3,2,1,0:T(8,128)(2,1)} %copy-done.7) | copy-start | bytes 393220
  230.9 42.4 %copy-start.4 = (bf16[2,192,256]{2,1,0:T(8,128)(2,1)S(1)}, bf16[2,192,256]{2,1,0:T(8,128)(2,1)}, u32[]{:S(2)}) copy-start(bf16[2,192,256]{2,1,0:T(8,128)(2,1)} %copy-done.3) | copy-start | bytes 589828
  230.9 42.4 %copy-start.6 = (bf16[2,192,256]{2,1,0:T(8,128)(2,1)S(1)}, bf16[2,192,256]{2,1,0:T(8,128)(2,1)}, u32[]{:S(2)}) copy-start(bf16[2,192,256]{2,1,0:T(8,128)(2,1)} %copy-done.5) | copy-start | bytes 589828
